TPU v7x, 128 devices: a whole 4x4x4 slice. The times are simulated.
128 devices in a mesh: slab: 32 (over y, x, core), img: 4 (over z).
Axes of the slice: x: 4, y: 4, z: 4, core: 2. Of those that a mesh axis runs over, the one named last changes fastest.
Arguments:
- volume: float32 [128, 1024, 1024], P('img', 'slab'), may hold values from -6 to 6
- blk_plane: int32 [512, 8], replicated, may hold values from 0 to 126, all different within a row; in each aligned block of 4 rows (0 to 3, 4 to 7, ...) at most 2 rows name the same one
- blk_row: int32 [512, 8], replicated, may hold values from 0 to 1022
- blk_col: int32 [512, 8], replicated, may hold values from 0 to 7
- frac_plane: float32 [512, 8], replicated, may hold values from 0 to 1
- frac_row: float32 [512, 8], replicated, may hold values from 0 to 1
- defocus: float32 [512], replicated, may hold values from 0.5 to 4
Outputs:
- slices: float32 [512, 8, 2, 128], P(('slab', 'img'))
Inputs may be any that keep to these rules, and one draw needn't show every extreme that they name: `blk_plane`: the blocks of one image name different lower planes. Among the 4 images of one device (aligned groups of images), no plane is the lower plane of more than 2 blocks, and some plane reaches 2.
All inputs are finite; a program needn't handle non-finite values.
Results may differ from a plain program's by a relative error of at most 0.0003.
Values sent between devices are 32-bit elements; how exact they have to be, the bound alone decides.
No kernel may reach another device: no remote copies, remote signals or barrier semaphores. Data moves between devices by JAX's collectives and lax.ppermute only.
A program may use at most 128 MiB of HBM per device.

v0:
```python
import math

import jax
import jax.numpy as jnp
from jax import lax
from jax.sharding import PartitionSpec as P

LANES = 128


CTF_SCALE = 20.0
CTF_PHASE = 0.07
HIGH = lax.Precision.HIGHEST


def dft_tables(length):
    steps = lax.iota(jnp.int32, length)
    phase = steps[:, None] * steps[None, :] % length
    angle = phase.astype(jnp.float32) * (2.0 * math.pi / length)
    factor = 1.0 / math.sqrt(length)
    return (jnp.cos(angle) * factor, jnp.sin(angle) * factor)


def column_transform(field, cosine, sine):
    real_part = jnp.einsum("prx,xk->prk", field, cosine, precision=HIGH)
    imag_part = -jnp.einsum("prx,xk->prk", field, sine, precision=HIGH)
    return (real_part, imag_part)


def row_transform(pieces, cosine, sine):
    real_part, imag_part = pieces
    out_real = jnp.einsum("kr,prc->pkc", cosine, real_part, precision=HIGH) + jnp.einsum(
        "kr,prc->pkc", sine, imag_part, precision=HIGH
    )
    out_imag = jnp.einsum("kr,prc->pkc", cosine, imag_part, precision=HIGH) - jnp.einsum(
        "kr,prc->pkc", sine, real_part, precision=HIGH
    )
    return (out_real, out_imag)


def extract(plane_real, plane_imag, first_plane, meta, box):
    plane_idx, rows, cols, frac_z, frac_y, focus = [v.reshape(-1) for v in meta]
    frac_y = frac_y[:, None]
    lane = lax.iota(jnp.int32, LANES)
    column_x = cols[:, None] * LANES + lane[None, :]
    fold_x = jnp.minimum(column_x, box - column_x).astype(jnp.float32)
    fold_y = jnp.minimum(rows, box - rows).astype(jnp.float32)
    wave_sq = (fold_x * fold_x + (fold_y * fold_y)[:, None]) / float(box * box)
    ctf_value = -jnp.sin(CTF_SCALE * focus[:, None] * wave_sq + CTF_PHASE)
    per_row = box // LANES
    index_low = rows * per_row + cols
    index_high = index_low + per_row
    here = first_plane + 0
    weight = jnp.where(plane_idx == here, 1.0 - frac_z, 0.0) + jnp.where(
        plane_idx + 1 == here, frac_z, 0.0
    )
    scale = weight[:, None] * ctf_value
    flat_real = plane_real[0].reshape(-1, LANES)
    flat_imag = plane_imag[0].reshape(-1, LANES)
    total_real = scale * ((1.0 - frac_y) * flat_real[index_low] + frac_y * flat_real[index_high])
    total_imag = scale * ((1.0 - frac_y) * flat_imag[index_low] + frac_y * flat_imag[index_high])
    return jnp.stack([total_real, total_imag], axis=1)


def on_device(volume, blk_plane, blk_row, blk_col, frac_plane, frac_row, defocus):
    box = volume.shape[2]
    cosine, sine = dft_tables(box)
    n_slab = lax.axis_size("slab")
    col_real, col_imag = column_transform(volume, cosine, sine)
    plane_real, plane_imag = row_transform(
        (
            lax.all_to_all(col_real, "slab", split_axis=0, concat_axis=1, tiled=True),
            lax.all_to_all(col_imag, "slab", split_axis=0, concat_axis=1, tiled=True),
        ),
        cosine,
        sine,
    )
    first_plane = (lax.axis_index("img") * n_slab + lax.axis_index("slab")) * plane_real.shape[0]
    focus_blocks = jnp.broadcast_to(defocus[:, None], blk_plane.shape)
    meta = (blk_plane, blk_row, blk_col, frac_plane, frac_row, focus_blocks)
    partial_value = extract(plane_real, plane_imag, first_plane, meta, box)
    partial_value = partial_value.reshape(blk_plane.shape[0], blk_plane.shape[1], 2, LANES)
    return lax.psum_scatter(partial_value, ("slab", "img"), scatter_dimension=0, tiled=True)


def solution(mesh):
    placed = (P("img", "slab", None), P(), P(), P(), P(), P(), P())
    return jax.shard_map(
        on_device,
        mesh=mesh,
        in_specs=placed,
        out_specs=P(("slab", "img"), None, None, None),
        check_vma=False,
    )
```

profile of v0, /device:TPU:1, one launch (start us, length us, event | category | flops | bytes accessed | tf_op | source)
XLA Modules:
  0.0 1037.0 jit_solution(18043371418869886259)
XLA Ops:
  6.5 31.0 %fusion.14 = f32[32,32,1024]{2,1,0:T(8,128)} fusion(f32[32,32,1024]{2,1,0:T(8,128)} %param.7), kind=kOutput, calls=%fused_computation.28 | convolution fusion | flops 12900630528 | bytes 8388608 | tf_op jit(solution)/shard_map/prx,xk->prk/dot_general | solution.py:25
  37.5 9.0 all-to-all-start
  46.5 31.2 %negate_bitcast_fusion = f32[32,32,1024]{2,1,0:T(8,128)} fusion(f32[32,32,1024]{2,1,0:T(8,128)} %param.7), kind=kOutput, calls=%fused_computation.17 | convolution fusion | flops 12901679104 | bytes 8388608 | tf_op jit(solution)/shard_map/prx,xk->prk/dot_general | solution.py:26
  77.8 0.0 copy-start.1
  77.8 0.0 copy-start.4
  77.8 0.0 copy-start.2
  77.8 0.0 copy-start.3
  77.8 0.0 copy-start
  77.8 0.0 copy-start.5
  77.8 19.1 %all-to-all-done = f32[32,32,1024]{2,1,0:T(8,128)} async-done(((f32[32,32,1024]{2,1,0:T(8,128)}), f32[32,32,1024]{2,1,0:T(8,128)}, u32[]{:S(2)}, u32[]{:S(2)}) %all-to-all-start) | async-done | bytes 4194336 | tf_op jit(solution)/shard_map/all_to_all | solution.py:72
  96.9 8.1 all-to-all-start.1
  105.0 0.4 reduce-scatter.2.cloned.1.call-start
  105.5 0.0 copy-done.1
  105.5 0.0 copy-done.4
  105.5 0.1 copy.34
  105.6 0.2 add.204
  105.8 0.0 copy-done.2
  105.8 0.0 copy-done.3
  105.9 0.1 copy.29
  106.0 0.1 copy.30
  106.1 0.1 copy.31
  106.3 0.0 copy-done
  106.3 0.1 copy.36
  106.4 0.1 copy.32
  106.5 0.0 copy-done.5
  106.6 44.3 %fusion.11 = f32[1024,1024]{1,0:T(8,128)} fusion(f32[1024,1024]{1,0:T(8,128)} %bitcast.2), kind=kOutput, calls=%fused_computation.24 | convolution fusion | flops 12900630528 | bytes 8388608 | tf_op jit(solution)/shard_map/kr,prc->pkc/dot_general | solution.py:32
  150.9 4.8 all-to-all-done.1
  155.7 0.0 copy-start.6
  155.7 44.6 %fusion.10 = f32[1024,1024]{1,0:T(8,128)} fusion(f32[1024,1024]{1,0:T(8,128)} %bitcast.5), kind=kOutput, calls=%fused_computation.23 | convolution fusion | flops 12900630528 | bytes 8388608 | tf_op jit(solution)/shard_map/kr,prc->pkc/dot_general | solution.py:35
  200.3 0.0 copy-done.6
  200.3 44.6 %add_bitcast_fusion = f32[1,1024,1024]{1,2,0:T(8,128)} fusion(f32[1024,1024]{1,0:T(8,128)S(1)} %copy-done.6, f32[1024,1024]{1,0:T(8,128)} %bitcast.5), kind=kOutput, calls=%fused_computation.16 | convolution fusion | flops 12901679104 | bytes 12582912 | tf_op jit(solution)/shard_map/kr,prc->pkc/dot_general | solution.py:32
  244.9 5.4 copy.33
  250.3 4.9 reshape_squeeze.6
  255.2 13.0 %gather_fusion = f32[4096,128]{1,0:T(8,128)S(1)} fusion(f32[8192,128]{1,0:T(8,128)} %reshape_squeeze.6, s32[4096]{0:T(1024)S(1)} %broadcast_clamp_fusion.1), kind=kCustom, calls=%fused_computation | custom fusion | bytes 4210688 | tf_op jit(solution)/shard_map/gather | solution.py:60
  268.2 16.4 %gather_fusion.1 = f32[4096,128]{1,0:T(8,128)} fusion(f32[8192,128]{1,0:T(8,128)} %reshape_squeeze.6, s32[4096]{0:T(1024)S(1)} %broadcast_clamp_fusion), kind=kCustom, calls=%fused_computation.1 | custom fusion | bytes 4210688 | tf_op jit(solution)/shard_map/gather | solution.py:60
  284.5 45.0 %subtract_bitcast_fusion = f32[1,1024,1024]{1,2,0:T(8,128)} fusion(f32[1024,1024]{1,0:T(8,128)} %fusion.10, f32[1024,1024]{1,0:T(8,128)} %bitcast.2), kind=kOutput, calls=%fused_computation.15 | convolution fusion | flops 12901679104 | bytes 12582912 | tf_op jit(solution)/shard_map/kr,prc->pkc/dot_general | solution.py:35
  329.5 5.3 copy.38
  334.8 4.9 reshape_squeeze.7
  339.7 16.3 %gather_fusion.2 = f32[4096,128]{1,0:T(8,128)} fusion(f32[8192,128]{1,0:T(8,128)} %reshape_squeeze.7, s32[4096]{0:T(1024)S(1)} %broadcast_clamp_fusion.1), kind=kCustom, calls=%fused_computation.2 | custom fusion | bytes 4210688 | tf_op jit(solution)/shard_map/gather | solution.py:61
  356.1 16.4 %gather_fusion.3 = f32[4096,128]{1,0:T(8,128)} fusion(f32[8192,128]{1,0:T(8,128)} %reshape_squeeze.7, s32[4096]{0:T(1024)S(1)} %broadcast_clamp_fusion), kind=kCustom, calls=%fused_computation.3 | custom fusion | bytes 4210688 | tf_op jit(solution)/shard_map/gather | solution.py:61
  372.5 11.0 %fusion.30 = (f32[512,8,1,128]{3,1,2,0:T(8,128)S(1)}, f32[512,8,1,128]{3,1,2,0:T(8,128)S(1)}) fusion(f32[4096,128]{1,0:T(8,128)} %gather_fusion.1, f32[4096,128]{1,0:T(8,128)S(1)} %gather_fusion, f32[512,8]{1,0:T(8,128)S(1)} %copy.36, f32[512,8]{1,0:T(8,128)S(1)} %copy.32, f32[512]{0:T(512)S(1)} %broadcast_multiply_fusion.1, f32[512,8]{1,0:T(8,128)S(1)} %copy.31, ...), kind=kLoop, calls=%fused_computation.43 | loop fusion | flops 9437184 | bytes 12666880 | tf_op jit(solution)/shard_map/mul | solution.py:60
  383.5 2.2 pad_maximum_fusion
  385.7 0.0 reduce-scatter.2.cloned.1.call-update
  385.7 642.6 %reduce-scatter.2.cloned.1.call-done = f32[4,8,2,128]{3,1,2,0:T(8,128)} async-done(((f32[512,8,2,128]{3,1,2,0:T(8,128)}), f32[4,8,2,128]{3,1,2,0:T(8,128)}) %reduce-scatter.2.cloned.1.call-update) | async-done | bytes 32784 | tf_op jit(solution)/shard_map/reduce_scatter | solution.py:83
  1028.3 1.4 copy.41
  (8 shorter events, 0.1 us)
Async XLA Ops:
  37.5 59.4 %all-to-all-start = ((f32[32,32,1024]{2,1,0:T(8,128)}), f32[32,32,1024]{2,1,0:T(8,128)}, u32[]{:S(2)}, u32[]{:S(2)}) async-start(f32[32,32,1024]{2,1,0:T(8,128)} %fusion.14), calls=%async_computation | async-start | bytes 8388608 | tf_op jit(solution)/shard_map/all_to_all | solution.py:72
  77.8 27.7 %copy-start.1 = (s32[512,8]{0,1:T(8,128)S(1)}, s32[512,8]{0,1:T(8,128)}, u32[]{:S(2)}) copy-start(s32[512,8]{0,1:T(8,128)} %param.9) | copy-start | bytes 49156
  77.8 27.7 %copy-start.4 = (s32[512,8]{0,1:T(8,128)S(1)}, s32[512,8]{0,1:T(8,128)}, u32[]{:S(2)}) copy-start(s32[512,8]{0,1:T(8,128)} %param.10) | copy-start | bytes 49156
  77.8 28.1 %copy-start.2 = (f32[512,8]{0,1:T(8,128)S(1)}, f32[512,8]{0,1:T(8,128)}, u32[]{:S(2)}) copy-start(f32[512,8]{0,1:T(8,128)} %param.11) | copy-start | bytes 49156
  77.8 28.1 %copy-start.3 = (s32[512,8]{0,1:T(8,128)S(1)}, s32[512,8]{0,1:T(8,128)}, u32[]{:S(2)}) copy-start(s32[512,8]{0,1:T(8,128)} %param.8) | copy-start | bytes 49156
  77.8 28.5 %copy-start = (f32[512,8]{0,1:T(8,128)S(1)}, f32[512,8]{0,1:T(8,128)}, u32[]{:S(2)}) copy-start(f32[512,8]{0,1:T(8,128)} %param.12) | copy-start | bytes 49156
  77.8 28.8 %copy-start.5 = (f32[512]{0:T(512)S(1)}, f32[512]{0:T(512)}, u32[]{:S(2)}) copy-start(f32[512]{0:T(512)} %param.13) | copy-start | bytes 6148
  96.9 58.8 %all-to-all-start.1 = ((f32[32,32,1024]{2,1,0:T(8,128)}), f32[32,32,1024]{2,1,0:T(8,128)}, u32[]{:S(2)}, u32[]{:S(2)}) async-start(f32[32,32,1024]{2,1,0:T(8,128)} %negate_bitcast_fusion), calls=%async_computation.1 | async-start | bytes 8388608 | tf_op jit(solution)/shard_map/all_to_all | solution.py:73
  105.0 923.3 %reduce-scatter.2.cloned.1.call-start = ((), (), s32[]{:S(2)}) async-start(), calls=%async_computation.3 | async-start | bytes 4227072 | tf_op jit(solution)/shard_map/reduce_scatter | solution.py:83
  155.7 44.6 %copy-start.6 = (f32[1024,1024]{1,0:T(8,128)S(1)}, f32[1024,1024]{1,0:T(8,128)}, u32[]{:S(2)}) copy-start(f32[1024,1024]{1,0:T(8,128)} %fusion.11) | copy-start | bytes 12582916
Sparse Core Ops, SparseCore 0:
  385.9 642.3 reduce-scatter.1
where the time goes:
time: 1050 us; the launch traced here: 1040 us
  waiting for transfers between devices  667 us (64%)
  matrix products  241 us (23%)
  local copies, waits for them, and re-layouts  84.9 us (8%)
  starting transfers between devices  17.5 us (2%)
  between operations  14.1 us (1%)
  other arithmetic  13.3 us (1%)
    reduce_scatter x1, waiting for transfers between devices, on_device(): lax.psum_scatter(partial_value, ('slab', 'img'), scatter_dimension=0, til...  643 us
    dot_general x1, matrix products, row_transform(): jnp.einsum('kr,prc->pkc', sine, real_part, precision=HIGH)  45 us
    dot_general x1, matrix products, row_transform(): jnp.einsum('kr,prc->pkc', sine, imag_part, precision=HIGH)  44.6 us
    dot_general x1, matrix products, row_transform(): jnp.einsum('kr,prc->pkc', cosine, imag_part, precision=HIGH)  44.6 us
    dot_general x1, matrix products, row_transform(): jnp.einsum('kr,prc->pkc', cosine, real_part, precision=HIGH)  44.3 us
    dot_general x1, matrix products, column_transform(): imag_part = -jnp.einsum('prx,xk->prk', field, sine, precision=HIGH)  31.2 us
    dot_general x1, matrix products, column_transform(): real_part = jnp.einsum('prx,xk->prk', field, cosine, precision=HIGH)  31 us
  transfers between devices with their start and end apart: 3, of which 3 were waited for; matrix products, arithmetic and copies ran while one was open for 7% of the time, Pallas kernels for 0%

commit v1 on v0

--- a/solution.py
+++ b/solution.py
@@ -38,9 +38,41 @@
     return (out_real, out_imag)
 
 
-def extract(plane_real, plane_imag, first_plane, meta, box):
-    plane_idx, rows, cols, frac_z, frac_y, focus = [v.reshape(-1) for v in meta]
-    frac_y = frac_y[:, None]
+def slot_tables(blk_plane, n_dev):
+    plane = blk_plane.reshape(n_dev, -1)
+    k_dev = plane.shape[1]
+    order = lax.iota(jnp.int32, k_dev)
+    same = plane[:, :, None] == plane[:, None, :]
+    earlier = order[None, None, :] < order[None, :, None]
+    rank = jnp.sum((same & earlier).astype(jnp.int32), axis=2)
+    return plane, rank
+
+
+def send_parts(plane_real, plane_imag, first_plane, meta, box, n_dev):
+    blk_plane, blk_row, blk_col, frac_plane, frac_row, defocus = meta
+    n_blk = blk_plane.shape[1]
+    plane, rank = slot_tables(blk_plane, n_dev)
+    k_dev = plane.shape[1]
+    own = plane_real.shape[0]
+    t = lax.iota(jnp.int32, own)[:, None, None]
+    side = lax.iota(jnp.int32, 2)[None, :, None]
+    u = lax.iota(jnp.int32, 2)[None, None, :]
+    target = first_plane + t - side
+    match = (plane[:, None, None, None, :] == target[None, :, :, :, None]) & (
+        rank[:, None, None, None, :] == u[None, :, :, :, None]
+    )
+    valid = jnp.any(match, axis=-1)
+    kidx = jnp.sum(jnp.where(match, lax.iota(jnp.int32, k_dev), 0), axis=-1)
+    g = lax.iota(jnp.int32, n_dev)[:, None, None, None] * k_dev + kidx
+    g = g.reshape(-1)
+    rows = blk_row.reshape(-1)[g]
+    cols = blk_col.reshape(-1)[g]
+    frac_z = frac_plane.reshape(-1)[g]
+    frac_y = frac_row.reshape(-1)[g][:, None]
+    focus = defocus[g // n_blk]
+    side_f = jnp.broadcast_to(side, (n_dev, own, 2, 2)).reshape(-1)
+    valid = valid.reshape(-1)
+    t_idx = jnp.broadcast_to(t, (n_dev, own, 2, 2)).reshape(-1)
     lane = lax.iota(jnp.int32, LANES)
     column_x = cols[:, None] * LANES + lane[None, :]
     fold_x = jnp.minimum(column_x, box - column_x).astype(jnp.float32)
@@ -48,24 +80,41 @@
     wave_sq = (fold_x * fold_x + (fold_y * fold_y)[:, None]) / float(box * box)
     ctf_value = -jnp.sin(CTF_SCALE * focus[:, None] * wave_sq + CTF_PHASE)
     per_row = box // LANES
-    index_low = rows * per_row + cols
+    index_low = t_idx * (box * per_row) + rows * per_row + cols
     index_high = index_low + per_row
-    here = first_plane + 0
-    weight = jnp.where(plane_idx == here, 1.0 - frac_z, 0.0) + jnp.where(
-        plane_idx + 1 == here, frac_z, 0.0
-    )
+    weight = jnp.where(side_f == 0, 1.0 - frac_z, frac_z)
+    weight = jnp.where(valid, weight, 0.0)
     scale = weight[:, None] * ctf_value
-    flat_real = plane_real[0].reshape(-1, LANES)
-    flat_imag = plane_imag[0].reshape(-1, LANES)
-    total_real = scale * ((1.0 - frac_y) * flat_real[index_low] + frac_y * flat_real[index_high])
-    total_imag = scale * ((1.0 - frac_y) * flat_imag[index_low] + frac_y * flat_imag[index_high])
-    return jnp.stack([total_real, total_imag], axis=1)
+    flat_real = plane_real.reshape(-1, LANES)
+    flat_imag = plane_imag.reshape(-1, LANES)
+    part_real = scale * ((1.0 - frac_y) * flat_real[index_low] + frac_y * flat_real[index_high])
+    part_imag = scale * ((1.0 - frac_y) * flat_imag[index_low] + frac_y * flat_imag[index_high])
+    parts = jnp.stack([part_real, part_imag], axis=1)
+    return parts.reshape(n_dev, own * 4, 2, LANES)
+
+
+def gather_parts(recv, blk_plane, me, own, n_slab, n_img):
+    n_dev = n_slab * n_img
+    plane, rank = slot_tables(blk_plane, n_dev)
+    mine = plane[me]
+    my_rank = rank[me]
+    slots = own * 4
+
+    def place(q, side):
+        holder = q // own
+        src = (holder % n_slab) * n_img + holder // n_slab
+        return src * slots + (q % own) * 4 + side * 2 + my_rank
+
+    flat = recv.reshape(-1, 2, LANES)
+    return flat[place(mine, 0)] + flat[place(mine + 1, 1)]
 
 
 def on_device(volume, blk_plane, blk_row, blk_col, frac_plane, frac_row, defocus):
     box = volume.shape[2]
     cosine, sine = dft_tables(box)
     n_slab = lax.axis_size("slab")
+    n_img = lax.axis_size("img")
+    n_dev = n_slab * n_img
     col_real, col_imag = column_transform(volume, cosine, sine)
     plane_real, plane_imag = row_transform(
         (
@@ -75,12 +124,15 @@
         cosine,
         sine,
     )
-    first_plane = (lax.axis_index("img") * n_slab + lax.axis_index("slab")) * plane_real.shape[0]
-    focus_blocks = jnp.broadcast_to(defocus[:, None], blk_plane.shape)
-    meta = (blk_plane, blk_row, blk_col, frac_plane, frac_row, focus_blocks)
-    partial_value = extract(plane_real, plane_imag, first_plane, meta, box)
-    partial_value = partial_value.reshape(blk_plane.shape[0], blk_plane.shape[1], 2, LANES)
-    return lax.psum_scatter(partial_value, ("slab", "img"), scatter_dimension=0, tiled=True)
+    own = plane_real.shape[0]
+    first_plane = (lax.axis_index("img") * n_slab + lax.axis_index("slab")) * own
+    meta = (blk_plane, blk_row, blk_col, frac_plane, frac_row, defocus)
+    parts = send_parts(plane_real, plane_imag, first_plane, meta, box, n_dev)
+    recv = lax.all_to_all(parts, ("slab", "img"), split_axis=0, concat_axis=0, tiled=True)
+    me = lax.axis_index("slab") * n_img + lax.axis_index("img")
+    total = gather_parts(recv, blk_plane, me, own, n_slab, n_img)
+    n_blk = blk_plane.shape[1]
+    return total.reshape(-1, n_blk, 2, LANES)
 
 
 def solution(mesh):

time: 1050 us -> 367 us (0.35)
  waiting for transfers between devices: 667 us -> 32.7 us
  local copies, waits for them, and re-layouts: 84.9 us -> 55.6 us
  between operations: 14.1 us -> 0.92 us
  other arithmetic: 13.3 us -> 2.33 us
    reduce_scatter x1 -> x0, waiting for transfers between devices: 643 us -> none  [on_device(): lax.psum_scatter(partial_value, ('slab', 'img'), scatter_dimension=0, til...]
    gather x4 -> x17, local copies, waits for them, and re-layouts: 62.1 us -> 31 us  [the longest x1 3.51 us: send_parts(): focus = defocus[g // n_blk]]
    all_to_all x0 -> x1, waiting for transfers between devices: none -> 13.5 us  [on_device(): lax.all_to_all(parts, ('slab', 'img'), split_axis=0, concat_axis=0, tiled...]
  transfers between devices with their start and end apart: 3 -> 3, of which waited for: 3 -> 2; matrix products, arithmetic and copies ran while one was open for 7% -> 27% of each run, Pallas kernels for 0% -> 0%
where the time goes in v1:
time: 367 us; the launch traced here: 360 us
  matrix products  241 us (66%)
  local copies, waits for them, and re-layouts  55.6 us (15%)
  waiting for transfers between devices  32.7 us (9%)
  starting transfers between devices  27.5 us (7%)
    dot_general x1, matrix products, row_transform(): jnp.einsum('kr,prc->pkc', sine, real_part, precision=HIGH)  45 us
    dot_general x1, matrix products, row_transform(): jnp.einsum('kr,prc->pkc', cosine, real_part, precision=HIGH)  44.7 us
    dot_general x1, matrix products, row_transform(): jnp.einsum('kr,prc->pkc', cosine, imag_part, precision=HIGH)  44.6 us
    dot_general x1, matrix products, row_transform(): jnp.einsum('kr,prc->pkc', sine, imag_part, precision=HIGH)  44.6 us
    dot_general x1, matrix products, column_transform(): imag_part = -jnp.einsum('prx,xk->prk', field, sine, precision=HIGH)  31.2 us
    dot_general x1, matrix products, column_transform(): real_part = jnp.einsum('prx,xk->prk', field, cosine, precision=HIGH)  31 us
    all_to_all x1, waiting for transfers between devices, on_device(): lax.all_to_all(col_real, 'slab', split_axis=0, concat_axis=1, tiled=True)  19.2 us
    all_to_all x1, waiting for transfers between devices, on_device(): lax.all_to_all(parts, ('slab', 'img'), split_axis=0, concat_axis=0, tiled...  13.5 us
  transfers between devices with their start and end apart: 3, of which 2 were waited for; matrix products, arithmetic and copies ran while one was open for 27% of the time, Pallas kernels for 0%

profile of v1, /device:TPU:1, one launch (start us, length us, event | category | flops | bytes accessed | tf_op | source)
XLA Modules:
  0.0 360.2 jit_solution(14056283938939351456)
XLA Ops:
  0.0 31.0 %fusion.14 = f32[32,32,1024]{2,1,0:T(8,128)} fusion(f32[32,32,1024]{2,1,0:T(8,128)} %param.7), kind=kOutput, calls=%fused_computation.33 | convolution fusion | flops 12900630528 | bytes 8388608 | tf_op jit(solution)/shard_map/prx,xk->prk/dot_general | solution.py:25
  31.0 9.0 %all-to-all-start = ((f32[32,32,1024]{2,1,0:T(8,128)}), f32[32,32,1024]{2,1,0:T(8,128)}, u32[]{:S(2)}, u32[]{:S(2)}) async-start(f32[32,32,1024]{2,1,0:T(8,128)} %fusion.14), calls=%async_computation | async-start | bytes 8388608 | tf_op jit(solution)/shard_map/all_to_all | solution.py:121
  40.0 31.2 %negate_bitcast_fusion = f32[32,32,1024]{2,1,0:T(8,128)} fusion(f32[32,32,1024]{2,1,0:T(8,128)} %param.7), kind=kOutput, calls=%fused_computation.23 | convolution fusion | flops 12901679104 | bytes 8388608 | tf_op jit(solution)/shard_map/prx,xk->prk/dot_general | solution.py:26
  71.2 19.2 %all-to-all-done = f32[32,32,1024]{2,1,0:T(8,128)} async-done(((f32[32,32,1024]{2,1,0:T(8,128)}), f32[32,32,1024]{2,1,0:T(8,128)}, u32[]{:S(2)}, u32[]{:S(2)}) %all-to-all-start) | async-done | bytes 4194336 | tf_op jit(solution)/shard_map/all_to_all | solution.py:121
  90.4 8.1 %all-to-all-start.1 = ((f32[32,32,1024]{2,1,0:T(8,128)}), f32[32,32,1024]{2,1,0:T(8,128)}, u32[]{:S(2)}, u32[]{:S(2)}) async-start(f32[32,32,1024]{2,1,0:T(8,128)} %negate_bitcast_fusion), calls=%async_computation.1 | async-start | bytes 8388608 | tf_op jit(solution)/shard_map/all_to_all | solution.py:122
  98.5 0.1 copy.109
  98.7 0.2 reshape.733
  98.8 0.2 add.393
  99.0 0.2 add.394
  99.2 0.1 copy.101
  99.4 0.1 eq.75
  99.6 0.2 convert_reduce_fusion
  99.9 0.2 copy.106
  100.1 0.2 reduce_sum.26
  100.3 0.1 copy.111
  100.4 0.2 reshape.734
  100.6 3.1 gather_fusion.1
  103.8 3.1 gather_fusion.2
  106.9 0.1 copy.115
  107.1 0.2 reshape.735
  107.2 3.1 gather_fusion.4
  110.6 3.5 gather_fusion.3
  114.3 0.1 gather.51
  114.5 0.1 mul.310
  114.7 0.1 copy.105
  114.9 0.2 reshape.732
  115.0 3.1 gather_fusion
  118.4 44.7 %fusion.11 = f32[1024,1024]{1,0:T(8,128)} fusion(f32[1024,1024]{1,0:T(8,128)} %bitcast.4), kind=kOutput, calls=%fused_computation.30 | convolution fusion | flops 12900630528 | bytes 8388608 | tf_op jit(solution)/shard_map/kr,prc->pkc/dot_general | solution.py:32
  163.1 44.6 %fusion.10 = f32[1024,1024]{1,0:T(8,128)} fusion(f32[1024,1024]{1,0:T(8,128)} %bitcast.7), kind=kOutput, calls=%fused_computation.29 | convolution fusion | flops 12900630528 | bytes 8388608 | tf_op jit(solution)/shard_map/kr,prc->pkc/dot_general | solution.py:35
  207.7 44.6 %add_bitcast_fusion = f32[1,1024,1024]{1,2,0:T(8,128)} fusion(f32[1024,1024]{1,0:T(8,128)S(1)} %copy-done.6, f32[1024,1024]{1,0:T(8,128)} %bitcast.7), kind=kOutput, calls=%fused_computation.22 | convolution fusion | flops 12901679104 | bytes 12582912 | tf_op jit(solution)/shard_map/kr,prc->pkc/dot_general | solution.py:32
  252.3 5.4 %copy.117 = f32[1,1024,1024]{2,1,0:T(8,128)} copy(f32[1,1024,1024]{1,2,0:T(8,128)} %add_bitcast_fusion) | data formatting | bytes 8388608 | tf_op jit(solution)/shard_map/add | solution.py:32
  257.7 4.9 %reshape.738 = f32[8192,128]{1,0:T(8,128)} reshape(f32[1,1024,1024]{2,1,0:T(8,128)} %copy.117) | data formatting | bytes 8388608 | tf_op jit(solution)/shard_map/reshape | solution.py:88
  262.6 3.2 gather_fusion.6
  265.8 3.2 gather_fusion.5
  269.0 45.0 %subtract_bitcast_fusion = f32[1,1024,1024]{1,2,0:T(8,128)} fusion(f32[1024,1024]{1,0:T(8,128)} %fusion.10, f32[1024,1024]{1,0:T(8,128)} %bitcast.4), kind=kOutput, calls=%fused_computation.21 | convolution fusion | flops 12901679104 | bytes 12582912 | tf_op jit(solution)/shard_map/kr,prc->pkc/dot_general | solution.py:35
  314.0 5.3 %copy.121 = f32[1,1024,1024]{2,1,0:T(8,128)} copy(f32[1,1024,1024]{1,2,0:T(8,128)} %subtract_bitcast_fusion) | data formatting | bytes 8388608 | tf_op jit(solution)/shard_map/sub | solution.py:35
  319.4 4.9 %reshape.739 = f32[8192,128]{1,0:T(8,128)} reshape(f32[1,1024,1024]{2,1,0:T(8,128)} %copy.121) | data formatting | bytes 8388608 | tf_op jit(solution)/shard_map/reshape | solution.py:89
  324.3 3.2 gather_fusion.8
  327.5 3.5 gather_fusion.7
  331.0 1.1 fusion.42
  332.2 1.1 copy.124
  333.4 10.4 %all-to-all-start.2 = ((f32[128,4,2,128]{3,1,2,0:T(4,128)}), f32[128,4,2,128]{3,1,2,0:T(4,128)S(1)}, u32[]{:S(2)}, u32[]{:S(2)}) async-start(f32[128,4,2,128]{3,1,2,0:T(4,128)} %copy.124), calls=%async_computation.2 | async-start | bytes 1048576 | tf_op jit(solution)/shard_map/all_to_all | solution.py:131
  343.8 0.2 dynamic-slice_reduce_fusion
  344.0 13.5 %all-to-all-done.2 = f32[128,4,2,128]{3,1,2,0:T(4,128)S(1)} async-done(((f32[128,4,2,128]{3,1,2,0:T(4,128)}), f32[128,4,2,128]{3,1,2,0:T(4,128)S(1)}, u32[]{:S(2)}, u32[]{:S(2)}) %all-to-all-start.2) | async-done | bytes 524320 | tf_op jit(solution)/shard_map/all_to_all | solution.py:131
  357.5 0.3 copy.125
  357.8 0.6 gather_fusion.9
  358.4 0.6 gather_fusion.10
  359.0 0.6 add.433
  (47 shorter events, 1.1 us)
Async XLA Ops:
  0.0 110.5 %copy-start = (f32[512]{0:T(512)S(1)}, f32[512]{0:T(512)}, u32[]{:S(2)}) copy-start(f32[512]{0:T(512)} %param.13) | copy-start | bytes 6148
  31.0 59.4 %all-to-all-start = ((f32[32,32,1024]{2,1,0:T(8,128)}), f32[32,32,1024]{2,1,0:T(8,128)}, u32[]{:S(2)}, u32[]{:S(2)}) async-start(f32[32,32,1024]{2,1,0:T(8,128)} %fusion.14), calls=%async_computation | async-start | bytes 8388608 | tf_op jit(solution)/shard_map/all_to_all | solution.py:121
  71.2 27.3 %copy-start.1 = (s32[512,8]{0,1:T(8,128)S(1)}, s32[512,8]{0,1:T(8,128)}, u32[]{:S(2)}) copy-start(s32[512,8]{0,1:T(8,128)} %param.10) | copy-start | bytes 49156
  71.2 28.0 %copy-start.2 = (s32[512,8]{0,1:T(8,128)S(1)}, s32[512,8]{0,1:T(8,128)}, u32[]{:S(2)}) copy-start(s32[512,8]{0,1:T(8,128)} %param.8) | copy-start | bytes 49156
  71.2 29.0 %copy-start.3 = (s32[512,8]{0,1:T(8,128)S(1)}, s32[512,8]{0,1:T(8,128)}, u32[]{:S(2)}) copy-start(s32[512,8]{0,1:T(8,128)} %param.9) | copy-start | bytes 49156
  90.4 72.7 %all-to-all-start.1 = ((f32[32,32,1024]{2,1,0:T(8,128)}), f32[32,32,1024]{2,1,0:T(8,128)}, u32[]{:S(2)}, u32[]{:S(2)}) async-start(f32[32,32,1024]{2,1,0:T(8,128)} %negate_bitcast_fusion), calls=%async_computation.1 | async-start | bytes 8388608 | tf_op jit(solution)/shard_map/all_to_all | solution.py:122
  98.5 8.4 %copy-start.4 = (f32[512,8]{0,1:T(8,128)S(1)}, f32[512,8]{0,1:T(8,128)}, u32[]{:S(2)}) copy-start(f32[512,8]{0,1:T(8,128)} %param.12) | copy-start | bytes 49156
  103.7 11.0 %copy-start.5 = (f32[512,8]{0,1:T(8,128)S(1)}, f32[512,8]{0,1:T(8,128)}, u32[]{:S(2)}) copy-start(f32[512,8]{0,1:T(8,128)} %param.11) | copy-start | bytes 49156
  163.1 44.6 %copy-start.6 = (f32[1024,1024]{1,0:T(8,128)S(1)}, f32[1024,1024]{1,0:T(8,128)}, u32[]{:S(2)}) copy-start(f32[1024,1024]{1,0:T(8,128)} %fusion.11) | copy-start | bytes 12582916
  333.4 24.2 %all-to-all-start.2 = ((f32[128,4,2,128]{3,1,2,0:T(4,128)}), f32[128,4,2,128]{3,1,2,0:T(4,128)S(1)}, u32[]{:S(2)}, u32[]{:S(2)}) async-start(f32[128,4,2,128]{3,1,2,0:T(4,128)} %copy.124), calls=%async_computation.2 | async-start | bytes 1048576 | tf_op jit(solution)/shard_map/all_to_all | solution.py:131

commit v2 on v1

v2 whole, which is shorter than its diff:
```python
import math

import jax
import jax.numpy as jnp
from jax import lax
from jax.sharding import PartitionSpec as P

LANES = 128
SPLIT = 8


CTF_SCALE = 20.0
CTF_PHASE = 0.07
HIGH = lax.Precision.HIGHEST


def roots(rows, cols, length, factor):
    phase = rows * cols % length
    angle = phase.astype(jnp.float32) * (2.0 * math.pi / length)
    return (jnp.cos(angle) * factor, -jnp.sin(angle) * factor)


def small_dft(length):
    re, im = [], []
    for k in range(length):
        re.append([round(math.cos(2 * math.pi * k * n / length), 15) for n in range(length)])
        im.append([round(-math.sin(2 * math.pi * k * n / length), 15) for n in range(length)])
    return re, im


def combine(coef, pieces):
    total = None
    for c, piece in zip(coef, pieces):
        if c == 0.0:
            continue
        term = piece if c == 1.0 else (-piece if c == -1.0 else c * piece)
        total = term if total is None else total + term
    return total


def row_fft(plane):
    own, n, x = plane.shape
    m = n // SPLIT
    c8, s8 = small_dft(SPLIT)
    slabs = [plane[:, j * m:(j + 1) * m, :] for j in range(SPLIT)]
    a_re = jnp.stack([combine(c8[k], slabs) for k in range(SPLIT)], axis=1)
    a_im = jnp.stack(
        [combine(s8[k], slabs) if k != 0 else jnp.zeros_like(slabs[0]) for k in range(SPLIT)],
        axis=1,
    )
    k1 = lax.iota(jnp.int32, SPLIT)[:, None]
    n2 = lax.iota(jnp.int32, m)[None, :]
    t_re, t_im = roots(k1, n2, n, 1.0)
    t_re = t_re[None, :, :, None]
    t_im = t_im[None, :, :, None]
    b_re = a_re * t_re - a_im * t_im
    b_im = a_re * t_im + a_im * t_re
    idx = lax.iota(jnp.int32, m)
    w_re, w_im = roots(idx[:, None], idx[None, :], m, 1.0 / math.sqrt(n))
    mm = lambda w, b: jnp.einsum("kn,pjnc->pjkc", w, b, precision=HIGH)
    v_re = mm(w_re, b_re) - mm(w_im, b_im)
    v_im = mm(w_re, b_im) + mm(w_im, b_re)
    return v_re.reshape(own * n, x), v_im.reshape(own * n, x)


def column_fft_block(r_re, r_im, cols, box):
    s, x = r_re.shape
    m = x // SPLIT
    t_re = jnp.swapaxes(r_re.reshape(s, m, SPLIT), 1, 2)
    t_im = jnp.swapaxes(r_im.reshape(s, m, SPLIT), 1, 2)
    idx = lax.iota(jnp.int32, m)
    w_re, w_im = roots(idx[:, None], idx[None, :], m, 1.0 / math.sqrt(x))
    mm = lambda a, w: jnp.einsum("sjn,nl->sjl", a, w, precision=HIGH)
    y_re = mm(t_re, w_re) - mm(t_im, w_im)
    y_im = mm(t_re, w_im) + mm(t_im, w_re)
    n1 = lax.iota(jnp.int32, SPLIT)
    lane = lax.iota(jnp.int32, LANES)
    column_x = cols[:, None, None] * LANES + lane[None, None, :]
    g_re, g_im = roots(n1[None, :, None], column_x, box, 1.0)
    out_re = jnp.sum(g_re * y_re - g_im * y_im, axis=1)
    out_im = jnp.sum(g_re * y_im + g_im * y_re, axis=1)
    return out_re, out_im


def slot_tables(blk_plane, n_dev):
    plane = blk_plane.reshape(n_dev, -1)
    k_dev = plane.shape[1]
    order = lax.iota(jnp.int32, k_dev)
    same = plane[:, :, None] == plane[:, None, :]
    earlier = order[None, None, :] < order[None, :, None]
    rank = jnp.sum((same & earlier).astype(jnp.int32), axis=2)
    return plane, rank


def send_parts(v_re, v_im, first_plane, own, meta, box, n_dev):
    blk_plane, blk_row, blk_col, frac_plane, frac_row, defocus = meta
    n_blk = blk_plane.shape[1]
    plane, rank = slot_tables(blk_plane, n_dev)
    k_dev = plane.shape[1]
    t = lax.iota(jnp.int32, own)[:, None, None]
    side = lax.iota(jnp.int32, 2)[None, :, None]
    u = lax.iota(jnp.int32, 2)[None, None, :]
    target = first_plane + t - side
    match = (plane[:, None, None, None, :] == target[None, :, :, :, None]) & (
        rank[:, None, None, None, :] == u[None, :, :, :, None]
    )
    valid = jnp.any(match, axis=-1)
    kidx = jnp.sum(jnp.where(match, lax.iota(jnp.int32, k_dev), 0), axis=-1)
    g = lax.iota(jnp.int32, n_dev)[:, None, None, None] * k_dev + kidx
    g = g.reshape(-1)
    rows = blk_row.reshape(-1)[g]
    cols = blk_col.reshape(-1)[g]
    frac_z = frac_plane.reshape(-1)[g]
    frac_y = frac_row.reshape(-1)[g][:, None]
    focus = defocus[g // n_blk]
    side_f = jnp.broadcast_to(side, (n_dev, own, 2, 2)).reshape(-1)
    valid = valid.reshape(-1)
    t_idx = jnp.broadcast_to(t, (n_dev, own, 2, 2)).reshape(-1)
    lane = lax.iota(jnp.int32, LANES)
    column_x = cols[:, None] * LANES + lane[None, :]
    fold_x = jnp.minimum(column_x, box - column_x).astype(jnp.float32)
    fold_y = jnp.minimum(rows, box - rows).astype(jnp.float32)
    wave_sq = (fold_x * fold_x + (fold_y * fold_y)[:, None]) / float(box * box)
    ctf_value = -jnp.sin(CTF_SCALE * focus[:, None] * wave_sq + CTF_PHASE)
    m = box // SPLIT

    def stored(r):
        return t_idx * box + (r % SPLIT) * m + r // SPLIT

    index_low = stored(rows)
    index_high = stored(rows + 1)
    weight = jnp.where(side_f == 0, 1.0 - frac_z, frac_z)
    weight = jnp.where(valid, weight, 0.0)
    scale = weight[:, None] * ctf_value
    r_re = (1.0 - frac_y) * v_re[index_low] + frac_y * v_re[index_high]
    r_im = (1.0 - frac_y) * v_im[index_low] + frac_y * v_im[index_high]
    o_re, o_im = column_fft_block(r_re, r_im, cols, box)
    parts = jnp.stack([scale * o_re, scale * o_im], axis=1)
    return parts.reshape(n_dev, own * 4, 2, LANES)


def gather_parts(recv, blk_plane, me, own, n_slab, n_img):
    n_dev = n_slab * n_img
    plane, rank = slot_tables(blk_plane, n_dev)
    mine = plane[me]
    my_rank = rank[me]
    slots = own * 4

    def place(q, side):
        holder = q // own
        src = (holder % n_slab) * n_img + holder // n_slab
        return src * slots + (q % own) * 4 + side * 2 + my_rank

    flat = recv.reshape(-1, 2, LANES)
    return flat[place(mine, 0)] + flat[place(mine + 1, 1)]


def on_device(volume, blk_plane, blk_row, blk_col, frac_plane, frac_row, defocus):
    box = volume.shape[2]
    n_slab = lax.axis_size("slab")
    n_img = lax.axis_size("img")
    n_dev = n_slab * n_img
    plane = lax.all_to_all(volume, "slab", split_axis=0, concat_axis=1, tiled=True)
    own = plane.shape[0]
    v_re, v_im = row_fft(plane)
    first_plane = (lax.axis_index("img") * n_slab + lax.axis_index("slab")) * own
    meta = (blk_plane, blk_row, blk_col, frac_plane, frac_row, defocus)
    parts = send_parts(v_re, v_im, first_plane, own, meta, box, n_dev)
    recv = lax.all_to_all(parts, ("slab", "img"), split_axis=0, concat_axis=0, tiled=True)
    me = lax.axis_index("slab") * n_img + lax.axis_index("img")
    total = gather_parts(recv, blk_plane, me, own, n_slab, n_img)
    n_blk = blk_plane.shape[1]
    return total.reshape(-1, n_blk, 2, LANES)


def solution(mesh):
    placed = (P("img", "slab", None), P(), P(), P(), P(), P(), P())
    return jax.shard_map(
        on_device,
        mesh=mesh,
        in_specs=placed,
        out_specs=P(("slab", "img"), None, None, None),
        check_vma=False,
    )
```

time: 367 us -> 216 us (0.59)
  matrix products: 241 us -> 54 us
  other arithmetic: 2.33 us -> 36.9 us
  waiting for transfers between devices: 32.7 us -> 42.9 us
  starting transfers between devices: 27.5 us -> 17.5 us
  local copies, waits for them, and re-layouts: 55.6 us -> 60.2 us
    dot_general x6 -> x8, matrix products: 241 us -> 54 us  [the longest x4 33.5 us: row_fft(): mm = lambda w, b: jnp.einsum('kn,pjnc->pjkc', w, b, precision=HIGH)]
    unnamed x0 -> x11, other arithmetic: none -> 23.8 us
    gather x4 -> x8, local copies, waits for them, and re-layouts: 13.2 us -> 32.3 us  [the longest x4 16.5 us: send_parts(): r_im = (1.0 - frac_y) * v_im[index_low] + frac_y * v_im[index_high]]
    all_to_all x2 -> x1, waiting for transfers between devices: 19.2 us -> 29.3 us  [on_device(): lax.all_to_all(volume, 'slab', split_axis=0, concat_axis=1, tiled=True)]
    reshape x2 -> x1, local copies, waits for them, and re-layouts: 9.8 us -> 0.41 us  [gather_parts(): flat = recv.reshape(-1, 2, LANES)]
    all_to_all x2 -> x1, starting transfers between devices: 17.1 us -> 8.77 us  [on_device(): lax.all_to_all(volume, 'slab', split_axis=0, concat_axis=1, tiled=True)]
    transpose x0 -> x1, other arithmetic: none -> 6.64 us  [column_fft_block(): t_im = jnp.swapaxes(r_im.reshape(s, m, SPLIT), 1, 2)]
    add x1 -> x0, local copies, waits for them, and re-layouts: 5.36 us -> none  [row_transform(): jnp.einsum('kr,prc->pkc', cosine, real_part, precision=HIGH)]
  transfers between devices with their start and end apart: 3 -> 2, of which waited for: 2 -> 2; matrix products, arithmetic and copies ran while one was open for 27% -> 10% of each run, Pallas kernels for 0% -> 0%
where the time goes in v2:
time: 216 us; the launch traced here: 212 us
  local copies, waits for them, and re-layouts  60.2 us (28%)
  matrix products  54 us (25%)
  waiting for transfers between devices  42.9 us (20%)
  other arithmetic  36.9 us (17%)
  starting transfers between devices  17.5 us (8%)
    dot_general x4, matrix products, row_fft(): mm = lambda w, b: jnp.einsum('kn,pjnc->pjkc', w, b, precision=HIGH)  33.5 us
    all_to_all x1, waiting for transfers between devices, on_device(): lax.all_to_all(volume, 'slab', split_axis=0, concat_axis=1, tiled=True)  29.3 us
    unnamed x11, other arithmetic  23.8 us
    dot_general x4, matrix products, column_fft_block(): mm = lambda a, w: jnp.einsum('sjn,nl->sjl', a, w, precision=HIGH)  20.5 us
    gather x4, local copies, waits for them, and re-layouts, send_parts(): r_im = (1.0 - frac_y) * v_im[index_low] + frac_y * v_im[index_high]  16.5 us
    gather x4, local copies, waits for them, and re-layouts, send_parts(): r_re = (1.0 - frac_y) * v_re[index_low] + frac_y * v_re[index_high]  15.8 us
    all_to_all x1, waiting for transfers between devices, on_device(): lax.all_to_all(parts, ('slab', 'img'), split_axis=0, concat_axis=0, tiled...  13.5 us
    all_to_all x1, starting transfers between devices, on_device(): lax.all_to_all(volume, 'slab', split_axis=0, concat_axis=1, tiled=True)  8.77 us
  transfers between devices with their start and end apart: 2, of which 2 were waited for; matrix products, arithmetic and copies ran while one was open for 10% of the time, Pallas kernels for 0%

profile of v2, /device:TPU:1, one launch (start us, length us, event | category | flops | bytes accessed | tf_op | source)
XLA Modules:
  0.0 212.2 jit_solution(29364945358003358)
XLA Ops:
  0.0 8.8 %all-to-all-start = ((f32[32,32,1024]{2,1,0:T(8,128)}), f32[32,32,1024]{2,1,0:T(8,128)}, u32[]{:S(2)}, u32[]{:S(2)}) async-start(f32[32,32,1024]{2,1,0:T(8,128)} %param.7), calls=%async_computation | async-start | bytes 8388608 | tf_op jit(solution)/shard_map/all_to_all | solution.py:163
  9.2 0.2 convert_reduce_fusion
  10.9 3.1 %gather_fusion.2 = s32[512]{0:T(512)S(1)} fusion(s32[4096]{0:T(1024)S(1)} %reshape.1128, s32[1024]{0:T(1024)S(1)} %pad_clamp_fusion.5), kind=kCustom, calls=%fused_computation.2 | custom fusion | bytes 6144 | tf_op jit(solution)/shard_map/gather | solution.py:111
  14.0 3.1 %gather_fusion.4 = f32[512]{0:T(512)S(1)} fusion(f32[4096]{0:T(1024)S(1)} %reshape.1129, s32[1024]{0:T(1024)S(1)} %pad_clamp_fusion.5), kind=kCustom, calls=%fused_computation.4 | custom fusion | bytes 6144 | tf_op jit(solution)/shard_map/gather | solution.py:114
  17.5 3.1 %gather_fusion.1 = s32[512]{0:T(512)S(1)} fusion(s32[4096]{0:T(1024)S(1)} %reshape.1127, s32[1024]{0:T(1024)S(1)} %pad_clamp_fusion.5), kind=kCustom, calls=%fused_computation.1 | custom fusion | bytes 6144 | tf_op jit(solution)/shard_map/gather | solution.py:112
  20.9 3.1 %gather_fusion = f32[512]{0:T(512)S(1)} fusion(f32[4096]{0:T(1024)S(1)} %reshape.1126, s32[1024]{0:T(1024)S(1)} %pad_clamp_fusion.5), kind=kCustom, calls=%fused_computation | custom fusion | bytes 6144 | tf_op jit(solution)/shard_map/gather | solution.py:113
  24.8 4.0 %gather_fusion.3 = f32[512]{0:T(512)S(1)} fusion(f32[512]{0:T(512)S(1)} %copy-done, s32[1024]{0:T(1024)S(1)} %pad_clamp_fusion.4), kind=kCustom, calls=%fused_computation.3 | custom fusion | bytes 6144 | tf_op jit(solution)/shard_map/gather | solution.py:115
  29.1 0.9 broadcast_dynamic-update-slice_fusion
  30.1 29.3 %all-to-all-done = f32[32,32,1024]{2,1,0:T(8,128)} async-done(((f32[32,32,1024]{2,1,0:T(8,128)}), f32[32,32,1024]{2,1,0:T(8,128)}, u32[]{:S(2)}, u32[]{:S(2)}) %all-to-all-start) | async-done | bytes 4194336 | tf_op jit(solution)/shard_map/all_to_all | solution.py:163
  59.5 2.5 %add_dynamic-update-slice_fusion.12 = f32[8,128,1024]{2,1,0:T(8,128)S(1)} fusion(f32[1,1024,1024]{2,1,0:T(8,128)} %bitcast.2), kind=kLoop, calls=%fused_computation.55 | loop fusion | flops 917503 | bytes 4718592
  62.0 2.2 %constant_dynamic-update-slice_fusion.1 = (f32[8,128,1024]{2,1,0:T(8,128)S(1)}, f32[1,128,1024]{2,1,0:T(8,128)S(1)}) fusion(f32[8,128,1024]{2,1,0:T(8,128)S(1)} %add_dynamic-update-slice_fusion.12, f32[1,1024,1024]{2,1,0:T(8,128)} %bitcast.2), kind=kLoop, calls=%fused_computation.96 | loop fusion | flops 1310720 | bytes 4194304
  64.2 1.7 add_dynamic-update-slice_fusion.11
  65.9 2.5 %add_dynamic-update-slice_fusion.10 = (f32[8,128,1024]{2,1,0:T(8,128)S(1)}, f32[1,128,1024]{2,1,0:T(8,128)S(1)}) fusion(f32[8,128,1024]{2,1,0:T(8,128)S(1)} %add_dynamic-update-slice_fusion.11, f32[1,1024,1024]{2,1,0:T(8,128)} %bitcast.2), kind=kLoop, calls=%fused_computation.51 | loop fusion | flops 1572864 | bytes 4718592
  68.4 2.6 %add_dynamic-update-slice_fusion.9 = f32[8,128,1024]{2,1,0:T(8,128)S(1)} fusion(f32[8,128,1024]{2,1,0:T(8,128)S(1)} %get-tuple-element.7, f32[1,1024,1024]{2,1,0:T(8,128)} %bitcast.2), kind=kLoop, calls=%fused_computation.50 | loop fusion | flops 1441792 | bytes 4718592
  71.0 2.2 %add_dynamic-update-slice_fusion.8 = (f32[8,128,1024]{2,1,0:T(8,128)S(1)}, f32[8,128,1024]{2,1,0:T(8,128)S(1)}) fusion(f32[8,128,1024]{2,1,0:T(8,128)S(1)} %add_dynamic-update-slice_fusion.9, f32[1,128,1024]{2,1,0:T(8,128)S(1)} %get-tuple-element.8, f32[1,1024,1024]{2,1,0:T(8,128)} %bitcast.2, f32[8,128,1024]{2,1,0:T(8,128)S(1)} %copy-done.2), kind=kLoop, calls=%fused_computation.49 | loop fusion | flops 1835008 | bytes 4718592
  73.2 1.7 add_dynamic-update-slice_fusion.5
  74.9 2.2 %add_dynamic-update-slice_fusion.4 = f32[8,128,1024]{2,1,0:T(8,128)S(1)} fusion(f32[8,128,1024]{2,1,0:T(8,128)S(1)} %add_dynamic-update-slice_fusion.5, f32[1,1024,1024]{2,1,0:T(8,128)} %bitcast.2), kind=kLoop, calls=%fused_computation.45 | loop fusion | flops 1310720 | bytes 3670016
  77.1 1.5 add_dynamic-update-slice_fusion.3
  78.6 2.6 %add_dynamic-update-slice_fusion.7 = (f32[8,128,1024]{2,1,0:T(8,128)S(1)}, f32[8,128,1024]{2,1,0:T(8,128)S(1)}) fusion(f32[8,128,1024]{2,1,0:T(8,128)S(1)} %get-tuple-element.13, f32[1,1024,1024]{2,1,0:T(8,128)} %bitcast.2, f32[8,128,1024]{2,1,0:T(8,128)S(1)} %add_dynamic-update-slice_fusion.3), kind=kLoop, calls=%fused_computation.48 | loop fusion | flops 2621440 | bytes 5242880
  81.2 2.2 %add_dynamic-update-slice_fusion.1 = (f32[8,128,1024]{2,1,0:T(8,128)S(1)}, f32[8,128,1024]{2,1,0:T(8,128)S(1)}) fusion(f32[8,128,1024]{2,1,0:T(8,128)S(1)} %get-tuple-element.12, f32[1,1024,1024]{2,1,0:T(8,128)} %bitcast.2, f32[8,128,1024]{2,1,0:T(8,128)S(1)} %get-tuple-element.11, f32[1,128,1024]{2,1,0:T(8,128)S(1)} %get-tuple-element.10), kind=kLoop, calls=%fused_computation.42 | loop fusion | flops 1179648 | bytes 4718592
  83.4 3.9 %add_dynamic-update-slice_fusion = f32[8,128,1024]{2,1,0:T(8,128)S(1)} fusion(f32[8,128,1024]{2,1,0:T(8,128)S(1)} %get-tuple-element.25, f32[1,1024,1024]{2,1,0:T(8,128)} %bitcast.2), kind=kLoop, calls=%fused_computation.41 | loop fusion | flops 1572864 | bytes 4194304 | tf_op jit(solution)/shard_map/stack | solution.py:47
  87.3 6.4 %fusion.10 = f32[8,1024,128]{1,2,0:T(8,128)S(1)} fusion(f32[8,128,1024]{2,1,0:T(8,128)S(1)} %add_dynamic-update-slice_fusion, f32[8,128,1024]{2,1,0:T(8,128)S(1)} %get-tuple-element.26, f32[8,128]{1,0:T(8,128)S(1)} %get-tuple-element.27, f32[8,128]{1,0:T(8,128)S(1)} %get-tuple-element.28), kind=kOutput, calls=%fused_computation.37 | convolution fusion | flops 1614004224 | bytes 12591104 | tf_op jit(solution)/shard_map/kn,pjnc->pjkc/dot_general | solution.py:60
  93.7 6.8 %fusion.11 = f32[8,1024,128]{1,2,0:T(8,128)} fusion(f32[8,128,1024]{2,1,0:T(8,128)S(1)} %add_dynamic-update-slice_fusion, f32[8,128,1024]{2,1,0:T(8,128)S(1)} %get-tuple-element.26, f32[8,128]{1,0:T(8,128)S(1)} %get-tuple-element.27, f32[8,128]{1,0:T(8,128)S(1)} %get-tuple-element.28), kind=kOutput, calls=%fused_computation.38 | convolution fusion | flops 1614004224 | bytes 12591104 | tf_op jit(solution)/shard_map/kn,pjnc->pjkc/dot_general | solution.py:60
  100.6 6.7 %convolution_subtract_fusion = f32[8,1024,128]{1,2,0:T(8,128)} fusion(f32[8,1024,128]{1,2,0:T(8,128)S(1)} %fusion.10, f32[8,128,1024]{2,1,0:T(8,128)S(1)} %add_dynamic-update-slice_fusion, f32[8,128,1024]{2,1,0:T(8,128)S(1)} %get-tuple-element.26, f32[8,128]{1,0:T(8,128)S(1)} %get-tuple-element.27, f32[8,128]{1,0:T(8,128)S(1)} %get-tuple-element.28), kind=kOutput, calls=%fused_computation.17 | convolution fusion | flops 1615069184 | bytes 16785408 | tf_op jit(solution)/shard_map/kn,pjnc->pjkc/dot_general | solution.py:60
  107.3 5.8 %gather_fusion.5 = f32[512,1024]{1,0:T(8,128)} fusion(f32[1024,1024]{1,0:T(8,128)} %bitcast.105, s32[1024]{0:T(1024)S(1)} %pad_clamp_fusion.3), kind=kCustom, calls=%fused_computation.5 | custom fusion | bytes 4196352 | tf_op jit(solution)/shard_map/gather | solution.py:135
  113.1 5.2 %gather_fusion.6 = f32[512,1024]{1,0:T(8,128)S(1)} fusion(f32[1024,1024]{1,0:T(8,128)} %bitcast.106, s32[1024]{0:T(1024)S(1)} %pad_clamp_fusion.2), kind=kCustom, calls=%fused_computation.6 | custom fusion | bytes 4196352 | tf_op jit(solution)/shard_map/gather | solution.py:135
  118.3 13.5 %convolution_add_fusion = f32[8,1024,128]{1,2,0:T(8,128)} fusion(f32[8,1024,128]{1,2,0:T(8,128)} %fusion.11, f32[8,128,1024]{2,1,0:T(8,128)} %copy-done.3, f32[8,128,1024]{2,1,0:T(8,128)} %copy-done.4, f32[8,128]{1,0:T(8,128)S(1)} %get-tuple-element.27, f32[8,128]{1,0:T(8,128)S(1)} %get-tuple-element.28), kind=kOutput, calls=%fused_computation.16 | convolution fusion | flops 1615069184 | bytes 16785408 | tf_op jit(solution)/shard_map/kn,pjnc->pjkc/dot_general | solution.py:60
  131.8 5.8 %gather_fusion.7 = f32[512,1024]{1,0:T(8,128)} fusion(f32[1024,1024]{1,0:T(8,128)} %bitcast.103, s32[1024]{0:T(1024)S(1)} %pad_clamp_fusion.3), kind=kCustom, calls=%fused_computation.7 | custom fusion | bytes 4196352 | tf_op jit(solution)/shard_map/gather | solution.py:136
  137.6 5.8 %gather_fusion.8 = f32[512,1024]{1,0:T(8,128)} fusion(f32[1024,1024]{1,0:T(8,128)} %bitcast.104, s32[1024]{0:T(1024)S(1)} %pad_clamp_fusion.2), kind=kCustom, calls=%fused_computation.8 | custom fusion | bytes 4196352 | tf_op jit(solution)/shard_map/gather | solution.py:136
  143.4 2.9 %copy.161 = f32[512,1024]{0,1:T(8,128)} copy(f32[512,1024]{1,0:T(8,128)} %gather_fusion.5) | data formatting | bytes 4194304 | tf_op jit(solution)/shard_map/gather | solution.py:135
  146.4 1.8 copy.162
  148.2 3.1 %copy.164 = f32[512,1024]{0,1:T(8,128)} copy(f32[512,1024]{1,0:T(8,128)} %gather_fusion.7) | data formatting | bytes 4194304 | tf_op jit(solution)/shard_map/gather | solution.py:136
  151.2 1.9 copy.165
  153.1 6.6 %fusion.4 = (f32[512,8,128]{0,1,2:T(8,128)}, f32[512,8,128]{0,1,2:T(8,128)}) fusion(f32[512,1024]{0,1:T(8,128)} %copy.165, f32[512,1024]{0,1:T(8,128)} %copy.164, f32[512]{0:T(512)S(1)} %gather_fusion.4, f32[512]{0:T(512)S(1)} %broadcast_subtract_fusion, f32[512,1024]{0,1:T(8,128)} %copy.162, f32[512,1024]{0,1:T(8,128)} %copy.161), kind=kLoop, calls=%fused_computation.23 | loop fusion | flops 3145728 | bytes 12587008 | tf_op jit(solution)/shard_map/transpose | solution.py:70
  159.7 2.0 copy.163
  161.7 3.4 %fusion.32 = f32[512,8,128]{2,0,1:T(8,128)} fusion(f32[512,8,128]{2,0,1:T(8,128)S(1)} %copy.163), kind=kOutput, calls=%fused_computation.87 | convolution fusion | flops 805552128 | bytes 4194304 | tf_op jit(solution)/shard_map/sjn,nl->sjl/dot_general | solution.py:73
  165.1 3.4 %fusion.25 = f32[512,8,128]{2,0,1:T(8,128)} fusion(f32[512,8,128]{2,0,1:T(8,128)S(1)} %copy.163), kind=kOutput, calls=%fused_computation.80 | convolution fusion | flops 805568512 | bytes 4194304 | tf_op jit(solution)/shard_map/sjn,nl->sjl/dot_general | solution.py:73
  168.4 2.4 %copy.166 = f32[512,8,128]{2,0,1:T(8,128)S(1)} copy(f32[512,8,128]{0,1,2:T(8,128)} %get-tuple-element.21) | data formatting | bytes 4194304 | tf_op jit(solution)/shard_map/transpose | solution.py:70
  170.9 3.9 %convolution_subtract_fusion.1 = f32[512,8,128]{2,0,1:T(8,128)S(1)} fusion(f32[512,8,128]{2,0,1:T(8,128)} %fusion.32, f32[512,8,128]{2,0,1:T(8,128)S(1)} %copy.166), kind=kOutput, calls=%fused_computation.36 | convolution fusion | flops 806092800 | bytes 6291456 | tf_op jit(solution)/shard_map/sjn,nl->sjl/dot_general | solution.py:73
  174.7 10.0 %subtract_reduce_fusion = (f32[512,128]{1,0:T(8,128)S(1)}, f32[512,128]{1,0:T(8,128)S(1)}) fusion(f32[512,8,128]{2,0,1:T(8,128)S(1)} %convolution_subtract_fusion.1, s32[512,128]{1,0:T(8,128)S(1)} %iota_add_fusion, f32[512,8,128]{2,0,1:T(8,128)S(1)} %copy-done.6, f32[512,8,128]{2,0,1:T(8,128)S(1)} %copy.166), kind=kOutput, calls=%fused_computation.30 | convolution fusion | flops 818003968 | bytes 7077888 | tf_op jit(solution)/shard_map/sjn,nl->sjl/dot_general | solution.py:73
  184.7 1.1 copy_multiply_fusion.1
  185.8 1.2 copy.171
  187.0 8.8 %all-to-all-start.1 = ((f32[128,4,2,128]{3,2,1,0:T(2,128)}), f32[128,4,2,128]{3,2,1,0:T(2,128)S(1)}, u32[]{:S(2)}, u32[]{:S(2)}) async-start(f32[128,4,2,128]{3,2,1,0:T(2,128)} %copy.171), calls=%async_computation.1 | async-start | bytes 1048576 | tf_op jit(solution)/shard_map/all_to_all | solution.py:169
  196.0 13.5 %all-to-all-done.1 = f32[128,4,2,128]{3,2,1,0:T(2,128)S(1)} async-done(((f32[128,4,2,128]{3,2,1,0:T(2,128)}), f32[128,4,2,128]{3,2,1,0:T(2,128)S(1)}, u32[]{:S(2)}, u32[]{:S(2)}) %all-to-all-start.1) | async-done | bytes 524320 | tf_op jit(solution)/shard_map/all_to_all | solution.py:169
  209.7 0.4 copy.173
  210.1 0.6 gather_fusion.10
  210.7 0.6 gather_fusion.9
  211.3 0.6 add.804
  (74 shorter events, 3.8 us)
Async XLA Ops:
  0.0 24.7 %copy-start = (f32[512]{0:T(512)S(1)}, f32[512]{0:T(512)}, u32[]{:S(2)}) copy-start(f32[512]{0:T(512)} %param.13) | copy-start | bytes 6148
  0.0 8.8 %copy-start.7 = (s32[512,8]{0,1:T(8,128)S(1)}, s32[512,8]{0,1:T(8,128)}, u32[]{:S(2)}) copy-start(s32[512,8]{0,1:T(8,128)} %param.8) | copy-start | bytes 49156
  0.0 10.3 %copy-start.8 = (s32[512,8]{0,1:T(8,128)S(1)}, s32[512,8]{0,1:T(8,128)}, u32[]{:S(2)}) copy-start(s32[512,8]{0,1:T(8,128)} %param.9) | copy-start | bytes 49156
  0.0 10.6 %copy-start.9 = (f32[512,8]{0,1:T(8,128)S(1)}, f32[512,8]{0,1:T(8,128)}, u32[]{:S(2)}) copy-start(f32[512,8]{0,1:T(8,128)} %param.12) | copy-start | bytes 49156
  0.0 59.5 %all-to-all-start = ((f32[32,32,1024]{2,1,0:T(8,128)}), f32[32,32,1024]{2,1,0:T(8,128)}, u32[]{:S(2)}, u32[]{:S(2)}) async-start(f32[32,32,1024]{2,1,0:T(8,128)} %param.7), calls=%async_computation | async-start | bytes 8388608 | tf_op jit(solution)/shard_map/all_to_all | solution.py:163
  8.8 8.4 %copy-start.10 = (s32[512,8]{0,1:T(8,128)S(1)}, s32[512,8]{0,1:T(8,128)}, u32[]{:S(2)}) copy-start(s32[512,8]{0,1:T(8,128)} %param.10) | copy-start | bytes 49156
  9.7 11.0 %copy-start.11 = (f32[512,8]{0,1:T(8,128)S(1)}, f32[512,8]{0,1:T(8,128)}, u32[]{:S(2)}) copy-start(f32[512,8]{0,1:T(8,128)} %param.11) | copy-start | bytes 49156
  65.9 5.1 %copy-start.2 = (f32[8,128,1024]{2,1,0:T(8,128)S(1)}, f32[8,128,1024]{2,1,0:T(8,128)}, u32[]{:S(2)}) copy-start(f32[8,128,1024]{2,1,0:T(8,128)} %broadcast_dynamic-update-slice_fusion) | copy-start | bytes 12582916
  83.4 17.2 %copy-start.4 = (f32[8,128,1024]{2,1,0:T(8,128)}, f32[8,128,1024]{2,1,0:T(8,128)S(1)}, u32[]{:S(2)}) copy-start(f32[8,128,1024]{2,1,0:T(8,128)S(1)} %get-tuple-element.26) | copy-start | bytes 12582916
  87.3 13.3 %copy-start.3 = (f32[8,128,1024]{2,1,0:T(8,128)}, f32[8,128,1024]{2,1,0:T(8,128)S(1)}, u32[]{:S(2)}) copy-start(f32[8,128,1024]{2,1,0:T(8,128)S(1)} %add_dynamic-update-slice_fusion) | copy-start | bytes 12582916
  148.2 3.1 %copy-start.5 = (f32[512,1024]{1,0:T(8,128)S(1)}, f32[512,1024]{1,0:T(8,128)}, u32[]{:S(2)}) copy-start(f32[512,1024]{1,0:T(8,128)} %gather_fusion.8) | copy-start | bytes 6291460
  170.8 3.9 %copy-start.6 = (f32[512,8,128]{2,0,1:T(8,128)S(1)}, f32[512,8,128]{2,0,1:T(8,128)}, u32[]{:S(2)}) copy-start(f32[512,8,128]{2,0,1:T(8,128)} %fusion.25) | copy-start | bytes 6291460
  174.7 37.2 %copy-start.1 = (f32[512]{0:T(512)S(1)}, f32[512]{0:T(512)}, u32[]{:S(2)}) copy-start(f32[512]{0:T(512)} %param.13) | copy-start | bytes 6148
  187.0 22.5 %all-to-all-start.1 = ((f32[128,4,2,128]{3,2,1,0:T(2,128)}), f32[128,4,2,128]{3,2,1,0:T(2,128)S(1)}, u32[]{:S(2)}, u32[]{:S(2)}) async-start(f32[128,4,2,128]{3,2,1,0:T(2,128)} %copy.171), calls=%async_computation.1 | async-start | bytes 1048576 | tf_op jit(solution)/shard_map/all_to_all | solution.py:169

commit v3 on v1

v3 whole, which is shorter than its diff:
```python
import math

import jax
import jax.numpy as jnp
from jax import lax
from jax.sharding import PartitionSpec as P

LANES = 128
SPLIT = 8


CTF_SCALE = 20.0
CTF_PHASE = 0.07
MID = lax.Precision.HIGH


def roots(rows, cols, length, factor):
    phase = rows * cols % length
    angle = phase.astype(jnp.float32) * (2.0 * math.pi / length)
    return (jnp.cos(angle) * factor, -jnp.sin(angle) * factor)


def slot_tables(blk_plane, n_dev):
    plane = blk_plane.reshape(n_dev, -1)
    k_dev = plane.shape[1]
    order = lax.iota(jnp.int32, k_dev)
    same = plane[:, :, None] == plane[:, None, :]
    earlier = order[None, None, :] < order[None, :, None]
    rank = jnp.sum((same & earlier).astype(jnp.int32), axis=2)
    return plane, rank


def send_parts(plane, first_plane, meta, box, n_dev):
    blk_plane, blk_row, blk_col, frac_plane, frac_row, defocus = meta
    n_blk = blk_plane.shape[1]
    own, n_rows, x = plane.shape
    plane_of, rank = slot_tables(blk_plane, n_dev)
    k_dev = plane_of.shape[1]
    t = lax.iota(jnp.int32, own)[:, None, None, None]
    side = lax.iota(jnp.int32, 2)[None, None, :, None]
    u = lax.iota(jnp.int32, 2)[None, None, None, :]
    target = first_plane + t - side
    match = (plane_of[None, :, None, None, :] == target[..., None]) & (
        rank[None, :, None, None, :] == u[..., None]
    )
    valid = jnp.any(match, axis=-1)
    kidx = jnp.sum(jnp.where(match, lax.iota(jnp.int32, k_dev), 0), axis=-1)
    g = lax.iota(jnp.int32, n_dev)[None, :, None, None] * k_dev + kidx
    g = g.reshape(-1)
    rows = blk_row.reshape(-1)[g]
    cols = blk_col.reshape(-1)[g]
    frac_z = frac_plane.reshape(-1)[g]
    frac_y = frac_row.reshape(-1)[g][:, None]
    focus = defocus[g // n_blk]
    side_f = jnp.broadcast_to(side, (own, n_dev, 2, 2)).reshape(-1)
    valid = valid.reshape(-1)
    lane = lax.iota(jnp.int32, LANES)
    column_x = cols[:, None] * LANES + lane[None, :]
    fold_x = jnp.minimum(column_x, box - column_x).astype(jnp.float32)
    fold_y = jnp.minimum(rows, box - rows).astype(jnp.float32)
    wave_sq = (fold_x * fold_x + (fold_y * fold_y)[:, None]) / float(box * box)
    ctf_value = -jnp.sin(CTF_SCALE * focus[:, None] * wave_sq + CTF_PHASE)
    weight = jnp.where(side_f == 0, 1.0 - frac_z, frac_z)
    weight = jnp.where(valid, weight, 0.0)
    scale = weight[:, None] * ctf_value
    step = int(math.isqrt(n_rows))
    a = lax.iota(jnp.int32, n_rows // step)[None, :]
    b = lax.iota(jnp.int32, step)[None, :]

    def row_roots(r):
        a_re, a_im = roots(r[:, None], a * step, n_rows, 1.0)
        b_re, b_im = roots(r[:, None], b, n_rows, 1.0)
        w_re = a_re[:, :, None] * b_re[:, None, :] - a_im[:, :, None] * b_im[:, None, :]
        w_im = a_re[:, :, None] * b_im[:, None, :] + a_im[:, :, None] * b_re[:, None, :]
        return w_re.reshape(-1, n_rows), w_im.reshape(-1, n_rows)

    lo_re, lo_im = row_roots(rows)
    hi_re, hi_im = row_roots(rows + 1)
    norm = 1.0 / math.sqrt(n_rows)
    w_re = ((1.0 - frac_y) * lo_re + frac_y * hi_re) * norm
    w_im = ((1.0 - frac_y) * lo_im + frac_y * hi_im) * norm
    n_s = w_re.shape[0] // own
    w_all = jnp.stack([w_re.reshape(own, n_s, n_rows), w_im.reshape(own, n_s, n_rows)], axis=1)
    r_all = jnp.einsum("tpsr,trc->tpsc", w_all, plane, precision=MID)
    m = x // SPLIT
    r4 = r_all.reshape(own, 2, n_s, SPLIT, m)
    idx = lax.iota(jnp.int32, m)
    c_re, c_im = roots(idx[:, None], idx[None, :], m, 1.0 / math.sqrt(x))
    w_col = jnp.stack(
        [jnp.concatenate([c_re, c_im], axis=1), jnp.concatenate([-c_im, c_re], axis=1)], axis=0
    )
    y = jnp.einsum("tpsjn,pnl->tsjl", r4, w_col, precision=MID).reshape(own * n_s, SPLIT, 2 * m)
    y_re = y[:, :, :m]
    y_im = y[:, :, m:]
    n1 = lax.iota(jnp.int32, SPLIT)
    e_re, e_im = roots(cols[:, None], n1[None, :], SPLIT, 1.0)
    t_re, t_im = roots(n1[:, None], lane[None, :], box, 1.0)
    g_re = e_re[:, :, None] * t_re[None] - e_im[:, :, None] * t_im[None]
    g_im = e_re[:, :, None] * t_im[None] + e_im[:, :, None] * t_re[None]
    o_re = jnp.sum(g_re * y_re - g_im * y_im, axis=1)
    o_im = jnp.sum(g_re * y_im + g_im * y_re, axis=1)
    parts = jnp.stack([scale * o_re, scale * o_im], axis=1)
    parts = parts.reshape(own, n_dev, 4, 2, LANES)
    return jnp.swapaxes(parts, 0, 1).reshape(n_dev, own * 4, 2, LANES)


def gather_parts(recv, blk_plane, me, own, n_slab, n_img):
    n_dev = n_slab * n_img
    plane, rank = slot_tables(blk_plane, n_dev)
    mine = plane[me]
    my_rank = rank[me]
    slots = own * 4

    def place(q, side):
        holder = q // own
        src = (holder % n_slab) * n_img + holder // n_slab
        return src * slots + (q % own) * 4 + side * 2 + my_rank

    flat = recv.reshape(-1, 2, LANES)
    return flat[place(mine, 0)] + flat[place(mine + 1, 1)]


def on_device(volume, blk_plane, blk_row, blk_col, frac_plane, frac_row, defocus):
    box = volume.shape[2]
    n_slab = lax.axis_size("slab")
    n_img = lax.axis_size("img")
    n_dev = n_slab * n_img
    p_loc, r_loc, x = volume.shape
    spread = jnp.swapaxes(volume.reshape(p_loc, r_loc, x // SPLIT, SPLIT), 2, 3)
    spread = spread.reshape(p_loc, r_loc, x)
    plane = lax.all_to_all(spread, "slab", split_axis=0, concat_axis=1, tiled=True)
    own = plane.shape[0]
    first_plane = (lax.axis_index("img") * n_slab + lax.axis_index("slab")) * own
    meta = (blk_plane, blk_row, blk_col, frac_plane, frac_row, defocus)
    parts = send_parts(plane, first_plane, meta, box, n_dev)
    recv = lax.all_to_all(parts, ("slab", "img"), split_axis=0, concat_axis=0, tiled=True)
    me = lax.axis_index("slab") * n_img + lax.axis_index("img")
    total = gather_parts(recv, blk_plane, me, own, n_slab, n_img)
    n_blk = blk_plane.shape[1]
    return total.reshape(-1, n_blk, 2, LANES)


def solution(mesh):
    placed = (P("img", "slab", None), P(), P(), P(), P(), P(), P())
    return jax.shard_map(
        on_device,
        mesh=mesh,
        in_specs=placed,
        out_specs=P(("slab", "img"), None, None, None),
        check_vma=False,
    )
```

time: 367 us -> 133 us (0.36); the launches traced: 360 us -> 132 us
  matrix products: 241 us -> 11.5 us
  other arithmetic: 2.33 us -> 15.7 us
  waiting for transfers between devices: 32.7 us -> 22.3 us
  starting transfers between devices: 27.5 us -> 17.5 us
  local copies, waits for them, and re-layouts: 55.6 us -> 64.6 us
    dot_general x6 -> x2, matrix products: 241 us -> 11.5 us  [the longest x1 9.62 us: send_parts(): r_all = jnp.einsum('tpsr,trc->tpsc', w_all, plane, precision=MID)]
    gather x4 -> x0, local copies, waits for them, and re-layouts: 13.2 us -> none  [the longest x1 3.51 us: send_parts(): flat_imag[index_low]]
    transpose x0 -> x1, local copies, waits for them, and re-layouts: none -> 11.4 us  [on_device(): spread = jnp.swapaxes(volume.reshape(p_loc, r_loc, x // SPLIT, SPLIT), 2, 3)]
    unnamed x19 -> x22, local copies, waits for them, and re-layouts: 0.66 us -> 11.1 us
    all_to_all x2 -> x1, waiting for transfers between devices: 19.2 us -> 8.75 us  [on_device(): lax.all_to_all(spread, 'slab', split_axis=0, concat_axis=1, tiled=True)]
    all_to_all x2 -> x1, starting transfers between devices: 17.1 us -> 8.76 us  [on_device(): lax.all_to_all(spread, 'slab', split_axis=0, concat_axis=1, tiled=True)]
    mul x2 -> x5, other arithmetic: 1.13 us -> 6.91 us  [the longest x1 5.55 us: send_parts(): w_re = ((1.0 - frac_y) * lo_re + frac_y * hi_re) * norm]
    another operation x1 -> x2, local copies, waits for them, and re-layouts: 1.14 us -> 6.74 us  [send_parts(): parts = jnp.stack([part_real, part_imag], axis=1)]
  transfers between devices with their start and end apart: 3 -> 2, of which waited for: 2 -> 2; matrix products, arithmetic and copies ran while one was open for 27% -> 32% of each run, Pallas kernels for 0% -> 0%
where the time goes in v3:
time: 133 us; the launch traced here: 132 us
  local copies, waits for them, and re-layouts  64.6 us (49%)
  waiting for transfers between devices  22.3 us (17%)
  starting transfers between devices  17.5 us (13%)
  other arithmetic  15.7 us (12%)
  matrix products  11.5 us (9%)
    all_to_all x1, waiting for transfers between devices, on_device(): lax.all_to_all(parts, ('slab', 'img'), split_axis=0, concat_axis=0, tiled...  13.5 us
    transpose x1, local copies, waits for them, and re-layouts, on_device(): spread = jnp.swapaxes(volume.reshape(p_loc, r_loc, x // SPLIT, SPLIT), 2, 3)  11.4 us
    unnamed x22, local copies, waits for them, and re-layouts  11.1 us
    dot_general x1, matrix products, send_parts(): r_all = jnp.einsum('tpsr,trc->tpsc', w_all, plane, precision=MID)  9.62 us
    all_to_all x1, starting transfers between devices, on_device(): lax.all_to_all(spread, 'slab', split_axis=0, concat_axis=1, tiled=True)  8.76 us
    all_to_all x1, waiting for transfers between devices, on_device(): lax.all_to_all(spread, 'slab', split_axis=0, concat_axis=1, tiled=True)  8.75 us
    all_to_all x1, starting transfers between devices, on_device(): lax.all_to_all(parts, ('slab', 'img'), split_axis=0, concat_axis=0, tiled...  8.75 us
    sub x2, local copies, waits for them, and re-layouts, row_roots(): a_re[:, :, None] * b_re[:, None, :] - a_im[:, :, None] * b_im[:, None, :]  5.84 us
  transfers between devices with their start and end apart: 2, of which 2 were waited for; matrix products, arithmetic and copies ran while one was open for 32% of the time, Pallas kernels for 0%

profile of v3, /device:TPU:1, one launch (start us, length us, event | category | flops | bytes accessed | tf_op | source)
XLA Modules:
  0.0 132.0 jit_solution(7653188547361315521)
XLA Ops:
  0.0 10.5 %copy.150 = f32[32,32,1024]{1,2,0:T(8,128)} copy(f32[32,32,1024]{2,1,0:T(8,128)} %param.7) | data formatting | bytes 8388608 | tf_op args[0]
  10.5 11.4 %copy.151 = f32[32,32,8,128]{3,2,1,0:T(8,128)} copy(f32[32,32,8,128]{1,2,3,0:T(8,128)} %bitcast.72) | data formatting | bytes 8388608 | tf_op jit(solution)/shard_map/transpose | solution.py:129
  21.8 4.9 %reshape.1229 = f32[32,32,1024]{2,1,0:T(8,128)} reshape(f32[32,32,8,128]{3,2,1,0:T(8,128)} %copy.151) | data formatting | bytes 8388608 | tf_op jit(solution)/shard_map/reshape | solution.py:130
  26.8 8.8 %all-to-all-start = ((f32[32,32,1024]{2,1,0:T(8,128)}), f32[32,32,1024]{2,1,0:T(8,128)}, u32[]{:S(2)}, u32[]{:S(2)}) async-start(f32[32,32,1024]{2,1,0:T(8,128)} %reshape.1229), calls=%async_computation | async-start | bytes 8388608 | tf_op jit(solution)/shard_map/all_to_all | solution.py:131
  35.6 0.1 copy.131
  35.7 0.1 eq.84
  35.9 0.2 convert_reduce_fusion
  36.3 0.2 copy.136
  36.4 0.2 add.448
  36.7 0.1 copy.141
  36.8 0.2 reshape.1225
  36.9 3.1 %gather_fusion.2 = s32[512]{0:T(512)S(1)} fusion(s32[4096]{0:T(1024)S(1)} %reshape.1225, s32[1024]{0:T(1024)S(1)} %pad_clamp_fusion.3), kind=kCustom, calls=%fused_computation.2 | custom fusion | bytes 6144 | tf_op jit(solution)/shard_map/gather | solution.py:50
  40.2 1.1 fusion.41
  41.3 1.9 %multiply_subtract_fusion = (f32[512,32,32]{0,2,1:T(8,128)}, f32[512,32,32]{0,2,1:T(8,128)S(1)}) fusion(f32[512,32]{0,1:T(8,128)S(1)} %get-tuple-element.32, f32[512,32]{0,1:T(8,128)S(1)} %get-tuple-element.33, f32[512,32]{0,1:T(8,128)S(1)} %get-tuple-element.31, f32[512,32]{0,1:T(8,128)S(1)} %get-tuple-element.34), kind=kLoop, calls=%fused_computation.19 | loop fusion | flops 3145728 | bytes 4456448 | tf_op jit(solution)/shard_map/sub | solution.py:73
  43.2 2.9 %copy.147 = f32[1,1,512,1024]{3,2,1,0:T(8,128)} copy(f32[1,1,512,1024]{2,3,1,0:T(8,128)} %bitcast.75) | data formatting | bytes 4194304 | tf_op jit(solution)/shard_map/sub | solution.py:73
  46.2 2.7 %multiply_subtract_fusion.1 = (f32[512,32,32]{0,2,1:T(8,128)}, f32[512,32,32]{0,2,1:T(8,128)}) fusion(f32[512,32]{0,1:T(8,128)S(1)} %get-tuple-element.27, f32[512,32]{0,1:T(8,128)S(1)} %get-tuple-element.20, f32[512,32]{0,1:T(8,128)S(1)} %get-tuple-element.28, f32[512,32]{0,1:T(8,128)S(1)} %get-tuple-element.19), kind=kLoop, calls=%fused_computation.20 | loop fusion | flops 3145728 | bytes 4456448 | tf_op jit(solution)/shard_map/sub | solution.py:73
  48.9 2.9 %copy.146 = f32[1,1,512,1024]{3,2,1,0:T(8,128)} copy(f32[1,1,512,1024]{2,3,1,0:T(8,128)} %bitcast.76) | data formatting | bytes 4194304 | tf_op jit(solution)/shard_map/sub | solution.py:73
  51.8 0.1 copy.145
  51.9 0.2 reshape.1226
  52.1 3.1 %gather_fusion.4 = f32[512]{0:T(512)S(1)} fusion(f32[4096]{0:T(1024)S(1)} %reshape.1226, s32[1024]{0:T(1024)S(1)} %pad_clamp_fusion.3), kind=kCustom, calls=%fused_computation.4 | custom fusion | bytes 6144 | tf_op jit(solution)/shard_map/gather | solution.py:53
  55.2 1.8 %copy.149 = f32[1,1,512,1024]{3,2,1,0:T(8,128)} copy(f32[1,1,512,1024]{2,3,1,0:T(8,128)S(1)} %bitcast.73) | data formatting | bytes 4194304 | tf_op jit(solution)/shard_map/add | solution.py:74
  57.0 2.9 %copy.148 = f32[1,1,512,1024]{3,2,1,0:T(8,128)} copy(f32[1,1,512,1024]{2,3,1,0:T(8,128)} %bitcast.74) | data formatting | bytes 4194304 | tf_op jit(solution)/shard_map/add | solution.py:74
  60.0 0.1 copy.139
  60.1 0.2 reshape.1224
  60.3 3.1 %gather_fusion.1 = s32[512]{0:T(512)S(1)} fusion(s32[4096]{0:T(1024)S(1)} %reshape.1224, s32[1024]{0:T(1024)S(1)} %pad_clamp_fusion.3), kind=kCustom, calls=%fused_computation.1 | custom fusion | bytes 6144 | tf_op jit(solution)/shard_map/gather | solution.py:51
  63.4 3.5 %gather_fusion.3 = f32[512]{0:T(512)S(1)} fusion(f32[512]{0:T(512)S(1)} %copy-done, s32[1024]{0:T(1024)S(1)} %pad_clamp_fusion.2), kind=kCustom, calls=%fused_computation.3 | custom fusion | bytes 6144 | tf_op jit(solution)/shard_map/gather | solution.py:54
  67.2 0.1 mul.728
  67.5 0.1 copy.135
  67.6 0.2 reshape.1223
  67.8 3.1 %gather_fusion = f32[512]{0:T(512)S(1)} fusion(f32[4096]{0:T(1024)S(1)} %reshape.1223, s32[1024]{0:T(1024)S(1)} %pad_clamp_fusion.3), kind=kCustom, calls=%fused_computation | custom fusion | bytes 6144 | tf_op jit(solution)/shard_map/gather | solution.py:52
  71.2 0.3 fusion.42
  71.5 0.3 negate_multiply_fusion
  71.9 5.5 %add_multiply_fusion.1 = (f32[1,1,512,1024]{3,2,1,0:T(8,128)}, f32[1,1,512,1024]{3,2,1,0:T(8,128)}) fusion(f32[1,1,512,1024]{3,2,1,0:T(8,128)S(1)} %copy-done.1, f32[1,1,512,1024]{3,2,1,0:T(8,128)} %copy.146, f32[512]{0:T(512)S(1)} %gather_fusion.4, f32[512]{0:T(512)S(1)} %broadcast_subtract_fusion, f32[1,1,512,1024]{3,2,1,0:T(8,128)} %copy.149, ...), kind=kLoop, calls=%fused_computation.18 | loop fusion | flops 4194304 | bytes 12587008 | tf_op jit(solution)/shard_map/mul | solution.py:80
  77.5 8.8 %all-to-all-done = f32[32,32,1024]{2,1,0:T(8,128)} async-done(((f32[32,32,1024]{2,1,0:T(8,128)}), f32[32,32,1024]{2,1,0:T(8,128)}, u32[]{:S(2)}, u32[]{:S(2)}) %all-to-all-start) | async-done | bytes 4194336 | tf_op jit(solution)/shard_map/all_to_all | solution.py:131
  86.2 5.5 %copy.152 = f32[1024,1024]{0,1:T(8,128)} copy(f32[1024,1024]{1,0:T(8,128)} %bitcast.10) | data formatting | bytes 8388608 | tf_op jit(solution)/shard_map/reshape.14
  91.8 9.6 %fusion = f32[2,512,8,128]{3,1,0,2:T(8,128)S(1)} fusion(f32[8,128,1024,1]{2,1,3,0:T(8,128)} %bitcast.77, f32[1,1,512,1024]{3,2,1,0:T(8,128)} %get-tuple-element.18, f32[1,1,512,1024]{3,2,1,0:T(8,128)S(1)} %copy-done.2), kind=kOutput, calls=%fused_computation.8 | convolution fusion | flops 6443499520 | bytes 12582912 | tf_op jit(solution)/shard_map/tpsr,trc->tpsc/dot_general | solution.py:84
  101.4 1.9 %convolution_bitcast_fusion = f32[512,8,256]{2,0,1:T(8,128)S(1)} fusion(f32[2,512,8,128]{3,1,0,2:T(8,128)S(1)} %fusion, f32[1,128,256]{2,1,0:T(8,128)S(1)} %get-tuple-element.14, f32[1,128,256]{2,1,0:T(8,128)S(1)} %get-tuple-element.13), kind=kOutput, calls=%fused_computation.11 | convolution fusion | flops 1610678272 | bytes 8650752 | tf_op jit(solution)/shard_map/tpsjn,pnl->tsjl/dot_general | solution.py:92
  103.3 1.5 %subtract_reduce_fusion = (f32[512,128]{1,0:T(8,128)S(1)}, f32[512,128]{1,0:T(8,128)S(1)}) fusion(f32[512,8,256]{2,0,1:T(8,128)S(1)} %convolution_bitcast_fusion, f32[8,128]{1,0:T(8,128)S(1)} %get-tuple-element.39, f32[512,8]{0,1:T(8,128)S(1)} %get-tuple-element.26, f32[8,128]{1,0:T(8,128)S(1)} %get-tuple-element.40, f32[512,8]{0,1:T(8,128)S(1)} %get-tuple-element.25), kind=kLoop, calls=%fused_computation.13 | loop fusion | flops 7208960 | bytes 4759552 | tf_op jit(solution)/shard_map/reduce_sum | solution.py:100
  104.7 1.1 copy_multiply_fusion.1
  105.9 1.2 copy.155
  107.1 8.8 %all-to-all-start.1 = ((f32[128,4,2,128]{3,2,1,0:T(2,128)}), f32[128,4,2,128]{3,2,1,0:T(2,128)S(1)}, u32[]{:S(2)}, u32[]{:S(2)}) async-start(f32[128,4,2,128]{3,2,1,0:T(2,128)} %copy.155), calls=%async_computation.1 | async-start | bytes 1048576 | tf_op jit(solution)/shard_map/all_to_all | solution.py:136
  115.8 0.2 dynamic-slice_reduce_fusion
  116.1 13.5 %all-to-all-done.1 = f32[128,4,2,128]{3,2,1,0:T(2,128)S(1)} async-done(((f32[128,4,2,128]{3,2,1,0:T(2,128)}), f32[128,4,2,128]{3,2,1,0:T(2,128)S(1)}, u32[]{:S(2)}, u32[]{:S(2)}) %all-to-all-start.1) | async-done | bytes 524320 | tf_op jit(solution)/shard_map/all_to_all | solution.py:136
  129.6 0.1 copy.156
  129.7 0.4 copy.157
  130.2 0.6 gather_fusion.5
  130.8 0.6 gather_fusion.6
  131.4 0.6 add.490
  (50 shorter events, 1.2 us)
Async XLA Ops:
  0.0 63.4 %copy-start = (f32[512]{0:T(512)S(1)}, f32[512]{0:T(512)}, u32[]{:S(2)}) copy-start(f32[512]{0:T(512)} %param.13) | copy-start | bytes 6148
  26.8 8.8 %copy-start.3 = (s32[512,8]{0,1:T(8,128)S(1)}, s32[512,8]{0,1:T(8,128)}, u32[]{:S(2)}) copy-start(s32[512,8]{0,1:T(8,128)} %param.8) | copy-start | bytes 49156
  26.8 9.9 %copy-start.4 = (s32[512,8]{0,1:T(8,128)S(1)}, s32[512,8]{0,1:T(8,128)}, u32[]{:S(2)}) copy-start(s32[512,8]{0,1:T(8,128)} %param.9) | copy-start | bytes 49156
  26.8 59.5 %all-to-all-start = ((f32[32,32,1024]{2,1,0:T(8,128)}), f32[32,32,1024]{2,1,0:T(8,128)}, u32[]{:S(2)}, u32[]{:S(2)}) async-start(f32[32,32,1024]{2,1,0:T(8,128)} %reshape.1229), calls=%async_computation | async-start | bytes 8388608 | tf_op jit(solution)/shard_map/all_to_all | solution.py:131
  48.9 2.9 %copy-start.5 = (f32[512,8]{0,1:T(8,128)S(1)}, f32[512,8]{0,1:T(8,128)}, u32[]{:S(2)}) copy-start(f32[512,8]{0,1:T(8,128)} %param.12) | copy-start | bytes 49156
  57.0 2.9 %copy-start.6 = (s32[512,8]{0,1:T(8,128)S(1)}, s32[512,8]{0,1:T(8,128)}, u32[]{:S(2)}) copy-start(s32[512,8]{0,1:T(8,128)} %param.10) | copy-start | bytes 49156
  60.2 7.3 %copy-start.7 = (f32[512,8]{0,1:T(8,128)S(1)}, f32[512,8]{0,1:T(8,128)}, u32[]{:S(2)}) copy-start(f32[512,8]{0,1:T(8,128)} %param.11) | copy-start | bytes 49156
  66.9 5.0 %copy-start.1 = (f32[1,1,512,1024]{3,2,1,0:T(8,128)S(1)}, f32[1,1,512,1024]{3,2,1,0:T(8,128)}, u32[]{:S(2)}) copy-start(f32[1,1,512,1024]{3,2,1,0:T(8,128)} %copy.147) | copy-start | bytes 6291460
  86.2 5.5 %copy-start.2 = (f32[1,1,512,1024]{3,2,1,0:T(8,128)S(1)}, f32[1,1,512,1024]{3,2,1,0:T(8,128)}, u32[]{:S(2)}) copy-start(f32[1,1,512,1024]{3,2,1,0:T(8,128)} %get-tuple-element.17) | copy-start | bytes 6291460
  107.1 22.5 %all-to-all-start.1 = ((f32[128,4,2,128]{3,2,1,0:T(2,128)}), f32[128,4,2,128]{3,2,1,0:T(2,128)S(1)}, u32[]{:S(2)}, u32[]{:S(2)}) async-start(f32[128,4,2,128]{3,2,1,0:T(2,128)} %copy.155), calls=%async_computation.1 | async-start | bytes 1048576 | tf_op jit(solution)/shard_map/all_to_all | solution.py:136

commit v4 on v3

--- a/solution.py
+++ b/solution.py
@@ -81,24 +81,31 @@
     w_im = ((1.0 - frac_y) * lo_im + frac_y * hi_im) * norm
     n_s = w_re.shape[0] // own
     w_all = jnp.stack([w_re.reshape(own, n_s, n_rows), w_im.reshape(own, n_s, n_rows)], axis=1)
-    r_all = jnp.einsum("tpsr,trc->tpsc", w_all, plane, precision=MID)
+    r_t = jnp.einsum("trc,tpsr->tpcs", plane, w_all, precision=MID)
     m = x // SPLIT
-    r4 = r_all.reshape(own, 2, n_s, SPLIT, m)
+    r5 = r_t.reshape(own, 2, m, SPLIT, n_s)
     idx = lax.iota(jnp.int32, m)
     c_re, c_im = roots(idx[:, None], idx[None, :], m, 1.0 / math.sqrt(x))
     w_col = jnp.stack(
-        [jnp.concatenate([c_re, c_im], axis=1), jnp.concatenate([-c_im, c_re], axis=1)], axis=0
+        [jnp.stack([c_re, -c_im], axis=1), jnp.stack([c_im, c_re], axis=1)], axis=0
     )
-    y = jnp.einsum("tpsjn,pnl->tsjl", r4, w_col, precision=MID).reshape(own * n_s, SPLIT, 2 * m)
-    y_re = y[:, :, :m]
-    y_im = y[:, :, m:]
+    y = jnp.einsum("qkpn,tpnjs->tqkjs", w_col, r5, precision=MID)
+    y_re = y[:, 0]
+    y_im = y[:, 1]
     n1 = lax.iota(jnp.int32, SPLIT)
-    e_re, e_im = roots(cols[:, None], n1[None, :], SPLIT, 1.0)
-    t_re, t_im = roots(n1[:, None], lane[None, :], box, 1.0)
-    g_re = e_re[:, :, None] * t_re[None] - e_im[:, :, None] * t_im[None]
-    g_im = e_re[:, :, None] * t_im[None] + e_im[:, :, None] * t_re[None]
-    o_re = jnp.sum(g_re * y_re - g_im * y_im, axis=1)
-    o_im = jnp.sum(g_re * y_im + g_im * y_re, axis=1)
+    cols_t = cols.reshape(own, n_s)
+    e_re, e_im = roots(n1[None, :, None], cols_t[:, None, :], SPLIT, 1.0)
+    t_re, t_im = roots(lane[:, None], n1[None, :], box, 1.0)
+    e_re = e_re[:, None]
+    e_im = e_im[:, None]
+    t_re = t_re[None, :, :, None]
+    t_im = t_im[None, :, :, None]
+    g_re = e_re * t_re - e_im * t_im
+    g_im = e_re * t_im + e_im * t_re
+    o_re = jnp.sum(g_re * y_re - g_im * y_im, axis=2)
+    o_im = jnp.sum(g_re * y_im + g_im * y_re, axis=2)
+    o_re = jnp.swapaxes(o_re, 1, 2).reshape(own * n_s, LANES)
+    o_im = jnp.swapaxes(o_im, 1, 2).reshape(own * n_s, LANES)
     parts = jnp.stack([scale * o_re, scale * o_im], axis=1)
     parts = parts.reshape(own, n_dev, 4, 2, LANES)
     return jnp.swapaxes(parts, 0, 1).reshape(n_dev, own * 4, 2, LANES)
@@ -125,10 +132,7 @@
     n_slab = lax.axis_size("slab")
     n_img = lax.axis_size("img")
     n_dev = n_slab * n_img
-    p_loc, r_loc, x = volume.shape
-    spread = jnp.swapaxes(volume.reshape(p_loc, r_loc, x // SPLIT, SPLIT), 2, 3)
-    spread = spread.reshape(p_loc, r_loc, x)
-    plane = lax.all_to_all(spread, "slab", split_axis=0, concat_axis=1, tiled=True)
+    plane = lax.all_to_all(volume, "slab", split_axis=0, concat_axis=1, tiled=True)
     own = plane.shape[0]
     first_plane = (lax.axis_index("img") * n_slab + lax.axis_index("slab")) * own
     meta = (blk_plane, blk_row, blk_col, frac_plane, frac_row, defocus)

time: 133 us -> 111 us (0.83)
  local copies, waits for them, and re-layouts: 64.6 us -> 36.6 us
  matrix products: 11.5 us -> 17.5 us
  waiting for transfers between devices: 22.3 us -> 24 us
    unnamed x22 -> x19, local copies, waits for them, and re-layouts: 11.1 us -> 0.65 us
    dot_general x2, matrix products: 11.5 us -> 17.5 us  [the longest x1 11.1 us: send_parts(): r_t = jnp.einsum('trc,tpsr->tpcs', plane, w_all, precision=MID)]
    transpose x1, local copies, waits for them, and re-layouts: 11.4 us -> 5.35 us  [send_parts(): r_t = jnp.einsum('trc,tpsr->tpcs', plane, w_all, precision=MID)]
    another operation x1 -> x0, local copies, waits for them, and re-layouts: 5.53 us -> none
    reshape x1 -> x0, local copies, waits for them, and re-layouts: 4.92 us -> none  [on_device(): spread = spread.reshape(p_loc, r_loc, x)]
    all_to_all x1, waiting for transfers between devices: 8.75 us -> 10.5 us  [on_device(): lax.all_to_all(volume, 'slab', split_axis=0, concat_axis=1, tiled=True)]
  transfers between devices with their start and end apart: 2 -> 2, of which waited for: 2 -> 2; matrix products, arithmetic and copies ran while one was open for 32% -> 36% of each run, Pallas kernels for 0% -> 0%
where the time goes in v4:
time: 111 us
  local copies, waits for them, and re-layouts  36.6 us (33%)
  waiting for transfers between devices  24 us (22%)
  starting transfers between devices  17.6 us (16%)
  matrix products  17.5 us (16%)
  other arithmetic  15 us (14%)
    all_to_all x1, waiting for transfers between devices, on_device(): lax.all_to_all(parts, ('slab', 'img'), split_axis=0, concat_axis=0, tiled...  13.5 us
    dot_general x1, matrix products, send_parts(): r_t = jnp.einsum('trc,tpsr->tpcs', plane, w_all, precision=MID)  11.1 us
    all_to_all x1, waiting for transfers between devices, on_device(): lax.all_to_all(volume, 'slab', split_axis=0, concat_axis=1, tiled=True)  10.5 us
    all_to_all x1, starting transfers between devices, on_device(): lax.all_to_all(volume, 'slab', split_axis=0, concat_axis=1, tiled=True)  8.78 us
    all_to_all x1, starting transfers between devices, on_device(): lax.all_to_all(parts, ('slab', 'img'), split_axis=0, concat_axis=0, tiled...  8.78 us
    dot_general x1, matrix products, send_parts(): y = jnp.einsum('qkpn,tpnjs->tqkjs', w_col, r5, precision=MID)  6.43 us
    sub x2, local copies, waits for them, and re-layouts, row_roots(): a_re[:, :, None] * b_re[:, None, :] - a_im[:, :, None] * b_im[:, None, :]  5.84 us
    mul x1, other arithmetic, send_parts(): w_re = ((1.0 - frac_y) * lo_re + frac_y * hi_re) * norm  5.6 us
  transfers between devices with their start and end apart: 2, of which 2 were waited for; matrix products, arithmetic and copies ran while one was open for 36% of the time, Pallas kernels for 0%

profile of v4, /device:TPU:1, one launch (start us, length us, event | category | flops | bytes accessed | tf_op | source)
XLA Modules:
  0.0 111.1 jit_solution(16287074114068073235)
XLA Ops:
  0.0 8.8 %all-to-all-start = ((f32[32,32,1024]{2,1,0:T(8,128)}), f32[32,32,1024]{2,1,0:T(8,128)}, u32[]{:S(2)}, u32[]{:S(2)}) async-start(f32[32,32,1024]{2,1,0:T(8,128)} %param.7), calls=%async_computation | async-start | bytes 8388608 | tf_op jit(solution)/shard_map/all_to_all | solution.py:135
  8.9 0.1 copy.138
  9.0 0.1 eq.84
  9.2 0.2 convert_reduce_fusion
  9.5 0.2 copy.143
  9.7 0.2 add.486
  9.9 0.1 copy.148
  10.1 0.2 reshape.1424
  10.2 3.1 %gather_fusion.2 = s32[512]{0:T(512)S(1)} fusion(s32[4096]{0:T(1024)S(1)} %reshape.1424, s32[1024]{0:T(1024)S(1)} %pad_clamp_fusion.3), kind=kCustom, calls=%fused_computation.2 | custom fusion | bytes 6144 | tf_op jit(solution)/shard_map/gather | solution.py:50
  13.4 0.1 gather.29
  13.5 1.1 fusion.47
  14.6 1.9 %multiply_subtract_fusion.1 = (f32[512,32,32]{0,2,1:T(8,128)}, f32[512,32,32]{0,2,1:T(8,128)S(1)}) fusion(f32[512,32]{0,1:T(8,128)S(1)} %get-tuple-element.27, f32[512,32]{0,1:T(8,128)S(1)} %get-tuple-element.20, f32[512,32]{0,1:T(8,128)S(1)} %get-tuple-element.28, f32[512,32]{0,1:T(8,128)S(1)} %get-tuple-element.19), kind=kLoop, calls=%fused_computation.25 | loop fusion | flops 3145728 | bytes 4456448 | tf_op jit(solution)/shard_map/sub | solution.py:73
  16.5 2.9 %copy.153 = f32[1,1,512,1024]{3,2,1,0:T(8,128)} copy(f32[1,1,512,1024]{2,3,1,0:T(8,128)} %bitcast.97) | data formatting | bytes 4194304 | tf_op jit(solution)/shard_map/sub | solution.py:73
  19.4 1.8 %copy.155 = f32[1,1,512,1024]{3,2,1,0:T(8,128)} copy(f32[1,1,512,1024]{2,3,1,0:T(8,128)S(1)} %bitcast.95) | data formatting | bytes 4194304 | tf_op jit(solution)/shard_map/add | solution.py:74
  21.3 2.0 %multiply_subtract_fusion = (f32[512,32,32]{0,2,1:T(8,128)}, f32[512,32,32]{0,2,1:T(8,128)S(1)}) fusion(f32[512,32]{0,1:T(8,128)S(1)} %get-tuple-element.32, f32[512,32]{0,1:T(8,128)S(1)} %get-tuple-element.33, f32[512,32]{0,1:T(8,128)S(1)} %get-tuple-element.31, f32[512,32]{0,1:T(8,128)S(1)} %get-tuple-element.34), kind=kLoop, calls=%fused_computation.24 | loop fusion | flops 3145728 | bytes 4456448 | tf_op jit(solution)/shard_map/sub | solution.py:73
  23.3 2.9 %copy.154 = f32[1,1,512,1024]{3,2,1,0:T(8,128)} copy(f32[1,1,512,1024]{2,3,1,0:T(8,128)} %bitcast.98) | data formatting | bytes 4194304 | tf_op jit(solution)/shard_map/sub | solution.py:73
  26.2 1.8 %copy.156 = f32[1,1,512,1024]{3,2,1,0:T(8,128)} copy(f32[1,1,512,1024]{2,3,1,0:T(8,128)S(1)} %bitcast.96) | data formatting | bytes 4194304 | tf_op jit(solution)/shard_map/add | solution.py:74
  28.0 0.1 copy.152
  28.1 0.2 reshape.1425
  28.3 3.1 %gather_fusion.4 = f32[512]{0:T(512)S(1)} fusion(f32[4096]{0:T(1024)S(1)} %reshape.1425, s32[1024]{0:T(1024)S(1)} %pad_clamp_fusion.3), kind=kCustom, calls=%fused_computation.4 | custom fusion | bytes 6144 | tf_op jit(solution)/shard_map/gather | solution.py:53
  31.5 0.1 copy.146
  31.6 0.2 reshape.1423
  31.8 3.1 %gather_fusion.1 = s32[512]{0:T(512)S(1)} fusion(s32[4096]{0:T(1024)S(1)} %reshape.1423, s32[1024]{0:T(1024)S(1)} %pad_clamp_fusion.3), kind=kCustom, calls=%fused_computation.1 | custom fusion | bytes 6144 | tf_op jit(solution)/shard_map/gather | solution.py:51
  34.9 0.1 copy.142
  35.0 0.2 reshape.1422
  35.2 3.1 %gather_fusion = f32[512]{0:T(512)S(1)} fusion(f32[4096]{0:T(1024)S(1)} %reshape.1422, s32[1024]{0:T(1024)S(1)} %pad_clamp_fusion.3), kind=kCustom, calls=%fused_computation | custom fusion | bytes 6144 | tf_op jit(solution)/shard_map/gather | solution.py:52
  38.4 0.1 gather.26
  38.7 0.1 mul.862
  38.9 3.5 %gather_fusion.3 = f32[512]{0:T(512)S(1)} fusion(f32[512]{0:T(512)S(1)} %copy-done, s32[1024]{0:T(1024)S(1)} %pad_clamp_fusion.2), kind=kCustom, calls=%fused_computation.3 | custom fusion | bytes 6144 | tf_op jit(solution)/shard_map/gather | solution.py:54
  42.4 0.1 mul.867
  42.7 0.3 fusion.48
  43.0 0.3 negate_multiply_fusion
  43.4 5.6 %add_multiply_fusion.1 = (f32[1,1,512,1024]{3,2,1,0:T(8,128)}, f32[1,1,512,1024]{3,2,1,0:T(8,128)}) fusion(f32[1,1,512,1024]{3,2,1,0:T(8,128)} %copy.154, f32[1,1,512,1024]{3,2,1,0:T(8,128)S(1)} %copy-done.1, f32[512]{0:T(512)S(1)} %gather_fusion.4, f32[512]{0:T(512)S(1)} %broadcast_subtract_fusion, f32[1,1,512,1024]{3,2,1,0:T(8,128)} %copy.156, ...), kind=kLoop, calls=%fused_computation.23 | loop fusion | flops 4194304 | bytes 12587008 | tf_op jit(solution)/shard_map/mul | solution.py:80
  49.0 10.5 %all-to-all-done = f32[32,32,1024]{2,1,0:T(8,128)} async-done(((f32[32,32,1024]{2,1,0:T(8,128)}), f32[32,32,1024]{2,1,0:T(8,128)}, u32[]{:S(2)}, u32[]{:S(2)}) %all-to-all-start) | async-done | bytes 4194336 | tf_op jit(solution)/shard_map/all_to_all | solution.py:135
  59.5 11.1 %fusion.8 = f32[1,2,1024,512]{2,3,1,0:T(8,128)} fusion(f32[1024,1024,1]{1,0,2:T(8,128)} %bitcast.8, f32[1,1,512,1024]{3,2,1,0:T(8,128)} %get-tuple-element.18, f32[1,1,512,1024]{3,2,1,0:T(8,128)} %get-tuple-element.17), kind=kOutput, calls=%fused_computation.14 | convolution fusion | flops 6443499520 | bytes 12582912 | tf_op jit(solution)/shard_map/trc,tpsr->tpcs/dot_general | solution.py:84
  70.6 5.4 %copy.157 = f32[1,2,1024,512]{3,2,1,0:T(8,128)} copy(f32[1,2,1024,512]{2,3,1,0:T(8,128)} %fusion.8) | data formatting | bytes 8388608 | tf_op jit(solution)/shard_map/trc,tpsr->tpcs/transpose | solution.py:84
  75.9 6.4 %fusion.5 = f32[1,2,128,8,512]{2,4,1,3,0:T(8,128)S(1)} fusion(f32[2,128,8,512,1]{3,2,1,0,4:T(8,128)} %bitcast.94, f32[1,128,2,128]{3,1,2,0:T(8,128)S(1)} %get-tuple-element.14, f32[1,128,2,128]{3,1,2,0:T(8,128)S(1)} %get-tuple-element.13), kind=kOutput, calls=%fused_computation.13 | convolution fusion | flops 1610678272 | bytes 8650752 | tf_op jit(solution)/shard_map/qkpn,tpnjs->tqkjs/dot_general | solution.py:92
  82.4 1.4 %subtract_reduce_fusion = (f32[128,512]{0,1:T(8,128)S(1)}, f32[128,512]{0,1:T(8,128)S(1)}) fusion(f32[1,2,128,8,512]{2,4,1,3,0:T(8,128)S(1)} %fusion.5, f32[128,8]{0,1:T(8,128)S(1)} %get-tuple-element.39, f32[8,512]{1,0:T(8,128)S(1)} %get-tuple-element.26, f32[128,8]{0,1:T(8,128)S(1)} %get-tuple-element.40, f32[8,512]{1,0:T(8,128)S(1)} %get-tuple-element.25), kind=kLoop, calls=%fused_computation.18 | loop fusion | flops 7208960 | bytes 4759552 | tf_op jit(solution)/shard_map/reduce_sum | solution.py:105
  83.8 1.1 copy_multiply_fusion.1
  85.0 1.2 %copy.162 = f32[128,4,2,128]{3,2,1,0:T(2,128)} copy(f32[128,4,2,128]{3,0,2,1:T(8,128)S(1)} %pad_maximum_fusion) | data formatting | bytes 1048576 | tf_op jit(solution)/shard_map/stack | solution.py:109
  86.2 8.8 %all-to-all-start.1 = ((f32[128,4,2,128]{3,2,1,0:T(2,128)}), f32[128,4,2,128]{3,2,1,0:T(2,128)S(1)}, u32[]{:S(2)}, u32[]{:S(2)}) async-start(f32[128,4,2,128]{3,2,1,0:T(2,128)} %copy.162), calls=%async_computation.1 | async-start | bytes 1048576 | tf_op jit(solution)/shard_map/all_to_all | solution.py:140
  94.9 0.2 dynamic-slice_reduce_fusion
  95.2 13.5 %all-to-all-done.1 = f32[128,4,2,128]{3,2,1,0:T(2,128)S(1)} async-done(((f32[128,4,2,128]{3,2,1,0:T(2,128)}), f32[128,4,2,128]{3,2,1,0:T(2,128)S(1)}, u32[]{:S(2)}, u32[]{:S(2)}) %all-to-all-start.1) | async-done | bytes 524320 | tf_op jit(solution)/shard_map/all_to_all | solution.py:140
  108.7 0.1 copy.163
  108.8 0.4 copy.164
  109.3 0.6 gather_fusion.6
  109.9 0.6 gather_fusion.5
  110.5 0.6 add.528
  (45 shorter events, 0.9 us)
Async XLA Ops:
  0.0 38.9 %copy-start = (f32[512]{0:T(512)S(1)}, f32[512]{0:T(512)}, u32[]{:S(2)}) copy-start(f32[512]{0:T(512)} %param.13) | copy-start | bytes 6148
  0.0 8.8 %copy-start.2 = (s32[512,8]{0,1:T(8,128)S(1)}, s32[512,8]{0,1:T(8,128)}, u32[]{:S(2)}) copy-start(s32[512,8]{0,1:T(8,128)} %param.8) | copy-start | bytes 49156
  0.0 9.9 %copy-start.3 = (s32[512,8]{0,1:T(8,128)S(1)}, s32[512,8]{0,1:T(8,128)}, u32[]{:S(2)}) copy-start(s32[512,8]{0,1:T(8,128)} %param.9) | copy-start | bytes 49156
  0.0 59.5 %all-to-all-start = ((f32[32,32,1024]{2,1,0:T(8,128)}), f32[32,32,1024]{2,1,0:T(8,128)}, u32[]{:S(2)}, u32[]{:S(2)}) async-start(f32[32,32,1024]{2,1,0:T(8,128)} %param.7), calls=%async_computation | async-start | bytes 8388608 | tf_op jit(solution)/shard_map/all_to_all | solution.py:135
  26.2 1.8 %copy-start.4 = (f32[512,8]{0,1:T(8,128)S(1)}, f32[512,8]{0,1:T(8,128)}, u32[]{:S(2)}) copy-start(f32[512,8]{0,1:T(8,128)} %param.12) | copy-start | bytes 49156
  28.0 3.4 %copy-start.5 = (s32[512,8]{0,1:T(8,128)S(1)}, s32[512,8]{0,1:T(8,128)}, u32[]{:S(2)}) copy-start(s32[512,8]{0,1:T(8,128)} %param.10) | copy-start | bytes 49156
  28.3 6.6 %copy-start.6 = (f32[512,8]{0,1:T(8,128)S(1)}, f32[512,8]{0,1:T(8,128)}, u32[]{:S(2)}) copy-start(f32[512,8]{0,1:T(8,128)} %param.11) | copy-start | bytes 49156
  38.3 5.1 %copy-start.1 = (f32[1,1,512,1024]{3,2,1,0:T(8,128)S(1)}, f32[1,1,512,1024]{3,2,1,0:T(8,128)}, u32[]{:S(2)}) copy-start(f32[1,1,512,1024]{3,2,1,0:T(8,128)} %copy.153) | copy-start | bytes 6291460
  86.2 22.6 %all-to-all-start.1 = ((f32[128,4,2,128]{3,2,1,0:T(2,128)}), f32[128,4,2,128]{3,2,1,0:T(2,128)S(1)}, u32[]{:S(2)}, u32[]{:S(2)}) async-start(f32[128,4,2,128]{3,2,1,0:T(2,128)} %copy.162), calls=%async_computation.1 | async-start | bytes 1048576 | tf_op jit(solution)/shard_map/all_to_all | solution.py:140

commit v5 on v4

--- a/solution.py
+++ b/solution.py
@@ -44,14 +44,15 @@
         rank[None, :, None, None, :] == u[..., None]
     )
     valid = jnp.any(match, axis=-1)
-    kidx = jnp.sum(jnp.where(match, lax.iota(jnp.int32, k_dev), 0), axis=-1)
-    g = lax.iota(jnp.int32, n_dev)[None, :, None, None] * k_dev + kidx
-    g = g.reshape(-1)
-    rows = blk_row.reshape(-1)[g]
-    cols = blk_col.reshape(-1)[g]
-    frac_z = frac_plane.reshape(-1)[g]
-    frac_y = frac_row.reshape(-1)[g][:, None]
-    focus = defocus[g // n_blk]
+    def pick(values):
+        table = values.reshape(n_dev, k_dev)[None, :, None, None, :]
+        return jnp.sum(jnp.where(match, table, jnp.zeros_like(table)), axis=-1).reshape(-1)
+
+    rows = pick(blk_row)
+    cols = pick(blk_col)
+    frac_z = pick(frac_plane)
+    frac_y = pick(frac_row)[:, None]
+    focus = pick(jnp.broadcast_to(defocus[:, None], blk_plane.shape))
     side_f = jnp.broadcast_to(side, (own, n_dev, 2, 2)).reshape(-1)
     valid = valid.reshape(-1)
     lane = lax.iota(jnp.int32, LANES)
@@ -137,7 +138,9 @@
     first_plane = (lax.axis_index("img") * n_slab + lax.axis_index("slab")) * own
     meta = (blk_plane, blk_row, blk_col, frac_plane, frac_row, defocus)
     parts = send_parts(plane, first_plane, meta, box, n_dev)
-    recv = lax.all_to_all(parts, ("slab", "img"), split_axis=0, concat_axis=0, tiled=True)
+    parts = parts.reshape(n_slab, n_img, *parts.shape[1:])
+    parts = lax.all_to_all(parts, "img", split_axis=1, concat_axis=1, tiled=True)
+    recv = lax.all_to_all(parts, "slab", split_axis=0, concat_axis=0, tiled=True)
     me = lax.axis_index("slab") * n_img + lax.axis_index("img")
     total = gather_parts(recv, blk_plane, me, own, n_slab, n_img)
     n_blk = blk_plane.shape[1]

time: 111 us -> 123 us (1.11)
  local copies, waits for them, and re-layouts: 36.6 us -> 22.7 us
  blocking collectives: 0 us -> 11.8 us
  waiting for transfers between devices: 24 us -> 35.8 us
  other arithmetic: 15 us -> 16.4 us
    gather x9 -> x0, local copies, waits for them, and re-layouts: 16.4 us -> none  [the longest x1 3.51 us: send_parts(): focus = defocus[g // n_blk]]
    all_to_all x1, waiting for transfers between devices: 10.5 us -> 24.6 us  [on_device(): lax.all_to_all(volume, 'slab', split_axis=0, concat_axis=1, tiled=True)]
    all_to_all x0 -> x1, blocking collectives: none -> 11.8 us  [on_device(): lax.all_to_all(parts, 'img', split_axis=1, concat_axis=1, tiled=True)]
    all_to_all x1, waiting for transfers between devices: 13.5 us -> 11.2 us  [on_device(): lax.all_to_all(parts, 'slab', split_axis=0, concat_axis=0, tiled=True)]
    mul x1, other arithmetic: 1.07 us -> 2.55 us  [send_parts(): parts = jnp.stack([scale * o_re, scale * o_im], axis=1)]
  transfers between devices with their start and end apart: 2 -> 2, of which waited for: 2 -> 2; matrix products, arithmetic and copies ran while one was open for 36% -> 21% of each run, Pallas kernels for 0% -> 0%
where the time goes in v5:
time: 123 us; the launch traced here: 122 us
  waiting for transfers between devices  35.8 us (29%)
  local copies, waits for them, and re-layouts  22.7 us (18%)
  starting transfers between devices  17.7 us (14%)
  matrix products  17.5 us (14%)
  other arithmetic  16.4 us (13%)
  blocking collectives  11.8 us (10%)
    all_to_all x1, waiting for transfers between devices, on_device(): lax.all_to_all(volume, 'slab', split_axis=0, concat_axis=1, tiled=True)  24.6 us
    all_to_all x1, blocking collectives, on_device(): lax.all_to_all(parts, 'img', split_axis=1, concat_axis=1, tiled=True)  11.8 us
    all_to_all x1, waiting for transfers between devices, on_device(): lax.all_to_all(parts, 'slab', split_axis=0, concat_axis=0, tiled=True)  11.2 us
    dot_general x1, matrix products, send_parts(): r_t = jnp.einsum('trc,tpsr->tpcs', plane, w_all, precision=MID)  11.1 us
    all_to_all x1, starting transfers between devices, on_device(): lax.all_to_all(parts, 'slab', split_axis=0, concat_axis=0, tiled=True)  8.97 us
    all_to_all x1, starting transfers between devices, on_device(): lax.all_to_all(volume, 'slab', split_axis=0, concat_axis=1, tiled=True)  8.78 us
    dot_general x1, matrix products, send_parts(): y = jnp.einsum('qkpn,tpnjs->tqkjs', w_col, r5, precision=MID)  6.38 us
    sub x2, local copies, waits for them, and re-layouts, row_roots(): a_re[:, :, None] * b_re[:, None, :] - a_im[:, :, None] * b_im[:, None, :]  5.86 us
  transfers between devices with their start and end apart: 2, of which 2 were waited for; matrix products, arithmetic and copies ran while one was open for 21% of the time, Pallas kernels for 0%

profile of v5, /device:TPU:1, one launch (start us, length us, event | category | flops | bytes accessed | tf_op | source)
XLA Modules:
  0.0 122.4 jit_solution(2395469357548548312)
XLA Ops:
  0.0 8.8 %all-to-all-start = ((f32[32,32,1024]{2,1,0:T(8,128)}), f32[32,32,1024]{2,1,0:T(8,128)}, u32[]{:S(2)}, u32[]{:S(2)}) async-start(f32[32,32,1024]{2,1,0:T(8,128)} %param.7), calls=%async_computation | async-start | bytes 8388608 | tf_op jit(solution)/shard_map/all_to_all | solution.py:136
  8.8 0.1 copy.186
  9.0 0.1 eq.87
  9.2 0.1 copy.193
  9.5 0.1 copy.196
  9.8 0.2 convert_reduce_fusion
  10.2 0.2 copy.207
  10.5 0.2 mul.880
  10.7 1.1 fusion.54
  11.7 1.9 %multiply_subtract_fusion.1 = (f32[512,32,32]{0,2,1:T(8,128)}, f32[512,32,32]{0,2,1:T(8,128)S(1)}) fusion(f32[512,32]{0,1:T(8,128)S(1)} %get-tuple-element.30, f32[512,32]{0,1:T(8,128)S(1)} %get-tuple-element.25, f32[512,32]{0,1:T(8,128)S(1)} %get-tuple-element.31, f32[512,32]{0,1:T(8,128)S(1)} %get-tuple-element.24), kind=kLoop, calls=%fused_computation.20 | loop fusion | flops 3145728 | bytes 4456448 | tf_op jit(solution)/shard_map/sub | solution.py:74
  13.7 2.9 %copy.208 = f32[1,1,512,1024]{3,2,1,0:T(8,128)} copy(f32[1,1,512,1024]{2,3,1,0:T(8,128)} %bitcast.105) | data formatting | bytes 4194304 | tf_op jit(solution)/shard_map/sub | solution.py:74
  16.6 1.9 %copy.210 = f32[1,1,512,1024]{3,2,1,0:T(8,128)} copy(f32[1,1,512,1024]{2,3,1,0:T(8,128)S(1)} %bitcast.103) | data formatting | bytes 4194304 | tf_op jit(solution)/shard_map/add | solution.py:75
  18.4 1.9 %multiply_subtract_fusion = (f32[512,32,32]{0,2,1:T(8,128)}, f32[512,32,32]{0,2,1:T(8,128)S(1)}) fusion(f32[512,32]{0,1:T(8,128)S(1)} %get-tuple-element.35, f32[512,32]{0,1:T(8,128)S(1)} %get-tuple-element.36, f32[512,32]{0,1:T(8,128)S(1)} %get-tuple-element.34, f32[512,32]{0,1:T(8,128)S(1)} %get-tuple-element.37), kind=kLoop, calls=%fused_computation.19 | loop fusion | flops 3145728 | bytes 4456448 | tf_op jit(solution)/shard_map/sub | solution.py:74
  20.4 3.0 %copy.209 = f32[1,1,512,1024]{3,2,1,0:T(8,128)} copy(f32[1,1,512,1024]{2,3,1,0:T(8,128)} %bitcast.106) | data formatting | bytes 4194304 | tf_op jit(solution)/shard_map/sub | solution.py:74
  23.3 1.8 %copy.211 = f32[1,1,512,1024]{3,2,1,0:T(8,128)} copy(f32[1,1,512,1024]{2,3,1,0:T(8,128)S(1)} %bitcast.104) | data formatting | bytes 4194304 | tf_op jit(solution)/shard_map/add | solution.py:75
  25.1 0.1 copy.190
  25.5 0.1 copy.204
  25.6 0.1 broadcast_in_dim.138
  25.8 0.1 broadcast_in_dim.134
  26.1 0.2 copy.206
  26.2 0.2 broadcast_in_dim_reshape.2
  26.4 0.2 copy.203
  26.6 0.2 mul.863
  26.9 0.1 reshape.1433
  27.0 0.1 eq.99
  27.2 0.3 copy.192
  27.6 0.3 copy.202
  28.3 0.3 copy.195
  28.6 0.3 fusion.55
  28.9 0.3 negate_multiply_fusion
  29.3 5.5 %add_multiply_fusion.1 = (f32[1,1,512,1024]{3,2,1,0:T(8,128)}, f32[1,1,512,1024]{3,2,1,0:T(8,128)}) fusion(f32[1,1,512,1024]{3,2,1,0:T(8,128)} %copy.209, f32[1,1,512,1024]{3,2,1,0:T(8,128)S(1)} %copy-done, f32[512]{0:T(512)S(1)} %broadcast_in_dim_reshape.2, f32[512]{0:T(512)S(1)} %broadcast_subtract_fusion, f32[1,1,512,1024]{3,2,1,0:T(8,128)} %copy.211, ...), kind=kLoop, calls=%fused_computation.18 | loop fusion | flops 4194304 | bytes 12587008 | tf_op jit(solution)/shard_map/mul | solution.py:81
  34.8 24.6 %all-to-all-done = f32[32,32,1024]{2,1,0:T(8,128)} async-done(((f32[32,32,1024]{2,1,0:T(8,128)}), f32[32,32,1024]{2,1,0:T(8,128)}, u32[]{:S(2)}, u32[]{:S(2)}) %all-to-all-start) | async-done | bytes 4194336 | tf_op jit(solution)/shard_map/all_to_all | solution.py:136
  59.5 11.1 %fusion.8 = f32[1,2,1024,512]{2,3,1,0:T(8,128)} fusion(f32[1024,1024,1]{1,0,2:T(8,128)} %bitcast.7, f32[1,1,512,1024]{3,2,1,0:T(8,128)} %get-tuple-element.23, f32[1,1,512,1024]{3,2,1,0:T(8,128)} %get-tuple-element.22), kind=kOutput, calls=%fused_computation.9 | convolution fusion | flops 6443499520 | bytes 12582912 | tf_op jit(solution)/shard_map/trc,tpsr->tpcs/dot_general | solution.py:85
  70.6 5.4 %copy.212 = f32[1,2,1024,512]{3,2,1,0:T(8,128)} copy(f32[1,2,1024,512]{2,3,1,0:T(8,128)} %fusion.8) | data formatting | bytes 8388608 | tf_op jit(solution)/shard_map/trc,tpsr->tpcs/transpose | solution.py:85
  76.0 6.4 %fusion.5 = f32[1,2,128,8,512]{2,4,1,3,0:T(8,128)S(1)} fusion(f32[2,128,8,512,1]{3,2,1,0,4:T(8,128)} %bitcast.102, f32[1,128,2,128]{3,1,2,0:T(8,128)S(1)} %get-tuple-element.21, f32[1,128,2,128]{3,1,2,0:T(8,128)S(1)} %get-tuple-element.20), kind=kOutput, calls=%fused_computation.8 | convolution fusion | flops 1610678272 | bytes 8650752 | tf_op jit(solution)/shard_map/qkpn,tpnjs->tqkjs/dot_general | solution.py:93
  82.4 1.4 %subtract_reduce_fusion = (f32[128,512]{0,1:T(8,128)S(1)}, f32[128,512]{0,1:T(8,128)S(1)}) fusion(f32[1,2,128,8,512]{2,4,1,3,0:T(8,128)S(1)} %fusion.5, f32[128,8]{0,1:T(8,128)S(1)} %get-tuple-element.42, f32[8,512]{1,0:T(8,128)S(1)} %get-tuple-element.29, f32[128,8]{0,1:T(8,128)S(1)} %get-tuple-element.43, f32[8,512]{1,0:T(8,128)S(1)} %get-tuple-element.28), kind=kLoop, calls=%fused_computation.13 | loop fusion | flops 7208960 | bytes 4759552 | tf_op jit(solution)/shard_map/reduce_sum | solution.py:106
  83.8 2.5 %fusion.20 = (f32[32,4,4,1,128]{4,2,1,0,3:T(4,128)S(1)}, f32[32,4,4,1,128]{4,2,1,0,3:T(4,128)S(1)}) fusion(f32[32,4,4,1,128]{4,2,1,0,3:T(4,128)S(1)} %bitcast.108, f32[32,4,4]{2,1,0:T(4,128)S(1)} %copy.202, f32[32,4,4]{2,1,0:T(4,128)S(1)} %copy.200, s32[32,4,4]{2,1,0:T(4,128)S(1)} %copy.195, f32[32,4,4]{2,1,0:T(4,128)S(1)} %copy.192, ...), kind=kLoop, calls=%fused_computation.51 | loop fusion | flops 786432 | bytes 1056768 | tf_op jit(solution)/shard_map/mul | solution.py:110
  86.5 0.4 copy.215
  86.9 11.8 %all_to_all.19 = f32[32,4,4,2,128]{4,3,2,0,1:T(2,128)S(1)} all-to-all(f32[32,4,4,2,128]{4,3,2,0,1:T(2,128)S(1)} %copy.215), channel_id=1, replica_groups=mesh['slab'=32,'img'=4] {'img'}, dimensions={1} | all-to-all | bytes 1048576 | tf_op jit(solution)/shard_map/all_to_all | solution.py:142
  98.7 0.9 copy.216
  99.6 9.0 %all-to-all-start.2 = ((f32[32,4,4,2,128]{4,3,2,1,0:T(2,128)}), f32[32,4,4,2,128]{4,3,2,1,0:T(2,128)S(1)}, u32[]{:S(2)}, u32[]{:S(2)}) async-start(f32[32,4,4,2,128]{4,3,2,1,0:T(2,128)} %copy.216), calls=%async_computation.2 | async-start | bytes 1048576 | tf_op jit(solution)/shard_map/all_to_all | solution.py:143
  108.5 0.2 dynamic-slice_reduce_fusion
  108.8 11.2 %all-to-all-done.2 = f32[32,4,4,2,128]{4,3,2,1,0:T(2,128)S(1)} async-done(((f32[32,4,4,2,128]{4,3,2,1,0:T(2,128)}), f32[32,4,4,2,128]{4,3,2,1,0:T(2,128)S(1)}, u32[]{:S(2)}, u32[]{:S(2)}) %all-to-all-start.2) | async-done | bytes 524320 | tf_op jit(solution)/shard_map/all_to_all | solution.py:143
  120.0 0.1 copy.217
  120.1 0.4 copy.218
  120.5 0.6 gather_fusion.1
  121.1 0.6 gather_fusion
  121.7 0.6 add.466
  (50 shorter events, 1.9 us)
Async XLA Ops:
  0.0 8.8 %copy-start.1 = (s32[512,8]{0,1:T(8,128)S(1)}, s32[512,8]{0,1:T(8,128)}, u32[]{:S(2)}) copy-start(s32[512,8]{0,1:T(8,128)} %param.8) | copy-start | bytes 49156
  0.0 9.2 %copy-start.2 = (s32[512,8]{0,1:T(8,128)S(1)}, s32[512,8]{0,1:T(8,128)}, u32[]{:S(2)}) copy-start(s32[512,8]{0,1:T(8,128)} %param.10) | copy-start | bytes 49156
  0.0 9.5 %copy-start.3 = (s32[512,8]{0,1:T(8,128)S(1)}, s32[512,8]{0,1:T(8,128)}, u32[]{:S(2)}) copy-start(s32[512,8]{0,1:T(8,128)} %param.9) | copy-start | bytes 49156
  0.0 59.5 %all-to-all-start = ((f32[32,32,1024]{2,1,0:T(8,128)}), f32[32,32,1024]{2,1,0:T(8,128)}, u32[]{:S(2)}, u32[]{:S(2)}) async-start(f32[32,32,1024]{2,1,0:T(8,128)} %param.7), calls=%async_computation | async-start | bytes 8388608 | tf_op jit(solution)/shard_map/all_to_all | solution.py:136
  23.3 1.8 %copy-start.4 = (f32[512,8]{0,1:T(8,128)S(1)}, f32[512,8]{0,1:T(8,128)}, u32[]{:S(2)}) copy-start(f32[512,8]{0,1:T(8,128)} %param.11) | copy-start | bytes 49156
  23.3 2.1 %copy-start.5 = (f32[512,8]{0,1:T(8,128)S(1)}, f32[512,8]{0,1:T(8,128)}, u32[]{:S(2)}) copy-start(f32[512,8]{0,1:T(8,128)} %param.12) | copy-start | bytes 49156
  23.3 2.5 %copy-start.6 = (f32[512]{0:T(512)S(1)}, f32[512]{0:T(512)}, u32[]{:S(2)}) copy-start(f32[512]{0:T(512)} %param.13) | copy-start | bytes 6148
  25.1 4.2 %copy-start = (f32[1,1,512,1024]{3,2,1,0:T(8,128)S(1)}, f32[1,1,512,1024]{3,2,1,0:T(8,128)}, u32[]{:S(2)}) copy-start(f32[1,1,512,1024]{3,2,1,0:T(8,128)} %copy.208) | copy-start | bytes 6291460
  99.6 20.4 %all-to-all-start.2 = ((f32[32,4,4,2,128]{4,3,2,1,0:T(2,128)}), f32[32,4,4,2,128]{4,3,2,1,0:T(2,128)S(1)}, u32[]{:S(2)}, u32[]{:S(2)}) async-start(f32[32,4,4,2,128]{4,3,2,1,0:T(2,128)} %copy.216), calls=%async_computation.2 | async-start | bytes 1048576 | tf_op jit(solution)/shard_map/all_to_all | solution.py:143

commit v6 on v5

--- a/solution.py
+++ b/solution.py
@@ -7,6 +7,7 @@
 
 LANES = 128
 SPLIT = 8
+CHUNKS = 2
 
 
 CTF_SCALE = 20.0
@@ -30,10 +31,11 @@
     return plane, rank
 
 
-def send_parts(plane, first_plane, meta, box, n_dev):
+def send_parts(planes, first_plane, meta, box, n_dev):
     blk_plane, blk_row, blk_col, frac_plane, frac_row, defocus = meta
     n_blk = blk_plane.shape[1]
-    own, n_rows, x = plane.shape
+    own, n_rows, width = planes[0].shape
+    x = width * len(planes)
     plane_of, rank = slot_tables(blk_plane, n_dev)
     k_dev = plane_of.shape[1]
     t = lax.iota(jnp.int32, own)[:, None, None, None]
@@ -82,15 +84,20 @@
     w_im = ((1.0 - frac_y) * lo_im + frac_y * hi_im) * norm
     n_s = w_re.shape[0] // own
     w_all = jnp.stack([w_re.reshape(own, n_s, n_rows), w_im.reshape(own, n_s, n_rows)], axis=1)
-    r_t = jnp.einsum("trc,tpsr->tpcs", plane, w_all, precision=MID)
     m = x // SPLIT
-    r5 = r_t.reshape(own, 2, m, SPLIT, n_s)
+    step_n2 = m // len(planes)
     idx = lax.iota(jnp.int32, m)
     c_re, c_im = roots(idx[:, None], idx[None, :], m, 1.0 / math.sqrt(x))
     w_col = jnp.stack(
         [jnp.stack([c_re, -c_im], axis=1), jnp.stack([c_im, c_re], axis=1)], axis=0
     )
-    y = jnp.einsum("qkpn,tpnjs->tqkjs", w_col, r5, precision=MID)
+    y = None
+    for j, piece in enumerate(planes):
+        r_t = jnp.einsum("trc,tpsr->tpcs", piece, w_all, precision=MID)
+        r5 = r_t.reshape(own, 2, step_n2, SPLIT, n_s)
+        w_j = w_col[:, :, :, j * step_n2:(j + 1) * step_n2]
+        y_j = jnp.einsum("qkpn,tpnjs->tqkjs", w_j, r5, precision=MID)
+        y = y_j if y is None else y + y_j
     y_re = y[:, 0]
     y_im = y[:, 1]
     n1 = lax.iota(jnp.int32, SPLIT)
@@ -133,14 +140,18 @@
     n_slab = lax.axis_size("slab")
     n_img = lax.axis_size("img")
     n_dev = n_slab * n_img
-    plane = lax.all_to_all(volume, "slab", split_axis=0, concat_axis=1, tiled=True)
-    own = plane.shape[0]
+    width = box // CHUNKS
+    planes = [
+        lax.all_to_all(
+            volume[:, :, j * width:(j + 1) * width], "slab", split_axis=0, concat_axis=1, tiled=True
+        )
+        for j in range(CHUNKS)
+    ]
+    own = planes[0].shape[0]
     first_plane = (lax.axis_index("img") * n_slab + lax.axis_index("slab")) * own
     meta = (blk_plane, blk_row, blk_col, frac_plane, frac_row, defocus)
-    parts = send_parts(plane, first_plane, meta, box, n_dev)
-    parts = parts.reshape(n_slab, n_img, *parts.shape[1:])
-    parts = lax.all_to_all(parts, "img", split_axis=1, concat_axis=1, tiled=True)
-    recv = lax.all_to_all(parts, "slab", split_axis=0, concat_axis=0, tiled=True)
+    parts = send_parts(planes, first_plane, meta, box, n_dev)
+    recv = lax.all_to_all(parts, ("slab", "img"), split_axis=0, concat_axis=0, tiled=True)
     me = lax.axis_index("slab") * n_img + lax.axis_index("img")
     total = gather_parts(recv, blk_plane, me, own, n_slab, n_img)
     n_blk = blk_plane.shape[1]

time: 123 us -> 116 us (0.943)
  blocking collectives: 11.8 us -> 0 us
  starting transfers between devices: 17.7 us -> 22.6 us
  waiting for transfers between devices: 35.8 us -> 39.2 us
  other arithmetic: 16.4 us -> 14.2 us
    all_to_all x1 -> x0, blocking collectives: 11.8 us -> none  [on_device(): lax.all_to_all(parts, 'img', split_axis=1, concat_axis=1, tiled=True)]
    transpose x1 -> x0, local copies, waits for them, and re-layouts: 5.41 us -> none  [send_parts(): r_t = jnp.einsum('trc,tpsr->tpcs', plane, w_all, precision=MID)]
    slice x0 -> x1, local copies, waits for them, and re-layouts: none -> 5 us  [on_device(): volume[:, :, j * width:(j + 1) * width]]
    all_to_all x2 -> x3, starting transfers between devices: 17.7 us -> 22.6 us  [the longest x2 14.7 us: on_device(): lax.all_to_all(volume[:, :, j * width:(j + 1) * width], 'slab', split_axi...]
    all_to_all x2 -> x3, waiting for transfers between devices: 35.8 us -> 39.2 us  [the longest x2 25.7 us: on_device(): lax.all_to_all(volume[:, :, j * width:(j + 1) * width], 'slab', split_axi...]
    mul x1, other arithmetic: 2.55 us -> 1.07 us  [send_parts(): parts = jnp.stack([scale * o_re, scale * o_im], axis=1)]
    mul x1, other arithmetic: 5.49 us -> 4.12 us  [send_parts(): w_re = ((1.0 - frac_y) * lo_re + frac_y * hi_re) * norm]
    unnamed x19 -> x23, local copies, waits for them, and re-layouts: 0.7 us -> 2.04 us
  transfers between devices with their start and end apart: 2 -> 3, of which waited for: 2 -> 3; matrix products, arithmetic and copies ran while one was open for 21% -> 26% of each run, Pallas kernels for 0% -> 0%
where the time goes in v6:
time: 116 us
  waiting for transfers between devices  39.2 us (34%)
  starting transfers between devices  22.6 us (19%)
  local copies, waits for them, and re-layouts  21.9 us (19%)
  matrix products  17.6 us (15%)
  other arithmetic  14.2 us (12%)
    all_to_all x2, waiting for transfers between devices, on_device(): lax.all_to_all(volume[:, :, j * width:(j + 1) * width], 'slab', split_axi...  25.7 us
    all_to_all x2, starting transfers between devices, on_device(): lax.all_to_all(volume[:, :, j * width:(j + 1) * width], 'slab', split_axi...  14.7 us
    all_to_all x1, waiting for transfers between devices, on_device(): lax.all_to_all(parts, ('slab', 'img'), split_axis=0, concat_axis=0, tiled...  13.5 us
    dot_general x2, matrix products, send_parts(): r_t = jnp.einsum('trc,tpsr->tpcs', piece, w_all, precision=MID)  12.1 us
    all_to_all x1, starting transfers between devices, on_device(): lax.all_to_all(parts, ('slab', 'img'), split_axis=0, concat_axis=0, tiled...  7.84 us
    sub x2, local copies, waits for them, and re-layouts, row_roots(): a_re[:, :, None] * b_re[:, None, :] - a_im[:, :, None] * b_im[:, None, :]  5.94 us
    dot_general x2, matrix products, send_parts(): y_j = jnp.einsum('qkpn,tpnjs->tqkjs', w_j, r5, precision=MID)  5.53 us
    slice x1, local copies, waits for them, and re-layouts, on_device(): volume[:, :, j * width:(j + 1) * width]  5 us
  transfers between devices with their start and end apart: 3, of which 3 were waited for; matrix products, arithmetic and copies ran while one was open for 26% of the time, Pallas kernels for 0%

profile of v6, /device:TPU:1, one launch (start us, length us, event | category | flops | bytes accessed | tf_op | source)
XLA Modules:
  0.0 115.9 jit_solution(2933493097637368302)
XLA Ops:
  0.0 5.0 %fusion.83 = (f32[32,32,512]{2,1,0:T(8,128)}, f32[32,32,512]{2,1,0:T(8,128)}) fusion(f32[32,32,1024]{2,1,0:T(8,128)} %param.7), kind=kLoop, calls=%fused_computation.179 | loop fusion | bytes 8388608 | tf_op jit(solution)/shard_map/slice | solution.py:146
  5.0 8.8 %all-to-all-start.1 = ((f32[32,32,512]{2,1,0:T(8,128)}), f32[32,32,512]{2,1,0:T(8,128)}, u32[]{:S(2)}, u32[]{:S(2)}) async-start(f32[32,32,512]{2,1,0:T(8,128)} %get-tuple-element.12), calls=%async_computation.1 | async-start | bytes 4194304 | tf_op jit(solution)/shard_map/all_to_all | solution.py:145
  13.8 0.3 fusion.55
  14.2 0.1 copy.177
  14.3 0.1 eq.87
  14.5 0.1 copy.183
  14.7 0.1 broadcast_in_dim.129
  14.8 0.1 copy.185
  15.0 0.1 broadcast_in_dim.132
  15.2 0.2 convert_reduce_fusion
  15.6 0.2 copy.192
  15.7 0.2 mul.880
  15.9 0.1 copy.181
  16.0 0.1 broadcast_in_dim.125
  16.2 0.1 copy.189
  16.6 0.1 broadcast_in_dim.134
  16.8 0.3 negate_multiply_fusion
  17.2 1.1 fusion.54
  18.2 2.0 %multiply_subtract_fusion.1 = (f32[512,32,32]{0,2,1:T(8,128)}, f32[512,32,32]{0,2,1:T(8,128)S(1)}) fusion(f32[512,32]{0,1:T(8,128)S(1)} %get-tuple-element.32, f32[512,32]{0,1:T(8,128)S(1)} %get-tuple-element.27, f32[512,32]{0,1:T(8,128)S(1)} %get-tuple-element.33, f32[512,32]{0,1:T(8,128)S(1)} %get-tuple-element.26), kind=kLoop, calls=%fused_computation.20 | loop fusion | flops 3145728 | bytes 4456448 | tf_op jit(solution)/shard_map/sub | solution.py:76
  20.2 2.6 %multiply_subtract_fusion = (f32[512,32,32]{0,2,1:T(8,128)}, f32[512,32,32]{0,2,1:T(8,128)}) fusion(f32[512,32]{0,1:T(8,128)S(1)} %get-tuple-element.37, f32[512,32]{0,1:T(8,128)S(1)} %get-tuple-element.38, f32[512,32]{0,1:T(8,128)S(1)} %get-tuple-element.36, f32[512,32]{0,1:T(8,128)S(1)} %get-tuple-element.39), kind=kLoop, calls=%fused_computation.19 | loop fusion | flops 3145728 | bytes 4456448 | tf_op jit(solution)/shard_map/sub | solution.py:76
  22.8 19.7 %all-to-all-done.1 = f32[32,32,512]{2,1,0:T(8,128)} async-done(((f32[32,32,512]{2,1,0:T(8,128)}), f32[32,32,512]{2,1,0:T(8,128)}, u32[]{:S(2)}, u32[]{:S(2)}) %all-to-all-start.1) | async-done | bytes 2097184 | tf_op jit(solution)/shard_map/all_to_all | solution.py:145
  42.5 6.0 %all-to-all-start = ((f32[32,32,512]{2,1,0:T(8,128)}), f32[32,32,512]{2,1,0:T(8,128)}, u32[]{:S(2)}, u32[]{:S(2)}) async-start(f32[32,32,512]{2,1,0:T(8,128)} %get-tuple-element.13), calls=%async_computation | async-start | bytes 4194304 | tf_op jit(solution)/shard_map/all_to_all | solution.py:145
  48.5 0.2 copy.188
  48.7 2.9 %copy.193 = f32[1,1,512,1024]{3,2,1,0:T(8,128)} copy(f32[1,1,512,1024]{2,3,1,0:T(8,128)} %bitcast.124) | data formatting | bytes 4194304 | tf_op jit(solution)/shard_map/sub | solution.py:76
  51.6 1.8 %copy.195 = f32[1,1,512,1024]{3,2,1,0:T(8,128)} copy(f32[1,1,512,1024]{2,3,1,0:T(8,128)S(1)} %bitcast.123) | data formatting | bytes 4194304 | tf_op jit(solution)/shard_map/add | solution.py:77
  53.4 3.0 %copy.194 = f32[1,1,512,1024]{3,2,1,0:T(8,128)} copy(f32[1,1,512,1024]{2,3,1,0:T(8,128)} %bitcast.126) | data formatting | bytes 4194304 | tf_op jit(solution)/shard_map/sub | solution.py:76
  56.4 1.8 %copy.196 = f32[1,1,512,1024]{3,2,1,0:T(8,128)} copy(f32[1,1,512,1024]{2,3,1,0:T(8,128)S(1)} %bitcast.125) | data formatting | bytes 4194304 | tf_op jit(solution)/shard_map/add | solution.py:77
  58.3 0.2 copy.191
  58.4 0.2 broadcast_in_dim_reshape.2
  58.6 0.2 mul.863
  59.0 4.1 %add_multiply_fusion.1 = (f32[1,1,512,1024]{3,2,1,0:T(8,128)S(1)}, f32[1,1,512,1024]{3,2,1,0:T(8,128)S(1)}) fusion(f32[1,1,512,1024]{3,2,1,0:T(8,128)} %copy.194, f32[1,1,512,1024]{3,2,1,0:T(8,128)} %copy.193, f32[512]{0:T(512)S(1)} %broadcast_in_dim_reshape.2, f32[512]{0:T(512)S(1)} %broadcast_subtract_fusion, f32[1,1,512,1024]{3,2,1,0:T(8,128)} %copy.196, ...), kind=kLoop, calls=%fused_computation.18 | loop fusion | flops 4194304 | bytes 12587008 | tf_op jit(solution)/shard_map/mul | solution.py:83
  63.1 1.3 %copy-done = f32[1,1,512,1024]{3,2,1,0:T(8,128)} copy-done((f32[1,1,512,1024]{3,2,1,0:T(8,128)}, f32[1,1,512,1024]{3,2,1,0:T(8,128)S(1)}, u32[]{:S(2)}) %copy-start) | copy-done | bytes 2097176
  64.4 6.4 %fusion.7 = f32[2,64,8,512,1]{3,2,1,0,4:T(8,128)} fusion(f32[1024,512,1]{1,0,2:T(8,128)} %bitcast.22, f32[1,1,512,1024]{3,2,1,0:T(8,128)S(1)} %get-tuple-element.25, f32[1,1,512,1024]{3,2,1,0:T(8,128)S(1)} %get-tuple-element.24), kind=kOutput, calls=%fused_computation.23 | convolution fusion | flops 3222274048 | bytes 8388608 | tf_op jit(solution)/shard_map/trc,tpsr->tpcs/dot_general | solution.py:96
  70.8 6.0 %all-to-all-done = f32[32,32,512]{2,1,0:T(8,128)} async-done(((f32[32,32,512]{2,1,0:T(8,128)}), f32[32,32,512]{2,1,0:T(8,128)}, u32[]{:S(2)}, u32[]{:S(2)}) %all-to-all-start) | async-done | bytes 2097184 | tf_op jit(solution)/shard_map/all_to_all | solution.py:145
  76.9 5.7 %fusion.6 = f32[2,64,8,512,1]{3,2,1,0,4:T(8,128)S(1)} fusion(f32[1024,512,1]{1,0,2:T(8,128)} %bitcast.11, f32[1,1,512,1024]{3,2,1,0:T(8,128)} %copy-done, f32[1,1,512,1024]{3,2,1,0:T(8,128)S(1)} %get-tuple-element.24), kind=kOutput, calls=%fused_computation.22 | convolution fusion | flops 3222274048 | bytes 8388608 | tf_op jit(solution)/shard_map/trc,tpsr->tpcs/dot_general | solution.py:96
  82.5 2.6 %fusion.4 = f32[8,512,2,128,1]{3,1,4,2,0:T(8,128)S(1)} fusion(f32[2,64,8,512,1]{3,2,1,0,4:T(8,128)S(1)} %fusion.6, f32[1,128,2,128]{1,3,2,0:T(8,128)S(1)} %get-tuple-element.21, f32[1,128,2,128]{1,3,2,0:T(8,128)S(1)} %get-tuple-element.20), kind=kOutput, calls=%fused_computation.10 | convolution fusion | flops 805339136 | bytes 6553600 | tf_op jit(solution)/shard_map/qkpn,tpnjs->tqkjs/dot_general | solution.py:99
  85.2 2.9 %fusion = f32[1,2,128,8,512]{2,4,1,3,0:T(8,128)S(1)} fusion(f32[8,512,2,128,1]{3,1,4,2,0:T(8,128)S(1)} %fusion.4, f32[2,64,8,512,1]{3,2,1,0,4:T(8,128)S(1)} %copy-done.2, f32[1,128,2,128]{1,3,2,0:T(8,128)S(1)} %get-tuple-element.20, f32[1,128,2,128]{1,3,2,0:T(8,128)S(1)} %get-tuple-element.21), kind=kOutput, calls=%fused_computation.4 | convolution fusion | flops 806387712 | bytes 10747904 | tf_op jit(solution)/shard_map/qkpn,tpnjs->tqkjs/dot_general | solution.py:99
  88.1 1.4 %subtract_reduce_fusion = (f32[128,512]{0,1:T(8,128)S(1)}, f32[128,512]{0,1:T(8,128)S(1)}) fusion(f32[1,2,128,8,512]{2,4,1,3,0:T(8,128)S(1)} %fusion, f32[128,8]{0,1:T(8,128)S(1)} %get-tuple-element.44, f32[8,512]{1,0:T(8,128)S(1)} %get-tuple-element.31, f32[128,8]{0,1:T(8,128)S(1)} %get-tuple-element.45, f32[8,512]{1,0:T(8,128)S(1)} %get-tuple-element.30), kind=kLoop, calls=%fused_computation.13 | loop fusion | flops 7208960 | bytes 4759552 | tf_op jit(solution)/shard_map/reduce_sum | solution.py:113
  89.6 1.1 copy_multiply_fusion.1
  90.7 1.2 %copy.204 = f32[128,4,2,128]{3,2,1,0:T(2,128)} copy(f32[128,4,2,128]{3,0,2,1:T(8,128)S(1)} %pad_maximum_fusion) | data formatting | bytes 1048576 | tf_op jit(solution)/shard_map/stack | solution.py:117
  91.9 7.8 %all-to-all-start.2 = ((f32[128,4,2,128]{3,2,1,0:T(2,128)}), f32[128,4,2,128]{3,2,1,0:T(2,128)S(1)}, u32[]{:S(2)}, u32[]{:S(2)}) async-start(f32[128,4,2,128]{3,2,1,0:T(2,128)} %copy.204), calls=%async_computation.2 | async-start | bytes 1048576 | tf_op jit(solution)/shard_map/all_to_all | solution.py:154
  99.7 0.2 dynamic-slice_reduce_fusion
  100.0 13.5 %all-to-all-done.2 = f32[128,4,2,128]{3,2,1,0:T(2,128)S(1)} async-done(((f32[128,4,2,128]{3,2,1,0:T(2,128)}), f32[128,4,2,128]{3,2,1,0:T(2,128)S(1)}, u32[]{:S(2)}, u32[]{:S(2)}) %all-to-all-start.2) | async-done | bytes 524320 | tf_op jit(solution)/shard_map/all_to_all | solution.py:154
  113.5 0.1 copy.205
  113.6 0.4 copy.206
  114.0 0.6 gather_fusion.1
  114.7 0.6 gather_fusion
  115.3 0.6 add.478
  (47 shorter events, 1.0 us)
Async XLA Ops:
  5.0 9.2 %copy-start.3 = (s32[512,8]{0,1:T(8,128)S(1)}, s32[512,8]{0,1:T(8,128)}, u32[]{:S(2)}) copy-start(s32[512,8]{0,1:T(8,128)} %param.8) | copy-start | bytes 49156
  5.0 9.5 %copy-start.4 = (s32[512,8]{0,1:T(8,128)S(1)}, s32[512,8]{0,1:T(8,128)}, u32[]{:S(2)}) copy-start(s32[512,8]{0,1:T(8,128)} %param.10) | copy-start | bytes 49156
  5.0 9.8 %copy-start.5 = (s32[512,8]{0,1:T(8,128)S(1)}, s32[512,8]{0,1:T(8,128)}, u32[]{:S(2)}) copy-start(s32[512,8]{0,1:T(8,128)} %param.9) | copy-start | bytes 49156
  5.0 37.5 %all-to-all-start.1 = ((f32[32,32,512]{2,1,0:T(8,128)}), f32[32,32,512]{2,1,0:T(8,128)}, u32[]{:S(2)}, u32[]{:S(2)}) async-start(f32[32,32,512]{2,1,0:T(8,128)} %get-tuple-element.12), calls=%async_computation.1 | async-start | bytes 4194304 | tf_op jit(solution)/shard_map/all_to_all | solution.py:145
  13.8 2.1 %copy-start.6 = (f32[512,8]{0,1:T(8,128)S(1)}, f32[512,8]{0,1:T(8,128)}, u32[]{:S(2)}) copy-start(f32[512,8]{0,1:T(8,128)} %param.11) | copy-start | bytes 49156
  13.8 2.4 %copy-start.7 = (f32[512,8]{0,1:T(8,128)S(1)}, f32[512,8]{0,1:T(8,128)}, u32[]{:S(2)}) copy-start(f32[512,8]{0,1:T(8,128)} %param.12) | copy-start | bytes 49156
  13.8 2.7 %copy-start.8 = (f32[512]{0:T(512)S(1)}, f32[512]{0:T(512)}, u32[]{:S(2)}) copy-start(f32[512]{0:T(512)} %param.13) | copy-start | bytes 6148
  42.5 34.3 %all-to-all-start = ((f32[32,32,512]{2,1,0:T(8,128)}), f32[32,32,512]{2,1,0:T(8,128)}, u32[]{:S(2)}, u32[]{:S(2)}) async-start(f32[32,32,512]{2,1,0:T(8,128)} %get-tuple-element.13), calls=%async_computation | async-start | bytes 4194304 | tf_op jit(solution)/shard_map/all_to_all | solution.py:145
  53.4 3.1 %copy-start.1 = (f32[512,32,32]{0,2,1:T(8,128)S(1)}, f32[512,32,32]{0,2,1:T(8,128)}, u32[]{:S(2)}) copy-start(f32[512,32,32]{0,2,1:T(8,128)} %get-tuple-element.17) | copy-start | bytes 6291460
  63.1 1.3 %copy-start = (f32[1,1,512,1024]{3,2,1,0:T(8,128)}, f32[1,1,512,1024]{3,2,1,0:T(8,128)S(1)}, u32[]{:S(2)}) copy-start(f32[1,1,512,1024]{3,2,1,0:T(8,128)S(1)} %get-tuple-element.25) | copy-start | bytes 6291460
  82.5 2.7 %copy-start.2 = (f32[2,64,8,512,1]{3,2,1,0,4:T(8,128)S(1)}, f32[2,64,8,512,1]{3,2,1,0,4:T(8,128)}, u32[]{:S(2)}) copy-start(f32[2,64,8,512,1]{3,2,1,0,4:T(8,128)} %fusion.7) | copy-start | bytes 6291460
  91.9 21.6 %all-to-all-start.2 = ((f32[128,4,2,128]{3,2,1,0:T(2,128)}), f32[128,4,2,128]{3,2,1,0:T(2,128)S(1)}, u32[]{:S(2)}, u32[]{:S(2)}) async-start(f32[128,4,2,128]{3,2,1,0:T(2,128)} %copy.204), calls=%async_computation.2 | async-start | bytes 1048576 | tf_op jit(solution)/shard_map/all_to_all | solution.py:154

commit v7 on v6

--- a/solution.py
+++ b/solution.py
@@ -7,7 +7,6 @@
 
 LANES = 128
 SPLIT = 8
-CHUNKS = 2
 
 
 CTF_SCALE = 20.0
@@ -140,13 +139,7 @@
     n_slab = lax.axis_size("slab")
     n_img = lax.axis_size("img")
     n_dev = n_slab * n_img
-    width = box // CHUNKS
-    planes = [
-        lax.all_to_all(
-            volume[:, :, j * width:(j + 1) * width], "slab", split_axis=0, concat_axis=1, tiled=True
-        )
-        for j in range(CHUNKS)
-    ]
+    planes = [lax.all_to_all(volume, "slab", split_axis=0, concat_axis=1, tiled=True)]
     own = planes[0].shape[0]
     first_plane = (lax.axis_index("img") * n_slab + lax.axis_index("slab")) * own
     meta = (blk_plane, blk_row, blk_col, frac_plane, frac_row, defocus)

time: 116 us -> 111 us (0.957)
  starting transfers between devices: 22.6 us -> 17.5 us
    all_to_all x2 -> x1, starting transfers between devices: 14.7 us -> 8.78 us  [on_device(): lax.all_to_all(volume, 'slab', split_axis=0, concat_axis=1, tiled=True)]
    transpose x0 -> x1, local copies, waits for them, and re-layouts: none -> 5.41 us  [send_parts(): r_t = jnp.einsum('trc,tpsr->tpcs', piece, w_all, precision=MID)]
    slice x1 -> x0, local copies, waits for them, and re-layouts: 5 us -> none  [on_device(): volume[:, :, j * width:(j + 1) * width]]
    mul x1, other arithmetic: 4.12 us -> 5.49 us  [send_parts(): w_re = ((1.0 - frac_y) * lo_re + frac_y * hi_re) * norm]
    unnamed x23 -> x19, local copies, waits for them, and re-layouts: 2.04 us -> 0.7 us
    dot_general x2 -> x1, matrix products: 12.1 us -> 11.1 us  [send_parts(): r_t = jnp.einsum('trc,tpsr->tpcs', piece, w_all, precision=MID)]
    dot_general x2 -> x1, matrix products: 5.53 us -> 6.38 us  [send_parts(): y_j = jnp.einsum('qkpn,tpnjs->tqkjs', w_j, r5, precision=MID)]
    all_to_all x2 -> x1, waiting for transfers between devices: 25.7 us -> 26.5 us  [on_device(): lax.all_to_all(volume, 'slab', split_axis=0, concat_axis=1, tiled=True)]
  transfers between devices with their start and end apart: 3 -> 2, of which waited for: 3 -> 2; matrix products, arithmetic and copies ran while one was open for 26% -> 22% of each run, Pallas kernels for 0% -> 0%
where the time goes in v7:
time: 111 us
  waiting for transfers between devices  40 us (36%)
  local copies, waits for them, and re-layouts  20.9 us (19%)
  starting transfers between devices  17.5 us (16%)
  matrix products  17.5 us (16%)
  other arithmetic  14.8 us (13%)
    all_to_all x1, waiting for transfers between devices, on_device(): lax.all_to_all(volume, 'slab', split_axis=0, concat_axis=1, tiled=True)  26.5 us
    all_to_all x1, waiting for transfers between devices, on_device(): lax.all_to_all(parts, ('slab', 'img'), split_axis=0, concat_axis=0, tiled...  13.5 us
    dot_general x1, matrix products, send_parts(): r_t = jnp.einsum('trc,tpsr->tpcs', piece, w_all, precision=MID)  11.1 us
    all_to_all x1, starting transfers between devices, on_device(): lax.all_to_all(volume, 'slab', split_axis=0, concat_axis=1, tiled=True)  8.78 us
    all_to_all x1, starting transfers between devices, on_device(): lax.all_to_all(parts, ('slab', 'img'), split_axis=0, concat_axis=0, tiled...  8.76 us
    dot_general x1, matrix products, send_parts(): y_j = jnp.einsum('qkpn,tpnjs->tqkjs', w_j, r5, precision=MID)  6.38 us
    sub x2, local copies, waits for them, and re-layouts, row_roots(): a_re[:, :, None] * b_re[:, None, :] - a_im[:, :, None] * b_im[:, None, :]  5.86 us
    mul x1, other arithmetic, send_parts(): w_re = ((1.0 - frac_y) * lo_re + frac_y * hi_re) * norm  5.49 us
  transfers between devices with their start and end apart: 2, of which 2 were waited for; matrix products, arithmetic and copies ran while one was open for 22% of the time, Pallas kernels for 0%

profile of v7, /device:TPU:1, one launch (start us, length us, event | category | flops | bytes accessed | tf_op | source)
XLA Modules:
  0.0 111.1 jit_solution(14803688463321089475)
XLA Ops:
  0.0 8.8 %all-to-all-start = ((f32[32,32,1024]{2,1,0:T(8,128)}), f32[32,32,1024]{2,1,0:T(8,128)}, u32[]{:S(2)}, u32[]{:S(2)}) async-start(f32[32,32,1024]{2,1,0:T(8,128)} %param.7), calls=%async_computation | async-start | bytes 8388608 | tf_op jit(solution)/shard_map/all_to_all | solution.py:142
  8.8 0.1 copy.162
  9.0 0.1 eq.87
  9.2 0.1 copy.168
  9.3 0.1 broadcast_in_dim.129
  9.5 0.1 copy.170
  9.6 0.1 broadcast_in_dim.132
  9.8 0.2 convert_reduce_fusion
  10.1 0.1 iota_compare_fusion
  10.2 0.2 copy.177
  10.3 0.2 mul.880
  10.5 1.1 fusion.51
  11.6 1.9 %multiply_subtract_fusion.1 = (f32[512,32,32]{0,2,1:T(8,128)}, f32[512,32,32]{0,2,1:T(8,128)S(1)}) fusion(f32[512,32]{0,1:T(8,128)S(1)} %get-tuple-element.30, f32[512,32]{0,1:T(8,128)S(1)} %get-tuple-element.25, f32[512,32]{0,1:T(8,128)S(1)} %get-tuple-element.31, f32[512,32]{0,1:T(8,128)S(1)} %get-tuple-element.24), kind=kLoop, calls=%fused_computation.20 | loop fusion | flops 3145728 | bytes 4456448 | tf_op jit(solution)/shard_map/sub | solution.py:75
  13.6 2.9 %copy.178 = f32[1,1,512,1024]{3,2,1,0:T(8,128)} copy(f32[1,1,512,1024]{2,3,1,0:T(8,128)} %bitcast.101) | data formatting | bytes 4194304 | tf_op jit(solution)/shard_map/sub | solution.py:75
  16.5 1.9 %copy.180 = f32[1,1,512,1024]{3,2,1,0:T(8,128)} copy(f32[1,1,512,1024]{2,3,1,0:T(8,128)S(1)} %bitcast.99) | data formatting | bytes 4194304 | tf_op jit(solution)/shard_map/add | solution.py:76
  18.3 1.9 %multiply_subtract_fusion = (f32[512,32,32]{0,2,1:T(8,128)}, f32[512,32,32]{0,2,1:T(8,128)S(1)}) fusion(f32[512,32]{0,1:T(8,128)S(1)} %get-tuple-element.35, f32[512,32]{0,1:T(8,128)S(1)} %get-tuple-element.36, f32[512,32]{0,1:T(8,128)S(1)} %get-tuple-element.34, f32[512,32]{0,1:T(8,128)S(1)} %get-tuple-element.37), kind=kLoop, calls=%fused_computation.19 | loop fusion | flops 3145728 | bytes 4456448 | tf_op jit(solution)/shard_map/sub | solution.py:75
  20.3 3.0 %copy.179 = f32[1,1,512,1024]{3,2,1,0:T(8,128)} copy(f32[1,1,512,1024]{2,3,1,0:T(8,128)} %bitcast.102) | data formatting | bytes 4194304 | tf_op jit(solution)/shard_map/sub | solution.py:75
  23.2 1.8 %copy.181 = f32[1,1,512,1024]{3,2,1,0:T(8,128)} copy(f32[1,1,512,1024]{2,3,1,0:T(8,128)S(1)} %bitcast.100) | data formatting | bytes 4194304 | tf_op jit(solution)/shard_map/add | solution.py:76
  25.0 0.1 copy.166
  25.2 0.1 broadcast_in_dim.125
  25.3 0.1 copy.174
  25.5 0.1 broadcast_in_dim.138
  25.7 0.1 broadcast_in_dim.134
  25.8 0.1 copy.172
  25.9 0.1 fusion.34
  25.9 0.2 copy.176
  26.1 0.2 broadcast_in_dim_reshape.2
  26.3 0.2 copy.173
  26.5 0.2 mul.863
  26.8 0.3 fusion.52
  27.0 0.3 negate_multiply_fusion
  27.4 0.1 fusion.59
  27.5 5.5 %add_multiply_fusion.1 = (f32[1,1,512,1024]{3,2,1,0:T(8,128)}, f32[1,1,512,1024]{3,2,1,0:T(8,128)}) fusion(f32[1,1,512,1024]{3,2,1,0:T(8,128)} %copy.179, f32[1,1,512,1024]{3,2,1,0:T(8,128)S(1)} %copy-done, f32[512]{0:T(512)S(1)} %broadcast_in_dim_reshape.2, f32[512]{0:T(512)S(1)} %broadcast_subtract_fusion, f32[1,1,512,1024]{3,2,1,0:T(8,128)} %copy.181, ...), kind=kLoop, calls=%fused_computation.18 | loop fusion | flops 4194304 | bytes 12587008 | tf_op jit(solution)/shard_map/mul | solution.py:82
  33.0 26.5 %all-to-all-done = f32[32,32,1024]{2,1,0:T(8,128)} async-done(((f32[32,32,1024]{2,1,0:T(8,128)}), f32[32,32,1024]{2,1,0:T(8,128)}, u32[]{:S(2)}, u32[]{:S(2)}) %all-to-all-start) | async-done | bytes 4194336 | tf_op jit(solution)/shard_map/all_to_all | solution.py:142
  59.5 11.1 %fusion.8 = f32[1,2,1024,512]{2,3,1,0:T(8,128)} fusion(f32[1024,1024,1]{1,0,2:T(8,128)} %bitcast.11, f32[1,1,512,1024]{3,2,1,0:T(8,128)} %get-tuple-element.23, f32[1,1,512,1024]{3,2,1,0:T(8,128)} %get-tuple-element.22), kind=kOutput, calls=%fused_computation.9 | convolution fusion | flops 6443499520 | bytes 12582912 | tf_op jit(solution)/shard_map/trc,tpsr->tpcs/dot_general | solution.py:95
  70.6 5.4 %copy.182 = f32[1,2,1024,512]{3,2,1,0:T(8,128)} copy(f32[1,2,1024,512]{2,3,1,0:T(8,128)} %fusion.8) | data formatting | bytes 8388608 | tf_op jit(solution)/shard_map/trc,tpsr->tpcs/transpose | solution.py:95
  76.0 6.4 %fusion.5 = f32[1,2,128,8,512]{2,4,1,3,0:T(8,128)S(1)} fusion(f32[2,128,8,512,1]{3,2,1,0,4:T(8,128)} %bitcast.98, f32[1,128,2,128]{3,1,2,0:T(8,128)S(1)} %get-tuple-element.19, f32[1,128,2,128]{3,1,2,0:T(8,128)S(1)} %get-tuple-element.18), kind=kOutput, calls=%fused_computation.8 | convolution fusion | flops 1610678272 | bytes 8650752 | tf_op jit(solution)/shard_map/qkpn,tpnjs->tqkjs/dot_general | solution.py:98
  82.4 1.4 %subtract_reduce_fusion = (f32[128,512]{0,1:T(8,128)S(1)}, f32[128,512]{0,1:T(8,128)S(1)}) fusion(f32[1,2,128,8,512]{2,4,1,3,0:T(8,128)S(1)} %fusion.5, f32[128,8]{0,1:T(8,128)S(1)} %get-tuple-element.42, f32[8,512]{1,0:T(8,128)S(1)} %get-tuple-element.29, f32[128,8]{0,1:T(8,128)S(1)} %get-tuple-element.43, f32[8,512]{1,0:T(8,128)S(1)} %get-tuple-element.28), kind=kLoop, calls=%fused_computation.13 | loop fusion | flops 7208960 | bytes 4759552 | tf_op jit(solution)/shard_map/reduce_sum | solution.py:112
  83.8 1.1 copy_multiply_fusion.1
  85.0 1.2 %copy.187 = f32[128,4,2,128]{3,2,1,0:T(2,128)} copy(f32[128,4,2,128]{3,0,2,1:T(8,128)S(1)} %pad_maximum_fusion) | data formatting | bytes 1048576 | tf_op jit(solution)/shard_map/stack | solution.py:116
  86.2 8.8 %all-to-all-start.1 = ((f32[128,4,2,128]{3,2,1,0:T(2,128)}), f32[128,4,2,128]{3,2,1,0:T(2,128)S(1)}, u32[]{:S(2)}, u32[]{:S(2)}) async-start(f32[128,4,2,128]{3,2,1,0:T(2,128)} %copy.187), calls=%async_computation.1 | async-start | bytes 1048576 | tf_op jit(solution)/shard_map/all_to_all | solution.py:147
  94.9 0.2 dynamic-slice_reduce_fusion
  95.2 13.5 %all-to-all-done.1 = f32[128,4,2,128]{3,2,1,0:T(2,128)S(1)} async-done(((f32[128,4,2,128]{3,2,1,0:T(2,128)}), f32[128,4,2,128]{3,2,1,0:T(2,128)S(1)}, u32[]{:S(2)}, u32[]{:S(2)}) %all-to-all-start.1) | async-done | bytes 524320 | tf_op jit(solution)/shard_map/all_to_all | solution.py:147
  108.7 0.1 copy.188
  108.8 0.4 copy.189
  109.3 0.6 gather_fusion.1
  109.9 0.6 gather_fusion
  110.5 0.6 add.466
  (39 shorter events, 0.6 us)
Async XLA Ops:
  0.0 8.8 %copy-start.1 = (s32[512,8]{0,1:T(8,128)S(1)}, s32[512,8]{0,1:T(8,128)}, u32[]{:S(2)}) copy-start(s32[512,8]{0,1:T(8,128)} %param.8) | copy-start | bytes 49156
  0.0 9.2 %copy-start.2 = (s32[512,8]{0,1:T(8,128)S(1)}, s32[512,8]{0,1:T(8,128)}, u32[]{:S(2)}) copy-start(s32[512,8]{0,1:T(8,128)} %param.10) | copy-start | bytes 49156
  0.0 9.5 %copy-start.3 = (s32[512,8]{0,1:T(8,128)S(1)}, s32[512,8]{0,1:T(8,128)}, u32[]{:S(2)}) copy-start(s32[512,8]{0,1:T(8,128)} %param.9) | copy-start | bytes 49156
  0.0 59.5 %all-to-all-start = ((f32[32,32,1024]{2,1,0:T(8,128)}), f32[32,32,1024]{2,1,0:T(8,128)}, u32[]{:S(2)}, u32[]{:S(2)}) async-start(f32[32,32,1024]{2,1,0:T(8,128)} %param.7), calls=%async_computation | async-start | bytes 8388608 | tf_op jit(solution)/shard_map/all_to_all | solution.py:142
  23.2 1.8 %copy-start.4 = (f32[512,8]{0,1:T(8,128)S(1)}, f32[512,8]{0,1:T(8,128)}, u32[]{:S(2)}) copy-start(f32[512,8]{0,1:T(8,128)} %param.11) | copy-start | bytes 49156
  23.2 2.1 %copy-start.5 = (f32[512,8]{0,1:T(8,128)S(1)}, f32[512,8]{0,1:T(8,128)}, u32[]{:S(2)}) copy-start(f32[512,8]{0,1:T(8,128)} %param.12) | copy-start | bytes 49156
  23.2 2.5 %copy-start.6 = (f32[512]{0:T(512)S(1)}, f32[512]{0:T(512)}, u32[]{:S(2)}) copy-start(f32[512]{0:T(512)} %param.13) | copy-start | bytes 6148
  25.0 2.5 %copy-start = (f32[1,1,512,1024]{3,2,1,0:T(8,128)S(1)}, f32[1,1,512,1024]{3,2,1,0:T(8,128)}, u32[]{:S(2)}) copy-start(f32[1,1,512,1024]{3,2,1,0:T(8,128)} %copy.178) | copy-start | bytes 6291460
  86.2 22.5 %all-to-all-start.1 = ((f32[128,4,2,128]{3,2,1,0:T(2,128)}), f32[128,4,2,128]{3,2,1,0:T(2,128)S(1)}, u32[]{:S(2)}, u32[]{:S(2)}) async-start(f32[128,4,2,128]{3,2,1,0:T(2,128)} %copy.187), calls=%async_computation.1 | async-start | bytes 1048576 | tf_op jit(solution)/shard_map/all_to_all | solution.py:147

commit v8 on v7

--- a/solution.py
+++ b/solution.py
@@ -113,9 +113,9 @@
     o_im = jnp.sum(g_re * y_im + g_im * y_re, axis=2)
     o_re = jnp.swapaxes(o_re, 1, 2).reshape(own * n_s, LANES)
     o_im = jnp.swapaxes(o_im, 1, 2).reshape(own * n_s, LANES)
-    parts = jnp.stack([scale * o_re, scale * o_im], axis=1)
-    parts = parts.reshape(own, n_dev, 4, 2, LANES)
-    return jnp.swapaxes(parts, 0, 1).reshape(n_dev, own * 4, 2, LANES)
+    parts = jnp.concatenate([scale * o_re, scale * o_im], axis=1)
+    parts = parts.reshape(own, n_dev, 4 * 2 * LANES)
+    return jnp.swapaxes(parts, 0, 1).reshape(n_dev, own * 4 * 2 * LANES)
 
 
 def gather_parts(recv, blk_plane, me, own, n_slab, n_img):

time: 111 us -> 111 us (level)
  waiting for transfers between devices: 40 us -> 38.8 us
    all_to_all x1, waiting for transfers between devices: 26.5 us -> 25.3 us  [on_device(): lax.all_to_all(volume, 'slab', split_axis=0, concat_axis=1, tiled=True)]
    all_to_all x1, local copies, waits for them, and re-layouts: 0.14 us -> 1.32 us  [on_device(): lax.all_to_all(parts, ('slab', 'img'), split_axis=0, concat_axis=0, tiled...]
  transfers between devices with their start and end apart: 2 -> 2, of which waited for: 2 -> 2; matrix products, arithmetic and copies ran while one was open for 22% -> 23% of each run, Pallas kernels for 0% -> 0%
where the time goes in v8:
time: 111 us
  waiting for transfers between devices  38.8 us (35%)
  local copies, waits for them, and re-layouts  21.6 us (19%)
  starting transfers between devices  17.5 us (16%)
  matrix products  17.5 us (16%)
  other arithmetic  15.2 us (14%)
    all_to_all x1, waiting for transfers between devices, on_device(): lax.all_to_all(volume, 'slab', split_axis=0, concat_axis=1, tiled=True)  25.3 us
    all_to_all x1, waiting for transfers between devices, on_device(): lax.all_to_all(parts, ('slab', 'img'), split_axis=0, concat_axis=0, tiled...  13.5 us
    dot_general x1, matrix products, send_parts(): r_t = jnp.einsum('trc,tpsr->tpcs', piece, w_all, precision=MID)  11.1 us
    all_to_all x1, starting transfers between devices, on_device(): lax.all_to_all(volume, 'slab', split_axis=0, concat_axis=1, tiled=True)  8.78 us
    all_to_all x1, starting transfers between devices, on_device(): lax.all_to_all(parts, ('slab', 'img'), split_axis=0, concat_axis=0, tiled...  8.76 us
    dot_general x1, matrix products, send_parts(): y_j = jnp.einsum('qkpn,tpnjs->tqkjs', w_j, r5, precision=MID)  6.38 us
    sub x2, local copies, waits for them, and re-layouts, row_roots(): a_re[:, :, None] * b_re[:, None, :] - a_im[:, :, None] * b_im[:, None, :]  5.86 us
    mul x1, other arithmetic, send_parts(): w_re = ((1.0 - frac_y) * lo_re + frac_y * hi_re) * norm  5.49 us
  transfers between devices with their start and end apart: 2, of which 2 were waited for; matrix products, arithmetic and copies ran while one was open for 23% of the time, Pallas kernels for 0%

profile of v8, /device:TPU:1, one launch (start us, length us, event | category | flops | bytes accessed | tf_op | source)
XLA Modules:
  0.0 111.0 jit_solution(15267744913054939678)
XLA Ops:
  0.0 8.8 %all-to-all-start = ((f32[32,32,1024]{2,1,0:T(8,128)}), f32[32,32,1024]{2,1,0:T(8,128)}, u32[]{:S(2)}, u32[]{:S(2)}) async-start(f32[32,32,1024]{2,1,0:T(8,128)} %param.7), calls=%async_computation | async-start | bytes 8388608 | tf_op jit(solution)/shard_map/all_to_all | solution.py:142
  8.8 0.1 copy.64
  9.0 0.1 eq.87
  9.2 0.1 copy.72
  9.3 0.1 broadcast_in_dim.129
  9.5 0.1 copy.75
  9.6 0.1 broadcast_in_dim.132
  9.8 0.2 convert_reduce_fusion
  10.2 0.2 copy.77
  10.3 0.2 reshape.1306
  10.5 1.1 fusion.51
  11.6 1.9 %multiply_subtract_fusion.1 = (f32[512,32,32]{0,2,1:T(8,128)}, f32[512,32,32]{0,2,1:T(8,128)S(1)}) fusion(f32[512,32]{0,1:T(8,128)S(1)} %get-tuple-element.30, f32[512,32]{0,1:T(8,128)S(1)} %get-tuple-element.25, f32[512,32]{0,1:T(8,128)S(1)} %get-tuple-element.31, f32[512,32]{0,1:T(8,128)S(1)} %get-tuple-element.24), kind=kLoop, calls=%fused_computation.20 | loop fusion | flops 3145728 | bytes 4456448 | tf_op jit(solution)/shard_map/sub | solution.py:75
  13.6 2.9 %copy.83 = f32[1,1,512,1024]{3,2,1,0:T(8,128)} copy(f32[1,1,512,1024]{2,3,1,0:T(8,128)} %bitcast.95) | data formatting | bytes 4194304 | tf_op jit(solution)/shard_map/sub | solution.py:75
  16.5 1.9 %copy.85 = f32[1,1,512,1024]{3,2,1,0:T(8,128)} copy(f32[1,1,512,1024]{2,3,1,0:T(8,128)S(1)} %bitcast.93) | data formatting | bytes 4194304 | tf_op jit(solution)/shard_map/add | solution.py:76
  18.3 1.9 %multiply_subtract_fusion = (f32[512,32,32]{0,2,1:T(8,128)}, f32[512,32,32]{0,2,1:T(8,128)S(1)}) fusion(f32[512,32]{0,1:T(8,128)S(1)} %get-tuple-element.35, f32[512,32]{0,1:T(8,128)S(1)} %get-tuple-element.36, f32[512,32]{0,1:T(8,128)S(1)} %get-tuple-element.34, f32[512,32]{0,1:T(8,128)S(1)} %get-tuple-element.37), kind=kLoop, calls=%fused_computation.19 | loop fusion | flops 3145728 | bytes 4456448 | tf_op jit(solution)/shard_map/sub | solution.py:75
  20.3 3.0 %copy.84 = f32[1,1,512,1024]{3,2,1,0:T(8,128)} copy(f32[1,1,512,1024]{2,3,1,0:T(8,128)} %bitcast.96) | data formatting | bytes 4194304 | tf_op jit(solution)/shard_map/sub | solution.py:75
  23.2 1.8 %copy.86 = f32[1,1,512,1024]{3,2,1,0:T(8,128)} copy(f32[1,1,512,1024]{2,3,1,0:T(8,128)S(1)} %bitcast.94) | data formatting | bytes 4194304 | tf_op jit(solution)/shard_map/add | solution.py:76
  25.0 0.1 copy.69
  25.2 0.1 broadcast_in_dim.125
  25.3 0.1 copy.80
  25.7 0.1 broadcast_in_dim.134
  25.9 0.2 copy.82
  26.1 0.2 broadcast_in_dim_reshape.5
  26.3 0.2 copy.74
  26.5 0.2 broadcast_in_dim_reshape.4
  26.7 0.2 copy.71
  26.8 0.2 reshape.1305
  27.0 0.2 copy.68
  27.2 0.2 reshape.1304
  27.4 0.1 eq.99
  27.6 0.2 copy.79
  27.8 0.2 mul.794
  28.0 0.3 fusion.52
  28.3 0.3 negate_multiply_fusion
  28.7 5.5 %add_multiply_fusion.1 = (f32[1,1,512,1024]{3,2,1,0:T(8,128)}, f32[1,1,512,1024]{3,2,1,0:T(8,128)}) fusion(f32[1,1,512,1024]{3,2,1,0:T(8,128)} %copy.84, f32[1,1,512,1024]{3,2,1,0:T(8,128)S(1)} %copy-done, f32[512]{0:T(512)S(1)} %broadcast_in_dim_reshape.5, f32[512]{0:T(512)S(1)} %broadcast_subtract_fusion, f32[1,1,512,1024]{3,2,1,0:T(8,128)} %copy.86, ...), kind=kLoop, calls=%fused_computation.18 | loop fusion | flops 4194304 | bytes 12587008 | tf_op jit(solution)/shard_map/mul | solution.py:82
  34.2 25.3 %all-to-all-done = f32[32,32,1024]{2,1,0:T(8,128)} async-done(((f32[32,32,1024]{2,1,0:T(8,128)}), f32[32,32,1024]{2,1,0:T(8,128)}, u32[]{:S(2)}, u32[]{:S(2)}) %all-to-all-start) | async-done | bytes 4194336 | tf_op jit(solution)/shard_map/all_to_all | solution.py:142
  59.5 11.1 %fusion.8 = f32[1,2,1024,512]{2,3,1,0:T(8,128)} fusion(f32[1024,1024,1]{1,0,2:T(8,128)} %bitcast.7, f32[1,1,512,1024]{3,2,1,0:T(8,128)} %get-tuple-element.23, f32[1,1,512,1024]{3,2,1,0:T(8,128)} %get-tuple-element.22), kind=kOutput, calls=%fused_computation.9 | convolution fusion | flops 6443499520 | bytes 12582912 | tf_op jit(solution)/shard_map/trc,tpsr->tpcs/dot_general | solution.py:95
  70.6 5.4 %copy.87 = f32[1,2,1024,512]{3,2,1,0:T(8,128)} copy(f32[1,2,1024,512]{2,3,1,0:T(8,128)} %fusion.8) | data formatting | bytes 8388608 | tf_op jit(solution)/shard_map/trc,tpsr->tpcs/transpose | solution.py:95
  76.0 6.4 %fusion.5 = f32[1,2,128,8,512]{2,4,1,3,0:T(8,128)S(1)} fusion(f32[2,128,8,512,1]{3,2,1,0,4:T(8,128)} %bitcast.92, f32[1,128,2,128]{3,1,2,0:T(8,128)S(1)} %get-tuple-element.19, f32[1,128,2,128]{3,1,2,0:T(8,128)S(1)} %get-tuple-element.18), kind=kOutput, calls=%fused_computation.8 | convolution fusion | flops 1610678272 | bytes 8650752 | tf_op jit(solution)/shard_map/qkpn,tpnjs->tqkjs/dot_general | solution.py:98
  82.4 1.4 %subtract_reduce_fusion = (f32[128,512]{0,1:T(8,128)S(1)}, f32[128,512]{0,1:T(8,128)S(1)}) fusion(f32[1,2,128,8,512]{2,4,1,3,0:T(8,128)S(1)} %fusion.5, f32[128,8]{0,1:T(8,128)S(1)} %get-tuple-element.42, f32[8,512]{1,0:T(8,128)S(1)} %get-tuple-element.29, f32[128,8]{0,1:T(8,128)S(1)} %get-tuple-element.43, f32[8,512]{1,0:T(8,128)S(1)} %get-tuple-element.28), kind=kLoop, calls=%fused_computation.13 | loop fusion | flops 7208960 | bytes 4759552 | tf_op jit(solution)/shard_map/reduce_sum | solution.py:112
  83.8 1.4 %bitcast_multiply_fusion.1 = (f32[512,128]{1,0:T(8,128)S(1)}, f32[512,128]{1,0:T(8,128)S(1)}) fusion(f32[128,512]{0,1:T(8,128)S(1)} %get-tuple-element.5, f32[512]{0:T(512)S(1)} %mul.794, f32[512]{0:T(512)S(1)} %fusion.68, s32[512]{0:T(512)S(1)} %broadcast_multiply_fusion.1, f32[512]{0:T(512)S(1)} %fusion.66, f32[128,512]{0,1:T(8,128)S(1)} %get-tuple-element.6), kind=kLoop, calls=%fused_computation.37 | loop fusion | flops 786432 | bytes 1056768 | tf_op jit(solution)/shard_map/mul | solution.py:116
  85.3 1.3 %all_to_all.14 = f32[128,1,1024]{2,1,0:T(1,128)} reshape(f32[512,256]{1,0:T(8,128)S(1)} %pad_maximum_fusion) | data formatting | bytes 1048576 | tf_op jit(solution)/shard_map/all_to_all | solution.py:147
  86.6 8.8 %all-to-all-start.1 = ((f32[128,1,1024]{2,1,0:T(1,128)}), f32[128,1,1024]{2,1,0:T(1,128)S(1)}, u32[]{:S(2)}, u32[]{:S(2)}) async-start(f32[128,1,1024]{2,1,0:T(1,128)} %all_to_all.14), calls=%async_computation.1 | async-start | bytes 1048576 | tf_op jit(solution)/shard_map/all_to_all | solution.py:147
  95.4 0.2 dynamic-slice_reduce_fusion
  95.6 13.5 %all-to-all-done.1 = f32[128,1,1024]{2,1,0:T(1,128)S(1)} async-done(((f32[128,1,1024]{2,1,0:T(1,128)}), f32[128,1,1024]{2,1,0:T(1,128)S(1)}, u32[]{:S(2)}, u32[]{:S(2)}) %all-to-all-start.1) | async-done | bytes 524320 | tf_op jit(solution)/shard_map/all_to_all | solution.py:147
  109.2 0.6 gather_fusion.1
  109.8 0.6 gather_fusion
  110.4 0.6 add.427
  (42 shorter events, 1.0 us)
Async XLA Ops:
  0.0 8.8 %copy-start.1 = (s32[512,8]{0,1:T(8,128)S(1)}, s32[512,8]{0,1:T(8,128)}, u32[]{:S(2)}) copy-start(s32[512,8]{0,1:T(8,128)} %param.8) | copy-start | bytes 49156
  0.0 9.2 %copy-start.2 = (s32[512,8]{0,1:T(8,128)S(1)}, s32[512,8]{0,1:T(8,128)}, u32[]{:S(2)}) copy-start(s32[512,8]{0,1:T(8,128)} %param.10) | copy-start | bytes 49156
  0.0 9.5 %copy-start.3 = (s32[512,8]{0,1:T(8,128)S(1)}, s32[512,8]{0,1:T(8,128)}, u32[]{:S(2)}) copy-start(s32[512,8]{0,1:T(8,128)} %param.9) | copy-start | bytes 49156
  0.0 59.5 %all-to-all-start = ((f32[32,32,1024]{2,1,0:T(8,128)}), f32[32,32,1024]{2,1,0:T(8,128)}, u32[]{:S(2)}, u32[]{:S(2)}) async-start(f32[32,32,1024]{2,1,0:T(8,128)} %param.7), calls=%async_computation | async-start | bytes 8388608 | tf_op jit(solution)/shard_map/all_to_all | solution.py:142
  23.2 1.8 %copy-start.4 = (f32[512,8]{0,1:T(8,128)S(1)}, f32[512,8]{0,1:T(8,128)}, u32[]{:S(2)}) copy-start(f32[512,8]{0,1:T(8,128)} %param.11) | copy-start | bytes 49156
  23.2 2.1 %copy-start.5 = (f32[512,8]{0,1:T(8,128)S(1)}, f32[512,8]{0,1:T(8,128)}, u32[]{:S(2)}) copy-start(f32[512,8]{0,1:T(8,128)} %param.12) | copy-start | bytes 49156
  23.2 2.5 %copy-start.6 = (f32[512]{0:T(512)S(1)}, f32[512]{0:T(512)}, u32[]{:S(2)}) copy-start(f32[512]{0:T(512)} %param.13) | copy-start | bytes 6148
  25.0 3.7 %copy-start = (f32[1,1,512,1024]{3,2,1,0:T(8,128)S(1)}, f32[1,1,512,1024]{3,2,1,0:T(8,128)}, u32[]{:S(2)}) copy-start(f32[1,1,512,1024]{3,2,1,0:T(8,128)} %copy.83) | copy-start | bytes 6291460
  86.6 22.5 %all-to-all-start.1 = ((f32[128,1,1024]{2,1,0:T(1,128)}), f32[128,1,1024]{2,1,0:T(1,128)S(1)}, u32[]{:S(2)}, u32[]{:S(2)}) async-start(f32[128,1,1024]{2,1,0:T(1,128)} %all_to_all.14), calls=%async_computation.1 | async-start | bytes 1048576 | tf_op jit(solution)/shard_map/all_to_all | solution.py:147

commit v9 on v7

--- a/solution.py
+++ b/solution.py
@@ -4,6 +4,7 @@
 import jax.numpy as jnp
 from jax import lax
 from jax.sharding import PartitionSpec as P
+from jax.experimental.layout import Layout, with_layout_constraint
 
 LANES = 128
 SPLIT = 8
@@ -93,6 +94,7 @@
     y = None
     for j, piece in enumerate(planes):
         r_t = jnp.einsum("trc,tpsr->tpcs", piece, w_all, precision=MID)
+        r_t = with_layout_constraint(r_t, Layout(major_to_minor=(0, 1, 2, 3)))
         r5 = r_t.reshape(own, 2, step_n2, SPLIT, n_s)
         w_j = w_col[:, :, :, j * step_n2:(j + 1) * step_n2]
         y_j = jnp.einsum("qkpn,tpnjs->tqkjs", w_j, r5, precision=MID)

time: 111 us -> 104 us (0.937)
  local copies, waits for them, and re-layouts: 20.9 us -> 15.5 us
  matrix products: 17.5 us -> 15.1 us
    transpose x1 -> x0, local copies, waits for them, and re-layouts: 5.41 us -> none  [send_parts(): r_t = jnp.einsum('trc,tpsr->tpcs', piece, w_all, precision=MID)]
    dot_general x1, matrix products: 6.38 us -> 5.14 us  [send_parts(): y_j = jnp.einsum('qkpn,tpnjs->tqkjs', w_j, r5, precision=MID)]
    dot_general x1, matrix products: 11.1 us -> 9.97 us  [send_parts(): r_t = jnp.einsum('trc,tpsr->tpcs', piece, w_all, precision=MID)]
  transfers between devices with their start and end apart: 2 -> 2, of which waited for: 2 -> 2; matrix products, arithmetic and copies ran while one was open for 22% -> 23% of each run, Pallas kernels for 0% -> 0%
where the time goes in v9:
time: 104 us; the launch traced here: 103 us
  waiting for transfers between devices  40 us (38%)
  starting transfers between devices  17.5 us (17%)
  local copies, waits for them, and re-layouts  15.5 us (15%)
  matrix products  15.1 us (15%)
  other arithmetic  14.8 us (14%)
    all_to_all x1, waiting for transfers between devices, on_device(): lax.all_to_all(volume, 'slab', split_axis=0, concat_axis=1, tiled=True)  26.5 us
    all_to_all x1, waiting for transfers between devices, on_device(): lax.all_to_all(parts, ('slab', 'img'), split_axis=0, concat_axis=0, tiled...  13.5 us
    dot_general x1, matrix products, send_parts(): r_t = jnp.einsum('trc,tpsr->tpcs', piece, w_all, precision=MID)  9.97 us
    all_to_all x1, starting transfers between devices, on_device(): lax.all_to_all(volume, 'slab', split_axis=0, concat_axis=1, tiled=True)  8.78 us
    all_to_all x1, starting transfers between devices, on_device(): lax.all_to_all(parts, ('slab', 'img'), split_axis=0, concat_axis=0, tiled...  8.76 us
    sub x2, local copies, waits for them, and re-layouts, row_roots(): a_re[:, :, None] * b_re[:, None, :] - a_im[:, :, None] * b_im[:, None, :]  5.86 us
    mul x1, other arithmetic, send_parts(): w_re = ((1.0 - frac_y) * lo_re + frac_y * hi_re) * norm  5.49 us
    dot_general x1, matrix products, send_parts(): y_j = jnp.einsum('qkpn,tpnjs->tqkjs', w_j, r5, precision=MID)  5.14 us
  transfers between devices with their start and end apart: 2, of which 2 were waited for; matrix products, arithmetic and copies ran while one was open for 23% of the time, Pallas kernels for 0%

profile of v9, /device:TPU:1, one launch (start us, length us, event | category | flops | bytes accessed | tf_op | source)
XLA Modules:
  0.0 103.3 jit_solution(10722848011177306512)
XLA Ops:
  0.0 8.8 %all-to-all-start = ((f32[32,32,1024]{2,1,0:T(8,128)}), f32[32,32,1024]{2,1,0:T(8,128)}, u32[]{:S(2)}, u32[]{:S(2)}) async-start(f32[32,32,1024]{2,1,0:T(8,128)} %param.7), calls=%async_computation | async-start | bytes 8388608 | tf_op jit(solution)/shard_map/all_to_all | solution.py:144
  8.8 0.1 copy.163
  9.0 0.1 eq.87
  9.1 0.1 copy.164
  9.2 0.1 copy.169
  9.3 0.1 broadcast_in_dim.129
  9.5 0.1 copy.171
  9.6 0.1 broadcast_in_dim.132
  9.8 0.2 convert_reduce_fusion
  10.1 0.1 iota_compare_fusion
  10.2 0.2 copy.178
  10.3 0.2 mul.880
  10.5 1.1 %fusion.51 = (f32[512,32]{0,1:T(8,128)S(1)}, f32[512,32]{0,1:T(8,128)S(1)}, f32[512,32]{0,1:T(8,128)S(1)}, f32[512,32]{0,1:T(8,128)S(1)}, f32[512,32]{0,1:T(8,12...) fusion(s32[32]{0:T(128)S(1)} %iota_multiply_fusion, s32[512]{0:T(512)S(1)} %mul.880, ...), kind=kLoop, calls=%fused_computation.103 | loop fusion | flops 983040 | bytes 528512 | tf_op jit(solution)/shard_map/cos | solution.py:21
  11.6 1.9 %multiply_subtract_fusion.1 = (f32[512,32,32]{0,2,1:T(8,128)}, f32[512,32,32]{0,2,1:T(8,128)S(1)}) fusion(f32[512,32]{0,1:T(8,128)S(1)} %get-tuple-element.30, f32[512,32]{0,1:T(8,128)S(1)} %get-tuple-element.25, f32[512,32]{0,1:T(8,128)S(1)} %get-tuple-element.31, f32[512,32]{0,1:T(8,128)S(1)} %get-tuple-element.24), kind=kLoop, calls=%fused_computation.20 | loop fusion | flops 3145728 | bytes 4456448 | tf_op jit(solution)/shard_map/sub | solution.py:76
  13.6 2.9 %copy.179 = f32[1,1,512,1024]{3,2,1,0:T(8,128)} copy(f32[1,1,512,1024]{2,3,1,0:T(8,128)} %bitcast.101) | data formatting | bytes 4194304 | tf_op jit(solution)/shard_map/sub | solution.py:76
  16.5 1.9 %copy.181 = f32[1,1,512,1024]{3,2,1,0:T(8,128)} copy(f32[1,1,512,1024]{2,3,1,0:T(8,128)S(1)} %bitcast.99) | data formatting | bytes 4194304 | tf_op jit(solution)/shard_map/add | solution.py:77
  18.3 1.9 %multiply_subtract_fusion = (f32[512,32,32]{0,2,1:T(8,128)}, f32[512,32,32]{0,2,1:T(8,128)S(1)}) fusion(f32[512,32]{0,1:T(8,128)S(1)} %get-tuple-element.35, f32[512,32]{0,1:T(8,128)S(1)} %get-tuple-element.36, f32[512,32]{0,1:T(8,128)S(1)} %get-tuple-element.34, f32[512,32]{0,1:T(8,128)S(1)} %get-tuple-element.37), kind=kLoop, calls=%fused_computation.19 | loop fusion | flops 3145728 | bytes 4456448 | tf_op jit(solution)/shard_map/sub | solution.py:76
  20.3 3.0 %copy.180 = f32[1,1,512,1024]{3,2,1,0:T(8,128)} copy(f32[1,1,512,1024]{2,3,1,0:T(8,128)} %bitcast.102) | data formatting | bytes 4194304 | tf_op jit(solution)/shard_map/sub | solution.py:76
  23.2 1.8 %copy.182 = f32[1,1,512,1024]{3,2,1,0:T(8,128)} copy(f32[1,1,512,1024]{2,3,1,0:T(8,128)S(1)} %bitcast.100) | data formatting | bytes 4194304 | tf_op jit(solution)/shard_map/add | solution.py:77
  25.0 0.1 copy.167
  25.2 0.1 broadcast_in_dim.125
  25.3 0.1 copy.175
  25.5 0.1 broadcast_in_dim.138
  25.7 0.1 broadcast_in_dim.134
  25.8 0.1 copy.173
  25.9 0.1 fusion.34
  25.9 0.2 copy.177
  26.1 0.2 broadcast_in_dim_reshape.2
  26.3 0.2 copy.174
  26.5 0.2 mul.863
  26.8 0.3 fusion.52
  27.0 0.3 negate_multiply_fusion
  27.4 0.1 fusion.59
  27.5 5.5 %add_multiply_fusion.1 = (f32[1,1,512,1024]{3,2,1,0:T(8,128)}, f32[1,1,512,1024]{3,2,1,0:T(8,128)}) fusion(f32[1,1,512,1024]{3,2,1,0:T(8,128)} %copy.180, f32[1,1,512,1024]{3,2,1,0:T(8,128)S(1)} %copy-done, f32[512]{0:T(512)S(1)} %broadcast_in_dim_reshape.2, f32[512]{0:T(512)S(1)} %broadcast_subtract_fusion, f32[1,1,512,1024]{3,2,1,0:T(8,128)} %copy.182, ...), kind=kLoop, calls=%fused_computation.18 | loop fusion | flops 4194304 | bytes 12587008 | tf_op jit(solution)/shard_map/mul | solution.py:83
  33.0 26.5 %all-to-all-done = f32[32,32,1024]{2,1,0:T(8,128)} async-done(((f32[32,32,1024]{2,1,0:T(8,128)}), f32[32,32,1024]{2,1,0:T(8,128)}, u32[]{:S(2)}, u32[]{:S(2)}) %all-to-all-start) | async-done | bytes 4194336 | tf_op jit(solution)/shard_map/all_to_all | solution.py:144
  59.5 10.0 %fusion.8 = f32[2,128,8,512,1]{3,2,1,0,4:T(8,128)S(1)} fusion(f32[1024,1024,1]{1,0,2:T(8,128)} %bitcast.11, f32[1,1,512,1024]{3,2,1,0:T(8,128)} %get-tuple-element.23, f32[1,1,512,1024]{3,2,1,0:T(8,128)} %get-tuple-element.22), kind=kOutput, calls=%fused_computation.9 | convolution fusion | flops 6443499520 | bytes 12582912 | tf_op jit(solution)/shard_map/trc,tpsr->tpcs/dot_general | solution.py:96
  69.5 5.1 %fusion.5 = f32[1,2,128,8,512]{2,4,1,3,0:T(8,128)S(1)} fusion(f32[2,128,8,512,1]{3,2,1,0,4:T(8,128)S(1)} %fusion.8, f32[1,128,2,128]{3,1,2,0:T(8,128)S(1)} %get-tuple-element.19, f32[1,128,2,128]{3,1,2,0:T(8,128)S(1)} %get-tuple-element.18), kind=kOutput, calls=%fused_computation.8 | convolution fusion | flops 1610678272 | bytes 8650752 | tf_op jit(solution)/shard_map/qkpn,tpnjs->tqkjs/dot_general | solution.py:100
  74.6 1.4 %subtract_reduce_fusion = (f32[128,512]{0,1:T(8,128)S(1)}, f32[128,512]{0,1:T(8,128)S(1)}) fusion(f32[1,2,128,8,512]{2,4,1,3,0:T(8,128)S(1)} %fusion.5, f32[128,8]{0,1:T(8,128)S(1)} %get-tuple-element.42, f32[8,512]{1,0:T(8,128)S(1)} %get-tuple-element.29, f32[128,8]{0,1:T(8,128)S(1)} %get-tuple-element.43, f32[8,512]{1,0:T(8,128)S(1)} %get-tuple-element.28), kind=kLoop, calls=%fused_computation.13 | loop fusion | flops 7208960 | bytes 4759552 | tf_op jit(solution)/shard_map/reduce_sum | solution.py:114
  76.1 1.1 %copy_multiply_fusion.1 = (f32[128,4,1,128]{3,0,2,1:T(8,128)S(1)}, f32[128,4,1,128]{3,0,2,1:T(8,128)S(1)}) fusion(f32[128,4,1,128]{3,1,0,2:T(4,128)S(1)} %bitcast.104, f32[128,4]{0,1:T(4,128)S(1)} %bitcast.108, f32[128,4]{0,1:T(4,128)S(1)} %fusion.68, s32[128,4]{0,1:T(4,128)S(1)} %bitcast.107, f32[128,4]{0,1:T(4,128)S(1)} %fusion.66, ...), kind=kLoop, calls=%fused_computation.37 | loop fusion | flops 786432 | bytes 1056768 | tf_op jit(solution)/shard_map/mul | solution.py:118
  77.2 1.2 %copy.188 = f32[128,4,2,128]{3,2,1,0:T(2,128)} copy(f32[128,4,2,128]{3,0,2,1:T(8,128)S(1)} %pad_maximum_fusion) | data formatting | bytes 1048576 | tf_op jit(solution)/shard_map/stack | solution.py:118
  78.4 8.8 %all-to-all-start.1 = ((f32[128,4,2,128]{3,2,1,0:T(2,128)}), f32[128,4,2,128]{3,2,1,0:T(2,128)S(1)}, u32[]{:S(2)}, u32[]{:S(2)}) async-start(f32[128,4,2,128]{3,2,1,0:T(2,128)} %copy.188), calls=%async_computation.1 | async-start | bytes 1048576 | tf_op jit(solution)/shard_map/all_to_all | solution.py:149
  87.1 0.2 dynamic-slice_reduce_fusion
  87.4 13.5 %all-to-all-done.1 = f32[128,4,2,128]{3,2,1,0:T(2,128)S(1)} async-done(((f32[128,4,2,128]{3,2,1,0:T(2,128)}), f32[128,4,2,128]{3,2,1,0:T(2,128)S(1)}, u32[]{:S(2)}, u32[]{:S(2)}) %all-to-all-start.1) | async-done | bytes 524320 | tf_op jit(solution)/shard_map/all_to_all | solution.py:149
  100.9 0.1 copy.189
  101.0 0.4 copy.190
  101.5 0.6 gather_fusion.1
  102.1 0.6 gather_fusion
  102.7 0.6 add.466
  (38 shorter events, 0.5 us)
Async XLA Ops:
  0.0 8.8 %copy-start.1 = (s32[512,8]{0,1:T(8,128)S(1)}, s32[512,8]{0,1:T(8,128)}, u32[]{:S(2)}) copy-start(s32[512,8]{0,1:T(8,128)} %param.8) | copy-start | bytes 49156
  0.0 9.2 %copy-start.2 = (s32[512,8]{0,1:T(8,128)S(1)}, s32[512,8]{0,1:T(8,128)}, u32[]{:S(2)}) copy-start(s32[512,8]{0,1:T(8,128)} %param.10) | copy-start | bytes 49156
  0.0 9.5 %copy-start.3 = (s32[512,8]{0,1:T(8,128)S(1)}, s32[512,8]{0,1:T(8,128)}, u32[]{:S(2)}) copy-start(s32[512,8]{0,1:T(8,128)} %param.9) | copy-start | bytes 49156
  0.0 59.5 %all-to-all-start = ((f32[32,32,1024]{2,1,0:T(8,128)}), f32[32,32,1024]{2,1,0:T(8,128)}, u32[]{:S(2)}, u32[]{:S(2)}) async-start(f32[32,32,1024]{2,1,0:T(8,128)} %param.7), calls=%async_computation | async-start | bytes 8388608 | tf_op jit(solution)/shard_map/all_to_all | solution.py:144
  23.2 1.8 %copy-start.4 = (f32[512,8]{0,1:T(8,128)S(1)}, f32[512,8]{0,1:T(8,128)}, u32[]{:S(2)}) copy-start(f32[512,8]{0,1:T(8,128)} %param.11) | copy-start | bytes 49156
  23.2 2.1 %copy-start.5 = (f32[512,8]{0,1:T(8,128)S(1)}, f32[512,8]{0,1:T(8,128)}, u32[]{:S(2)}) copy-start(f32[512,8]{0,1:T(8,128)} %param.12) | copy-start | bytes 49156
  23.2 2.5 %copy-start.6 = (f32[512]{0:T(512)S(1)}, f32[512]{0:T(512)}, u32[]{:S(2)}) copy-start(f32[512]{0:T(512)} %param.13) | copy-start | bytes 6148
  25.0 2.5 %copy-start = (f32[1,1,512,1024]{3,2,1,0:T(8,128)S(1)}, f32[1,1,512,1024]{3,2,1,0:T(8,128)}, u32[]{:S(2)}) copy-start(f32[1,1,512,1024]{3,2,1,0:T(8,128)} %copy.179) | copy-start | bytes 6291460
  78.4 22.5 %all-to-all-start.1 = ((f32[128,4,2,128]{3,2,1,0:T(2,128)}), f32[128,4,2,128]{3,2,1,0:T(2,128)S(1)}, u32[]{:S(2)}, u32[]{:S(2)}) async-start(f32[128,4,2,128]{3,2,1,0:T(2,128)} %copy.188), calls=%async_computation.1 | async-start | bytes 1048576 | tf_op jit(solution)/shard_map/all_to_all | solution.py:149

commit v10 on v9

--- a/solution.py
+++ b/solution.py
@@ -117,7 +117,8 @@
     o_im = jnp.swapaxes(o_im, 1, 2).reshape(own * n_s, LANES)
     parts = jnp.stack([scale * o_re, scale * o_im], axis=1)
     parts = parts.reshape(own, n_dev, 4, 2, LANES)
-    return jnp.swapaxes(parts, 0, 1).reshape(n_dev, own * 4, 2, LANES)
+    parts = jnp.swapaxes(parts, 0, 1).reshape(n_dev, own * 4, 2, LANES)
+    return with_layout_constraint(parts, Layout(major_to_minor=(0, 1, 2, 3)))
 
 
 def gather_parts(recv, blk_plane, me, own, n_slab, n_img):

time: 104 us -> 111 us (1.067)
  other arithmetic: 14.8 us -> 24 us
  local copies, waits for them, and re-layouts: 15.5 us -> 14.1 us
    mul x1 -> x2, other arithmetic: 1.07 us -> 8.83 us  [send_parts(): parts = jnp.stack([scale * o_re, scale * o_im], axis=1)]
    another operation x1, other arithmetic: 0.04 us -> 1.26 us  [send_parts(): parts = jnp.stack([scale * o_re, scale * o_im], axis=1)]
    another operation x1 -> x0, local copies, waits for them, and re-layouts: 1.19 us -> none  [send_parts(): parts = jnp.stack([scale * o_re, scale * o_im], axis=1)]
  transfers between devices with their start and end apart: 2 -> 2, of which waited for: 2 -> 2; matrix products, arithmetic and copies ran while one was open for 23% -> 22% of each run, Pallas kernels for 0% -> 0%
where the time goes in v10:
time: 111 us
  waiting for transfers between devices  39.5 us (36%)
  other arithmetic  24 us (22%)
  starting transfers between devices  17.5 us (16%)
  matrix products  15.1 us (14%)
  local copies, waits for them, and re-layouts  14.1 us (13%)
    all_to_all x1, waiting for transfers between devices, on_device(): lax.all_to_all(volume, 'slab', split_axis=0, concat_axis=1, tiled=True)  26 us
    all_to_all x1, waiting for transfers between devices, on_device(): lax.all_to_all(parts, ('slab', 'img'), split_axis=0, concat_axis=0, tiled...  13.5 us
    dot_general x1, matrix products, send_parts(): r_t = jnp.einsum('trc,tpsr->tpcs', piece, w_all, precision=MID)  9.97 us
    mul x2, other arithmetic, send_parts(): parts = jnp.stack([scale * o_re, scale * o_im], axis=1)  8.83 us
    all_to_all x1, starting transfers between devices, on_device(): lax.all_to_all(volume, 'slab', split_axis=0, concat_axis=1, tiled=True)  8.78 us
    all_to_all x1, starting transfers between devices, on_device(): lax.all_to_all(parts, ('slab', 'img'), split_axis=0, concat_axis=0, tiled...  8.76 us
    sub x2, local copies, waits for them, and re-layouts, row_roots(): a_re[:, :, None] * b_re[:, None, :] - a_im[:, :, None] * b_im[:, None, :]  5.86 us
    mul x1, other arithmetic, send_parts(): w_re = ((1.0 - frac_y) * lo_re + frac_y * hi_re) * norm  5.49 us
  transfers between devices with their start and end apart: 2, of which 2 were waited for; matrix products, arithmetic and copies ran while one was open for 22% of the time, Pallas kernels for 0%

profile of v10, /device:TPU:1, one launch (start us, length us, event | category | flops | bytes accessed | tf_op | source)
XLA Modules:
  0.0 110.5 jit_solution(2138929098733313145)
XLA Ops:
  0.0 8.8 %all-to-all-start = ((f32[32,32,1024]{2,1,0:T(8,128)}), f32[32,32,1024]{2,1,0:T(8,128)}, u32[]{:S(2)}, u32[]{:S(2)}) async-start(f32[32,32,1024]{2,1,0:T(8,128)} %param.7), calls=%async_computation | async-start | bytes 8388608 | tf_op jit(solution)/shard_map/all_to_all | solution.py:145
  8.9 0.1 copy.85
  9.0 0.1 eq.87
  9.2 0.1 copy.92
  9.3 0.1 broadcast_in_dim.129
  9.5 0.1 copy.97
  9.7 0.1 broadcast_in_dim.132
  9.8 0.2 convert_reduce_fusion
  10.1 0.1 iota_compare_fusion
  10.2 0.2 copy.106
  10.4 0.2 mul.880
  10.6 1.1 fusion.45
  11.6 2.0 %multiply_subtract_fusion.1 = (f32[512,32,32]{0,2,1:T(8,128)}, f32[512,32,32]{0,2,1:T(8,128)S(1)}) fusion(f32[512,32]{0,1:T(8,128)S(1)} %get-tuple-element.32, f32[512,32]{0,1:T(8,128)S(1)} %get-tuple-element.25, f32[512,32]{0,1:T(8,128)S(1)} %get-tuple-element.33, f32[512,32]{0,1:T(8,128)S(1)} %get-tuple-element.24), kind=kLoop, calls=%fused_computation.20 | loop fusion | flops 3145728 | bytes 4456448 | tf_op jit(solution)/shard_map/sub | solution.py:76
  13.6 2.9 %copy.107 = f32[1,1,512,1024]{3,2,1,0:T(8,128)} copy(f32[1,1,512,1024]{2,3,1,0:T(8,128)} %bitcast.101) | data formatting | bytes 4194304 | tf_op jit(solution)/shard_map/sub | solution.py:76
  16.5 1.9 %copy.109 = f32[1,1,512,1024]{3,2,1,0:T(8,128)} copy(f32[1,1,512,1024]{2,3,1,0:T(8,128)S(1)} %bitcast.99) | data formatting | bytes 4194304 | tf_op jit(solution)/shard_map/add | solution.py:77
  18.4 1.9 %multiply_subtract_fusion = (f32[512,32,32]{0,2,1:T(8,128)}, f32[512,32,32]{0,2,1:T(8,128)S(1)}) fusion(f32[512,32]{0,1:T(8,128)S(1)} %get-tuple-element.37, f32[512,32]{0,1:T(8,128)S(1)} %get-tuple-element.38, f32[512,32]{0,1:T(8,128)S(1)} %get-tuple-element.36, f32[512,32]{0,1:T(8,128)S(1)} %get-tuple-element.39), kind=kLoop, calls=%fused_computation.19 | loop fusion | flops 3145728 | bytes 4456448 | tf_op jit(solution)/shard_map/sub | solution.py:76
  20.3 3.0 %copy.108 = f32[1,1,512,1024]{3,2,1,0:T(8,128)} copy(f32[1,1,512,1024]{2,3,1,0:T(8,128)} %bitcast.102) | data formatting | bytes 4194304 | tf_op jit(solution)/shard_map/sub | solution.py:76
  23.2 1.8 %copy.110 = f32[1,1,512,1024]{3,2,1,0:T(8,128)} copy(f32[1,1,512,1024]{2,3,1,0:T(8,128)S(1)} %bitcast.100) | data formatting | bytes 4194304 | tf_op jit(solution)/shard_map/add | solution.py:77
  25.1 0.1 copy.103
  25.2 0.1 broadcast_in_dim.138
  25.4 0.1 copy.89
  25.5 0.1 broadcast_in_dim.125
  25.7 0.1 broadcast_in_dim.134
  26.0 0.2 copy.105
  26.1 0.2 broadcast_in_dim_reshape.2
  26.3 0.2 copy.102
  26.5 0.2 mul.863
  26.8 0.1 copy.91
  26.9 0.1 copy.101
  27.0 0.1 copy.99
  27.2 0.3 fusion.46
  27.4 0.3 negate_multiply_fusion.1
  27.8 0.1 fusion.53
  27.9 0.1 iota_add_fusion
  28.0 5.5 %add_multiply_fusion.1 = (f32[1,1,512,1024]{3,2,1,0:T(8,128)}, f32[1,1,512,1024]{3,2,1,0:T(8,128)}) fusion(f32[1,1,512,1024]{3,2,1,0:T(8,128)} %copy.108, f32[1,1,512,1024]{3,2,1,0:T(8,128)S(1)} %copy-done, f32[512]{0:T(512)S(1)} %broadcast_in_dim_reshape.2, f32[512]{0:T(512)S(1)} %broadcast_subtract_fusion.1, f32[1,1,512,1024]{3,2,1,0:T(8,128)} %copy.110, ...), kind=kLoop, calls=%fused_computation.18 | loop fusion | flops 4194304 | bytes 12587008 | tf_op jit(solution)/shard_map/mul | solution.py:83
  33.5 26.0 %all-to-all-done = f32[32,32,1024]{2,1,0:T(8,128)} async-done(((f32[32,32,1024]{2,1,0:T(8,128)}), f32[32,32,1024]{2,1,0:T(8,128)}, u32[]{:S(2)}, u32[]{:S(2)}) %all-to-all-start) | async-done | bytes 4194336 | tf_op jit(solution)/shard_map/all_to_all | solution.py:145
  59.5 10.0 %fusion.8 = f32[2,128,8,512,1]{3,2,1,0,4:T(8,128)S(1)} fusion(f32[1024,1024,1]{1,0,2:T(8,128)} %bitcast.11, f32[1,1,512,1024]{3,2,1,0:T(8,128)} %get-tuple-element.23, f32[1,1,512,1024]{3,2,1,0:T(8,128)} %get-tuple-element.22), kind=kOutput, calls=%fused_computation.9 | convolution fusion | flops 6443499520 | bytes 12582912 | tf_op jit(solution)/shard_map/trc,tpsr->tpcs/dot_general | solution.py:96
  69.5 5.1 %fusion.5 = f32[1,2,128,8,512]{2,4,1,3,0:T(8,128)S(1)} fusion(f32[2,128,8,512,1]{3,2,1,0,4:T(8,128)S(1)} %fusion.8, f32[1,128,2,128]{3,1,2,0:T(8,128)S(1)} %get-tuple-element.21, f32[1,128,2,128]{3,1,2,0:T(8,128)S(1)} %get-tuple-element.20), kind=kOutput, calls=%fused_computation.8 | convolution fusion | flops 1610678272 | bytes 8650752 | tf_op jit(solution)/shard_map/qkpn,tpnjs->tqkjs/dot_general | solution.py:100
  74.6 1.4 %subtract_reduce_fusion = (f32[128,512]{0,1:T(8,128)S(1)}, f32[128,512]{0,1:T(8,128)S(1)}) fusion(f32[1,2,128,8,512]{2,4,1,3,0:T(8,128)S(1)} %fusion.5, f32[128,8]{0,1:T(8,128)S(1)} %get-tuple-element.44, f32[8,512]{1,0:T(8,128)S(1)} %get-tuple-element.31, f32[128,8]{0,1:T(8,128)S(1)} %get-tuple-element.45, f32[8,512]{1,0:T(8,128)S(1)} %get-tuple-element.30), kind=kLoop, calls=%fused_computation.13 | loop fusion | flops 7208960 | bytes 4759552 | tf_op jit(solution)/shard_map/reduce_sum | solution.py:114
  76.1 8.6 %fusion.72 = (f32[128,4,1,128]{3,2,1,0:T(1,128)S(1)}, f32[128,4,1,128]{3,2,1,0:T(1,128)S(1)}) fusion(f32[128,4,1,128]{3,2,1,0:T(1,128)S(1)} %bitcast.104, f32[128,4]{1,0:T(8,128)S(1)} %copy.101, f32[128,4]{1,0:T(8,128)S(1)} %copy.99, s32[128,4,1,128]{3,0,2,1:T(8,128)S(1)} %get-tuple-element.29, s32[128,4,1,128]{3,0,2,1:T(8,128)S(1)} %get-tuple-element.28, ...), kind=kLoop, calls=%fused_computation.166 | loop fusion | flops 589824 | bytes 1316864 | tf_op jit(solution)/shard_map/mul | solution.py:118
  84.6 0.3 mul.932
  84.9 1.3 %pad_maximum_fusion = f32[128,4,2,128]{3,2,1,0:T(2,128)} fusion(f32[128,4,1,128]{3,2,1,0:T(1,128)S(1)} %mul.932, f32[128,4,1,128]{3,2,1,0:T(1,128)S(1)} %get-tuple-element.12), kind=kLoop, calls=%fused_computation.22 | loop fusion | flops 131072 | bytes 1048576 | tf_op jit(solution)/shard_map/stack | solution.py:118
  86.2 8.8 %all-to-all-start.1 = ((f32[128,4,2,128]{3,2,1,0:T(2,128)}), f32[128,4,2,128]{3,2,1,0:T(2,128)S(1)}, u32[]{:S(2)}, u32[]{:S(2)}) async-start(f32[128,4,2,128]{3,2,1,0:T(2,128)} %pad_maximum_fusion), calls=%async_computation.1 | async-start | bytes 1048576 | tf_op jit(solution)/shard_map/all_to_all | solution.py:150
  94.9 0.2 dynamic-slice_reduce_fusion
  95.2 13.5 %all-to-all-done.1 = f32[128,4,2,128]{3,2,1,0:T(2,128)S(1)} async-done(((f32[128,4,2,128]{3,2,1,0:T(2,128)}), f32[128,4,2,128]{3,2,1,0:T(2,128)S(1)}, u32[]{:S(2)}, u32[]{:S(2)}) %all-to-all-start.1) | async-done | bytes 524320 | tf_op jit(solution)/shard_map/all_to_all | solution.py:150
  108.7 0.6 gather_fusion.1
  109.3 0.6 gather_fusion
  109.9 0.6 add.466
  (40 shorter events, 0.7 us)
Async XLA Ops:
  0.0 8.8 %copy-start.1 = (s32[512,8]{0,1:T(8,128)S(1)}, s32[512,8]{0,1:T(8,128)}, u32[]{:S(2)}) copy-start(s32[512,8]{0,1:T(8,128)} %param.8) | copy-start | bytes 49156
  0.0 9.2 %copy-start.2 = (s32[512,8]{0,1:T(8,128)S(1)}, s32[512,8]{0,1:T(8,128)}, u32[]{:S(2)}) copy-start(s32[512,8]{0,1:T(8,128)} %param.10) | copy-start | bytes 49156
  0.0 9.5 %copy-start.3 = (s32[512,8]{0,1:T(8,128)S(1)}, s32[512,8]{0,1:T(8,128)}, u32[]{:S(2)}) copy-start(s32[512,8]{0,1:T(8,128)} %param.9) | copy-start | bytes 49156
  0.0 59.5 %all-to-all-start = ((f32[32,32,1024]{2,1,0:T(8,128)}), f32[32,32,1024]{2,1,0:T(8,128)}, u32[]{:S(2)}, u32[]{:S(2)}) async-start(f32[32,32,1024]{2,1,0:T(8,128)} %param.7), calls=%async_computation | async-start | bytes 8388608 | tf_op jit(solution)/shard_map/all_to_all | solution.py:145
  23.2 1.8 %copy-start.4 = (f32[512,8]{0,1:T(8,128)S(1)}, f32[512,8]{0,1:T(8,128)}, u32[]{:S(2)}) copy-start(f32[512,8]{0,1:T(8,128)} %param.12) | copy-start | bytes 49156
  23.2 2.1 %copy-start.5 = (f32[512,8]{0,1:T(8,128)S(1)}, f32[512,8]{0,1:T(8,128)}, u32[]{:S(2)}) copy-start(f32[512,8]{0,1:T(8,128)} %param.11) | copy-start | bytes 49156
  23.2 2.5 %copy-start.6 = (f32[512]{0:T(512)S(1)}, f32[512]{0:T(512)}, u32[]{:S(2)}) copy-start(f32[512]{0:T(512)} %param.13) | copy-start | bytes 6148
  25.1 2.9 %copy-start = (f32[1,1,512,1024]{3,2,1,0:T(8,128)S(1)}, f32[1,1,512,1024]{3,2,1,0:T(8,128)}, u32[]{:S(2)}) copy-start(f32[1,1,512,1024]{3,2,1,0:T(8,128)} %copy.107) | copy-start | bytes 6291460
  86.2 22.5 %all-to-all-start.1 = ((f32[128,4,2,128]{3,2,1,0:T(2,128)}), f32[128,4,2,128]{3,2,1,0:T(2,128)S(1)}, u32[]{:S(2)}, u32[]{:S(2)}) async-start(f32[128,4,2,128]{3,2,1,0:T(2,128)} %pad_maximum_fusion), calls=%async_computation.1 | async-start | bytes 1048576 | tf_op jit(solution)/shard_map/all_to_all | solution.py:150

commit v11 on v9

--- a/solution.py
+++ b/solution.py
@@ -3,7 +3,7 @@
 import jax
 import jax.numpy as jnp
 from jax import lax
-from jax.sharding import PartitionSpec as P
+from jax.sharding import Mesh, PartitionSpec as P
 from jax.experimental.layout import Layout, with_layout_constraint
 
 LANES = 128
@@ -138,27 +138,42 @@
 
 def on_device(volume, blk_plane, blk_row, blk_col, frac_plane, frac_row, defocus):
     box = volume.shape[2]
-    n_slab = lax.axis_size("slab")
+    n_slab = lax.axis_size("chip") * lax.axis_size("core")
     n_img = lax.axis_size("img")
     n_dev = n_slab * n_img
-    planes = [lax.all_to_all(volume, "slab", split_axis=0, concat_axis=1, tiled=True)]
-    own = planes[0].shape[0]
-    first_plane = (lax.axis_index("img") * n_slab + lax.axis_index("slab")) * own
+    slab_index = lax.axis_index("chip") * lax.axis_size("core") + lax.axis_index("core")
+    p_loc, r_loc, x = volume.shape
+    n_chip = lax.axis_size("chip")
+    own = p_loc // n_slab
+    core = lax.axis_index("core")
+    staged = volume.reshape(n_chip, 2, own, r_loc, x)
+    staged = lax.all_to_all(staged, "chip", split_axis=0, concat_axis=0, tiled=True)
+    mine = jnp.where(core == 0, staged[:, 0], staged[:, 1])
+    other = jnp.where(core == 0, staged[:, 1], staged[:, 0])
+    got = lax.ppermute(other, "core", perm=[(0, 1), (1, 0)])
+    low = jnp.where(core == 0, mine, got)
+    high = jnp.where(core == 0, got, mine)
+    full = jnp.stack([low, high], axis=1)
+    full = jnp.moveaxis(full, 2, 0)
+    planes = [full.reshape(own, n_slab * r_loc, x)]
+    first_plane = (lax.axis_index("img") * n_slab + slab_index) * own
     meta = (blk_plane, blk_row, blk_col, frac_plane, frac_row, defocus)
     parts = send_parts(planes, first_plane, meta, box, n_dev)
-    recv = lax.all_to_all(parts, ("slab", "img"), split_axis=0, concat_axis=0, tiled=True)
-    me = lax.axis_index("slab") * n_img + lax.axis_index("img")
+    recv = lax.all_to_all(parts, ("chip", "core", "img"), split_axis=0, concat_axis=0, tiled=True)
+    me = slab_index * n_img + lax.axis_index("img")
     total = gather_parts(recv, blk_plane, me, own, n_slab, n_img)
     n_blk = blk_plane.shape[1]
     return total.reshape(-1, n_blk, 2, LANES)
 
 
 def solution(mesh):
-    placed = (P("img", "slab", None), P(), P(), P(), P(), P(), P())
+    slab, img = mesh.devices.shape
+    split = Mesh(mesh.devices.reshape(slab // 2, 2, img), ("chip", "core", "img"))
+    placed = (P("img", ("chip", "core"), None), P(), P(), P(), P(), P(), P())
     return jax.shard_map(
         on_device,
-        mesh=mesh,
+        mesh=split,
         in_specs=placed,
-        out_specs=P(("slab", "img"), None, None, None),
+        out_specs=P(("chip", "core", "img"), None, None, None),
         check_vma=False,
     )

time: 104 us -> 123 us (1.18)
  waiting for transfers between devices: 40 us -> 58.7 us
  other arithmetic: 14.8 us -> 18.1 us
  matrix products: 15.1 us -> 12.5 us
    all_to_all x2, waiting for transfers between devices: 40 us -> 57.5 us  [the longest x1 44 us: on_device(): lax.all_to_all(staged, 'chip', split_axis=0, concat_axis=0, tiled=True)]
    another operation x0 -> x2, other arithmetic: none -> 3.53 us  [on_device(): full = jnp.stack([low, high], axis=1)]
    mul x1, other arithmetic: 5.49 us -> 2.38 us  [send_parts(): w_re = ((1.0 - frac_y) * lo_re + frac_y * hi_re) * norm]
    dot_general x1, matrix products: 9.97 us -> 7.08 us  [send_parts(): r_t = jnp.einsum('trc,tpsr->tpcs', piece, w_all, precision=MID)]
    select_n x0 -> x1, other arithmetic: none -> 2.84 us  [on_device(): other = jnp.where(core == 0, staged[:, 1], staged[:, 0])]
    ppermute x0 -> x1, starting transfers between devices: none -> 2.03 us  [on_device(): got = lax.ppermute(other, 'core', perm=[(0, 1), (1, 0)])]
    all_to_all x2, starting transfers between devices: 17.5 us -> 15.8 us  [the longest x1 8 us: on_device(): lax.all_to_all(parts, ('chip', 'core', 'img'), split_axis=0, concat_axis=...]
  transfers between devices with their start and end apart: 2 -> 3, of which waited for: 2 -> 3; matrix products, arithmetic and copies ran while one was open for 23% -> 17% of each run, Pallas kernels for 0% -> 0%
where the time goes in v11:
time: 123 us
  waiting for transfers between devices  58.7 us (48%)
  other arithmetic  18.1 us (15%)
  starting transfers between devices  17.8 us (14%)
  local copies, waits for them, and re-layouts  15.5 us (13%)
  matrix products  12.5 us (10%)
    all_to_all x1, waiting for transfers between devices, on_device(): lax.all_to_all(staged, 'chip', split_axis=0, concat_axis=0, tiled=True)  44 us
    all_to_all x1, waiting for transfers between devices, on_device(): lax.all_to_all(parts, ('chip', 'core', 'img'), split_axis=0, concat_axis=...  13.5 us
    all_to_all x1, starting transfers between devices, on_device(): lax.all_to_all(parts, ('chip', 'core', 'img'), split_axis=0, concat_axis=...  8 us
    all_to_all x1, starting transfers between devices, on_device(): lax.all_to_all(staged, 'chip', split_axis=0, concat_axis=0, tiled=True)  7.77 us
    dot_general x1, matrix products, send_parts(): r_t = jnp.einsum('trc,tpsr->tpcs', piece, w_all, precision=MID)  7.08 us
    sub x2, local copies, waits for them, and re-layouts, row_roots(): a_re[:, :, None] * b_re[:, None, :] - a_im[:, :, None] * b_im[:, None, :]  5.87 us
    dot_general x1, matrix products, send_parts(): y_j = jnp.einsum('qkpn,tpnjs->tqkjs', w_j, r5, precision=MID)  5.37 us
    sub x2, other arithmetic, row_roots(): a_re[:, :, None] * b_re[:, None, :] - a_im[:, :, None] * b_im[:, None, :]  3.9 us
  transfers between devices with their start and end apart: 3, of which 3 were waited for; matrix products, arithmetic and copies ran while one was open for 17% of the time, Pallas kernels for 0%

profile of v11, /device:TPU:1, one launch (start us, length us, event | category | flops | bytes accessed | tf_op | source)
XLA Modules:
  0.0 122.9 jit_solution(3645060585395625187)
XLA Ops:
  0.0 7.8 %all-to-all-start = ((f32[16,2,1,32,1024]{4,3,1,2,0:T(8,128)}), f32[16,2,1,32,1024]{4,3,1,2,0:T(8,128)}, u32[]{:S(2)}, u32[]{:S(2)}) async-start(f32[16,2,1,32,1024]{4,3,1,2,0:T(8,128)} %bitcast.141), calls=%async_computation | async-start | bytes 8388608 | tf_op jit(solution)/shard_map/all_to_all | solution.py:150
  7.8 0.1 copy.234
  7.9 0.1 eq.93
  8.1 0.1 copy.240
  8.3 0.1 broadcast_in_dim.129
  8.4 0.1 copy.242
  8.6 0.1 broadcast_in_dim.132
  8.8 0.2 convert_reduce_fusion
  9.2 0.2 copy.249
  9.3 0.2 mul.884
  9.5 1.1 fusion.54
  10.6 2.0 %multiply_subtract_fusion.1 = (f32[512,32,32]{0,2,1:T(8,128)}, f32[512,32,32]{0,2,1:T(8,128)S(1)}) fusion(f32[512,32]{0,1:T(8,128)S(1)} %get-tuple-element.32, f32[512,32]{0,1:T(8,128)S(1)} %get-tuple-element.27, f32[512,32]{0,1:T(8,128)S(1)} %get-tuple-element.33, f32[512,32]{0,1:T(8,128)S(1)} %get-tuple-element.26), kind=kLoop, calls=%fused_computation.28 | loop fusion | flops 3145728 | bytes 4456448 | tf_op jit(solution)/shard_map/sub | solution.py:76
  12.5 2.9 %copy.250 = f32[1,1,512,1024]{3,2,1,0:T(8,128)} copy(f32[1,1,512,1024]{2,3,1,0:T(8,128)} %bitcast.139) | data formatting | bytes 4194304 | tf_op jit(solution)/shard_map/sub | solution.py:76
  15.5 1.8 %copy.252 = f32[1,1,512,1024]{3,2,1,0:T(8,128)} copy(f32[1,1,512,1024]{2,3,1,0:T(8,128)S(1)} %bitcast.137) | data formatting | bytes 4194304 | tf_op jit(solution)/shard_map/add | solution.py:77
  17.3 1.9 %multiply_subtract_fusion = (f32[512,32,32]{0,2,1:T(8,128)}, f32[512,32,32]{0,2,1:T(8,128)S(1)}) fusion(f32[512,32]{0,1:T(8,128)S(1)} %get-tuple-element.37, f32[512,32]{0,1:T(8,128)S(1)} %get-tuple-element.38, f32[512,32]{0,1:T(8,128)S(1)} %get-tuple-element.36, f32[512,32]{0,1:T(8,128)S(1)} %get-tuple-element.39), kind=kLoop, calls=%fused_computation.27 | loop fusion | flops 3145728 | bytes 4456448 | tf_op jit(solution)/shard_map/sub | solution.py:76
  19.2 3.0 %copy.251 = f32[1,1,512,1024]{3,2,1,0:T(8,128)} copy(f32[1,1,512,1024]{2,3,1,0:T(8,128)} %bitcast.140) | data formatting | bytes 4194304 | tf_op jit(solution)/shard_map/sub | solution.py:76
  22.2 1.8 %copy.253 = f32[1,1,512,1024]{3,2,1,0:T(8,128)} copy(f32[1,1,512,1024]{2,3,1,0:T(8,128)S(1)} %bitcast.138) | data formatting | bytes 4194304 | tf_op jit(solution)/shard_map/add | solution.py:77
  24.0 0.1 copy.238
  24.2 0.1 broadcast_in_dim.125
  24.3 0.1 copy.246
  24.5 0.1 broadcast_in_dim.138
  24.7 0.1 broadcast_in_dim.134
  24.9 0.2 copy.248
  25.1 0.2 broadcast_in_dim_reshape.2
  25.3 0.2 copy.245
  25.5 0.2 mul.867
  25.7 0.3 fusion.55
  26.0 0.3 negate_multiply_fusion
  26.3 44.0 %all-to-all-done = f32[16,2,1,32,1024]{4,3,1,2,0:T(8,128)} async-done(((f32[16,2,1,32,1024]{4,3,1,2,0:T(8,128)}), f32[16,2,1,32,1024]{4,3,1,2,0:T(8,128)}, u32[]{:S(2)}, u32[]{:S(2)}) %all-to-all-start) | async-done | bytes 4194336 | tf_op jit(solution)/shard_map/all_to_all | solution.py:150
  70.3 2.8 %select_bitcast_fusion = f32[16,1,32,1024]{3,2,0,1:T(8,128)S(1)} fusion(f32[16,2,1,32,1024]{4,3,1,2,0:T(8,128)} %all-to-all-done, pred[]{:T(512)S(6)} %eq.106), kind=kLoop, calls=%fused_computation.22 | loop fusion | flops 524288 | bytes 6291457 | tf_op jit(solution)/shard_map/jit(_where)/select_n | solution.py:152
  73.1 2.0 %collective-permute-start = (f32[16,1,32,1024]{3,2,0,1:T(8,128)S(1)}, f32[16,1,32,1024]{3,2,0,1:T(8,128)S(1)}, u32[]{:S(2)}, u32[]{:S(2)}) collective-permute-start(f32[16,1,32,1024]{3,2,0,1:T(8,128)S(1)} %select_bitcast_fusion), channel_id=1, source_target_pairs={{0,4},{4,0},{1,5},{5,1},{2,6},{6,2},{3,7},{7,3},{8,12},{12,8},{9,1... | collective-permute-start | bytes 6291464 | tf_op jit(solution)/shard_map/ppermute | solution.py:153
  75.4 2.4 %add_multiply_fusion.1 = (f32[1,1,512,1024]{3,2,1,0:T(8,128)S(1)}, f32[1,1,512,1024]{3,2,1,0:T(8,128)S(1)}) fusion(f32[1,1,512,1024]{3,2,1,0:T(8,128)S(1)} %copy-done.2, f32[1,1,512,1024]{3,2,1,0:T(8,128)S(1)} %copy-done, f32[512]{0:T(512)S(1)} %broadcast_in_dim_reshape.2, f32[512]{0:T(512)S(1)} %broadcast_subtract_fusion, f32[1,1,512,1024]{3,2,1,0:T(8,128)} %copy.253, ...), kind=kLoop, calls=%fused_computation.26 | loop fusion | flops 4194304 | bytes 12587008 | tf_op jit(solution)/shard_map/mul | solution.py:83
  77.8 1.1 collective-permute-done
  78.9 3.0 %fusion.9 = (f32[16,1,1,32,1024]{4,3,1,0,2:T(8,128)S(1)}, f32[16,1,1,32,1024]{4,3,1,0,2:T(8,128)S(1)}) fusion(f32[16,1,32,1024]{3,2,0,1:T(8,128)S(1)} %collective-permute-done, pred[]{:T(512)S(6)} %eq.106, f32[16,2,1,32,1024]{4,3,1,2,0:T(8,128)} %all-to-all-done), kind=kLoop, calls=%fused_computation.17 | loop fusion | flops 1572864 | bytes 10486784 | tf_op jit(solution)/shard_map/stack | solution.py:156
  81.9 0.6 pad_maximum_fusion
  82.5 7.1 %fusion.8 = f32[2,128,8,512,1]{3,2,1,0,4:T(8,128)S(1)} fusion(f32[1024,1024,1]{1,0,2:T(8,128)S(1)} %bitcast.142, f32[1,1,512,1024]{3,2,1,0:T(8,128)S(1)} %get-tuple-element.25, f32[1,1,512,1024]{3,2,1,0:T(8,128)S(1)} %get-tuple-element.24), kind=kOutput, calls=%fused_computation.10 | convolution fusion | flops 6443499520 | bytes 12582912 | tf_op jit(solution)/shard_map/trc,tpsr->tpcs/dot_general | solution.py:96
  89.6 5.4 %fusion.5 = f32[1,2,128,8,512]{2,4,1,3,0:T(8,128)S(1)} fusion(f32[2,128,8,512,1]{3,2,1,0,4:T(8,128)S(1)} %fusion.8, f32[1,128,2,128]{3,1,2,0:T(8,128)S(1)} %get-tuple-element.21, f32[1,128,2,128]{3,1,2,0:T(8,128)S(1)} %get-tuple-element.20), kind=kOutput, calls=%fused_computation.9 | convolution fusion | flops 1610678272 | bytes 8650752 | tf_op jit(solution)/shard_map/qkpn,tpnjs->tqkjs/dot_general | solution.py:100
  94.9 1.4 %subtract_reduce_fusion = (f32[128,512]{0,1:T(8,128)S(1)}, f32[128,512]{0,1:T(8,128)S(1)}) fusion(f32[1,2,128,8,512]{2,4,1,3,0:T(8,128)S(1)} %fusion.5, f32[128,8]{0,1:T(8,128)S(1)} %get-tuple-element.44, f32[8,512]{1,0:T(8,128)S(1)} %get-tuple-element.31, f32[128,8]{0,1:T(8,128)S(1)} %get-tuple-element.45, f32[8,512]{1,0:T(8,128)S(1)} %get-tuple-element.30), kind=kLoop, calls=%fused_computation.20 | loop fusion | flops 7208960 | bytes 4759552 | tf_op jit(solution)/shard_map/reduce_sum | solution.py:114
  96.4 1.1 copy_multiply_fusion.1
  97.5 1.2 copy.263
  98.7 8.0 %all-to-all-start.1 = ((f32[128,4,2,128]{3,2,1,0:T(2,128)}), f32[128,4,2,128]{3,2,1,0:T(2,128)S(1)}, u32[]{:S(2)}, u32[]{:S(2)}) async-start(f32[128,4,2,128]{3,2,1,0:T(2,128)} %copy.263), calls=%async_computation.1 | async-start | bytes 1048576 | tf_op jit(solution)/shard_map/all_to_all | solution.py:162
  106.7 0.2 dynamic-slice_reduce_fusion
  107.0 13.5 %all-to-all-done.1 = f32[128,4,2,128]{3,2,1,0:T(2,128)S(1)} async-done(((f32[128,4,2,128]{3,2,1,0:T(2,128)}), f32[128,4,2,128]{3,2,1,0:T(2,128)S(1)}, u32[]{:S(2)}, u32[]{:S(2)}) %all-to-all-start.1) | async-done | bytes 524320 | tf_op jit(solution)/shard_map/all_to_all | solution.py:162
  120.5 0.1 copy.264
  120.6 0.4 copy.265
  121.0 0.6 gather_fusion.1
  121.6 0.6 gather_fusion
  122.3 0.6 add.470
  (47 shorter events, 0.9 us)
Async XLA Ops:
  0.0 7.8 %copy-start.3 = (s32[512,8]{0,1:T(8,128)S(1)}, s32[512,8]{0,1:T(8,128)}, u32[]{:S(2)}) copy-start(s32[512,8]{0,1:T(8,128)} %param.8) | copy-start | bytes 49156
  0.0 8.1 %copy-start.4 = (s32[512,8]{0,1:T(8,128)S(1)}, s32[512,8]{0,1:T(8,128)}, u32[]{:S(2)}) copy-start(s32[512,8]{0,1:T(8,128)} %param.10) | copy-start | bytes 49156
  0.0 8.4 %copy-start.5 = (s32[512,8]{0,1:T(8,128)S(1)}, s32[512,8]{0,1:T(8,128)}, u32[]{:S(2)}) copy-start(s32[512,8]{0,1:T(8,128)} %param.9) | copy-start | bytes 49156
  0.0 70.2 %all-to-all-start = ((f32[16,2,1,32,1024]{4,3,1,2,0:T(8,128)}), f32[16,2,1,32,1024]{4,3,1,2,0:T(8,128)}, u32[]{:S(2)}, u32[]{:S(2)}) async-start(f32[16,2,1,32,1024]{4,3,1,2,0:T(8,128)} %bitcast.141), calls=%async_computation | async-start | bytes 8388608 | tf_op jit(solution)/shard_map/all_to_all | solution.py:150
  22.2 1.8 %copy-start.6 = (f32[512,8]{0,1:T(8,128)S(1)}, f32[512,8]{0,1:T(8,128)}, u32[]{:S(2)}) copy-start(f32[512,8]{0,1:T(8,128)} %param.11) | copy-start | bytes 49156
  22.2 2.1 %copy-start.7 = (f32[512,8]{0,1:T(8,128)S(1)}, f32[512,8]{0,1:T(8,128)}, u32[]{:S(2)}) copy-start(f32[512,8]{0,1:T(8,128)} %param.12) | copy-start | bytes 49156
  22.2 2.5 %copy-start.8 = (f32[512]{0:T(512)S(1)}, f32[512]{0:T(512)}, u32[]{:S(2)}) copy-start(f32[512]{0:T(512)} %param.13) | copy-start | bytes 6148
  26.3 49.1 %copy-start = (f32[1,1,512,1024]{3,2,1,0:T(8,128)S(1)}, f32[1,1,512,1024]{3,2,1,0:T(8,128)}, u32[]{:S(2)}) copy-start(f32[1,1,512,1024]{3,2,1,0:T(8,128)} %copy.250) | copy-start | bytes 6291460
  70.3 5.1 %copy-start.1 = (f32[1,1,512,1024]{3,2,1,0:T(8,128)S(1)}, f32[1,1,512,1024]{3,2,1,0:T(8,128)}, u32[]{:S(2)}) copy-start(f32[1,1,512,1024]{3,2,1,0:T(8,128)} %copy.252) | copy-start | bytes 6291460
  70.3 5.1 %copy-start.2 = (f32[1,1,512,1024]{3,2,1,0:T(8,128)S(1)}, f32[1,1,512,1024]{3,2,1,0:T(8,128)}, u32[]{:S(2)}) copy-start(f32[1,1,512,1024]{3,2,1,0:T(8,128)} %copy.251) | copy-start | bytes 6291460
  73.1 5.8 %collective-permute-start = (f32[16,1,32,1024]{3,2,0,1:T(8,128)S(1)}, f32[16,1,32,1024]{3,2,0,1:T(8,128)S(1)}, u32[]{:S(2)}, u32[]{:S(2)}) collective-permute-start(f32[16,1,32,1024]{3,2,0,1:T(8,128)S(1)} %select_bitcast_fusion), channel_id=1, source_target_pairs={{0,4},{4,0},{1,5},{5,1},{2,6},{6,2},{3,7},{7,3},{8,12},{12,8},{9,1... | collective-permute-start | bytes 6291464 | tf_op jit(solution)/shard_map/ppermute | solution.py:153
  98.7 21.8 %all-to-all-start.1 = ((f32[128,4,2,128]{3,2,1,0:T(2,128)}), f32[128,4,2,128]{3,2,1,0:T(2,128)S(1)}, u32[]{:S(2)}, u32[]{:S(2)}) async-start(f32[128,4,2,128]{3,2,1,0:T(2,128)} %copy.263), calls=%async_computation.1 | async-start | bytes 1048576 | tf_op jit(solution)/shard_map/all_to_all | solution.py:162

commit v12 on v9

--- a/solution.py
+++ b/solution.py
@@ -132,8 +132,12 @@
         src = (holder % n_slab) * n_img + holder // n_slab
         return src * slots + (q % own) * 4 + side * 2 + my_rank
 
-    flat = recv.reshape(-1, 2, LANES)
-    return flat[place(mine, 0)] + flat[place(mine + 1, 1)]
+    flat = recv.reshape(-1, 2 * LANES)
+    rows = lax.iota(jnp.int32, flat.shape[0])[None, :]
+    pick = (rows == place(mine, 0)[:, None]).astype(jnp.float32) + (
+        rows == place(mine + 1, 1)[:, None]
+    ).astype(jnp.float32)
+    return jnp.dot(pick, flat, precision=lax.Precision.HIGHEST).reshape(-1, 2, LANES)
 
 
 def on_device(volume, blk_plane, blk_row, blk_col, frac_plane, frac_row, defocus):

time: 104 us -> 104 us (level)
    mul x1, other arithmetic: 1.07 us -> 2.55 us  [send_parts(): parts = jnp.stack([scale * o_re, scale * o_im], axis=1)]
    gather x2 -> x0, local copies, waits for them, and re-layouts: 1.22 us -> none  [gather_parts(): return flat[place(mine, 0)] + flat[place(mine + 1, 1)]]
  transfers between devices with their start and end apart: 2 -> 2, of which waited for: 2 -> 2; matrix products, arithmetic and copies ran while one was open for 23% -> 24% of each run, Pallas kernels for 0% -> 0%
where the time goes in v12:
time: 104 us
  waiting for transfers between devices  39.4 us (38%)
  starting transfers between devices  17.5 us (17%)
  other arithmetic  15.7 us (15%)
  matrix products  15.7 us (15%)
  local copies, waits for them, and re-layouts  15.2 us (15%)
    all_to_all x1, waiting for transfers between devices, on_device(): lax.all_to_all(volume, 'slab', split_axis=0, concat_axis=1, tiled=True)  26 us
    all_to_all x1, waiting for transfers between devices, on_device(): lax.all_to_all(parts, ('slab', 'img'), split_axis=0, concat_axis=0, tiled...  13.4 us
    dot_general x1, matrix products, send_parts(): r_t = jnp.einsum('trc,tpsr->tpcs', piece, w_all, precision=MID)  9.97 us
    all_to_all x1, starting transfers between devices, on_device(): lax.all_to_all(volume, 'slab', split_axis=0, concat_axis=1, tiled=True)  8.78 us
    all_to_all x1, starting transfers between devices, on_device(): lax.all_to_all(parts, ('slab', 'img'), split_axis=0, concat_axis=0, tiled...  8.76 us
    sub x2, local copies, waits for them, and re-layouts, row_roots(): a_re[:, :, None] * b_re[:, None, :] - a_im[:, :, None] * b_im[:, None, :]  5.86 us
    mul x1, other arithmetic, send_parts(): w_re = ((1.0 - frac_y) * lo_re + frac_y * hi_re) * norm  5.49 us
    dot_general x1, matrix products, send_parts(): y_j = jnp.einsum('qkpn,tpnjs->tqkjs', w_j, r5, precision=MID)  5.14 us
  transfers between devices with their start and end apart: 2, of which 2 were waited for; matrix products, arithmetic and copies ran while one was open for 24% of the time, Pallas kernels for 0%

profile of v12, /device:TPU:1, one launch (start us, length us, event | category | flops | bytes accessed | tf_op | source)
XLA Modules:
  0.0 103.9 jit_solution(11650716817164550324)
XLA Ops:
  0.0 8.8 %all-to-all-start = ((f32[32,32,1024]{2,1,0:T(8,128)}), f32[32,32,1024]{2,1,0:T(8,128)}, u32[]{:S(2)}, u32[]{:S(2)}) async-start(f32[32,32,1024]{2,1,0:T(8,128)} %param.7), calls=%async_computation | async-start | bytes 8388608 | tf_op jit(solution)/shard_map/all_to_all | solution.py:148
  8.8 0.1 copy.90
  9.0 0.1 reshape.1350
  9.2 0.1 copy.100
  9.3 0.1 broadcast_in_dim.133
  9.5 0.1 copy.97
  9.6 0.1 broadcast_in_dim.130
  9.8 0.2 convert_reduce_fusion
  10.2 0.2 copy.109
  10.3 0.2 mul.877
  10.5 1.1 %fusion.58 = (f32[512,32]{0,1:T(8,128)S(1)}, f32[512,32]{0,1:T(8,128)S(1)}, f32[512,32]{0,1:T(8,128)S(1)}, f32[512,32]{0,1:T(8,128)S(1)}, f32[512,32]{0,1:T(8,12...) fusion(s32[32]{0:T(128)S(1)} %iota_multiply_fusion, s32[512]{0:T(512)S(1)} %mul.877, ...), kind=kLoop, calls=%fused_computation.109 | loop fusion | flops 983040 | bytes 528512 | tf_op jit(solution)/shard_map/cos | solution.py:21
  11.6 1.9 %multiply_subtract_fusion.1 = (f32[512,32,32]{0,2,1:T(8,128)}, f32[512,32,32]{0,2,1:T(8,128)S(1)}) fusion(f32[512,32]{0,1:T(8,128)S(1)} %get-tuple-element.30, f32[512,32]{0,1:T(8,128)S(1)} %get-tuple-element.25, f32[512,32]{0,1:T(8,128)S(1)} %get-tuple-element.31, f32[512,32]{0,1:T(8,128)S(1)} %get-tuple-element.24), kind=kLoop, calls=%fused_computation.18 | loop fusion | flops 3145728 | bytes 4456448 | tf_op jit(solution)/shard_map/sub | solution.py:76
  13.6 2.9 %copy.110 = f32[1,1,512,1024]{3,2,1,0:T(8,128)} copy(f32[1,1,512,1024]{2,3,1,0:T(8,128)} %bitcast.88) | data formatting | bytes 4194304 | tf_op jit(solution)/shard_map/sub | solution.py:76
  16.5 1.9 %copy.112 = f32[1,1,512,1024]{3,2,1,0:T(8,128)} copy(f32[1,1,512,1024]{2,3,1,0:T(8,128)S(1)} %bitcast.86) | data formatting | bytes 4194304 | tf_op jit(solution)/shard_map/add | solution.py:77
  18.3 1.9 %multiply_subtract_fusion = (f32[512,32,32]{0,2,1:T(8,128)}, f32[512,32,32]{0,2,1:T(8,128)S(1)}) fusion(f32[512,32]{0,1:T(8,128)S(1)} %get-tuple-element.35, f32[512,32]{0,1:T(8,128)S(1)} %get-tuple-element.36, f32[512,32]{0,1:T(8,128)S(1)} %get-tuple-element.34, f32[512,32]{0,1:T(8,128)S(1)} %get-tuple-element.37), kind=kLoop, calls=%fused_computation.17 | loop fusion | flops 3145728 | bytes 4456448 | tf_op jit(solution)/shard_map/sub | solution.py:76
  20.2 3.0 %copy.111 = f32[1,1,512,1024]{3,2,1,0:T(8,128)} copy(f32[1,1,512,1024]{2,3,1,0:T(8,128)} %bitcast.89) | data formatting | bytes 4194304 | tf_op jit(solution)/shard_map/sub | solution.py:76
  23.2 1.8 %copy.113 = f32[1,1,512,1024]{3,2,1,0:T(8,128)} copy(f32[1,1,512,1024]{2,3,1,0:T(8,128)S(1)} %bitcast.87) | data formatting | bytes 4194304 | tf_op jit(solution)/shard_map/add | solution.py:77
  25.0 0.1 copy.106
  25.2 0.1 broadcast_in_dim.139
  25.3 0.1 copy.94
  25.5 0.1 broadcast_in_dim.126
  25.7 0.1 broadcast_in_dim.135
  25.9 0.2 copy.108
  26.1 0.2 broadcast_in_dim_reshape.2
  26.3 0.2 copy.105
  26.5 0.2 mul.860
  26.7 0.1 copy.96
  26.9 0.1 copy.104
  27.0 0.1 copy.102
  27.1 0.1 copy.99
  27.3 0.3 fusion.61
  27.5 0.3 negate_multiply_fusion
  27.8 0.1 fusion.68
  28.0 5.5 %add_multiply_fusion.1 = (f32[1,1,512,1024]{3,2,1,0:T(8,128)}, f32[1,1,512,1024]{3,2,1,0:T(8,128)}) fusion(f32[1,1,512,1024]{3,2,1,0:T(8,128)} %copy.111, f32[1,1,512,1024]{3,2,1,0:T(8,128)S(1)} %copy-done, f32[512]{0:T(512)S(1)} %broadcast_in_dim_reshape.2, f32[512]{0:T(512)S(1)} %broadcast_subtract_fusion, f32[1,1,512,1024]{3,2,1,0:T(8,128)} %copy.113, ...), kind=kLoop, calls=%fused_computation.16 | loop fusion | flops 4194304 | bytes 12587008 | tf_op jit(solution)/shard_map/mul | solution.py:83
  33.4 26.0 %all-to-all-done = f32[32,32,1024]{2,1,0:T(8,128)} async-done(((f32[32,32,1024]{2,1,0:T(8,128)}), f32[32,32,1024]{2,1,0:T(8,128)}, u32[]{:S(2)}, u32[]{:S(2)}) %all-to-all-start) | async-done | bytes 4194336 | tf_op jit(solution)/shard_map/all_to_all | solution.py:148
  59.5 10.0 %fusion.8 = f32[2,128,8,512,1]{3,2,1,0,4:T(8,128)S(1)} fusion(f32[1024,1024,1]{1,0,2:T(8,128)} %bitcast.14, f32[1,1,512,1024]{3,2,1,0:T(8,128)} %get-tuple-element.23, f32[1,1,512,1024]{3,2,1,0:T(8,128)} %get-tuple-element.22), kind=kOutput, calls=%fused_computation.7 | convolution fusion | flops 6443499520 | bytes 12582912 | tf_op jit(solution)/shard_map/trc,tpsr->tpcs/dot_general | solution.py:96
  69.5 5.1 %fusion.5 = f32[1,2,128,8,512]{2,4,1,3,0:T(8,128)S(1)} fusion(f32[2,128,8,512,1]{3,2,1,0,4:T(8,128)S(1)} %fusion.8, f32[1,128,2,128]{3,1,2,0:T(8,128)S(1)} %get-tuple-element.19, f32[1,128,2,128]{3,1,2,0:T(8,128)S(1)} %get-tuple-element.18), kind=kOutput, calls=%fused_computation.6 | convolution fusion | flops 1610678272 | bytes 8650752 | tf_op jit(solution)/shard_map/qkpn,tpnjs->tqkjs/dot_general | solution.py:100
  74.6 1.4 %subtract_reduce_fusion = (f32[128,512]{0,1:T(8,128)S(1)}, f32[128,512]{0,1:T(8,128)S(1)}) fusion(f32[1,2,128,8,512]{2,4,1,3,0:T(8,128)S(1)} %fusion.5, f32[128,8]{0,1:T(8,128)S(1)} %get-tuple-element.42, f32[8,512]{1,0:T(8,128)S(1)} %get-tuple-element.29, f32[128,8]{0,1:T(8,128)S(1)} %get-tuple-element.43, f32[8,512]{1,0:T(8,128)S(1)} %get-tuple-element.28), kind=kLoop, calls=%fused_computation.11 | loop fusion | flops 7208960 | bytes 4759552 | tf_op jit(solution)/shard_map/reduce_sum | solution.py:114
  76.1 2.5 %fusion.20 = (f32[128,4,1,128]{3,1,0,2:T(4,128)S(1)}, f32[128,4,1,128]{3,1,0,2:T(4,128)S(1)}) fusion(f32[128,4,1,128]{3,1,0,2:T(4,128)S(1)} %bitcast.93, f32[128,4]{1,0:T(8,128)S(1)} %copy.104, f32[128,4]{1,0:T(8,128)S(1)} %copy.102, s32[128,4]{1,0:T(8,128)S(1)} %copy.99, f32[128,4]{1,0:T(8,128)S(1)} %copy.96, f32[128,4,1,128]{3,1,0,2:T(4,128)S(1)} %bitcast.94), kind=kLoop, calls=%fused_computation.50 | loop fusion | flops 786432 | bytes 1056768 | tf_op jit(solution)/shard_map/mul | solution.py:118
  78.6 0.1 pad_maximum_fusion
  78.7 0.9 copy.117
  79.6 8.8 %all-to-all-start.1 = ((f32[128,4,2,128]{3,1,2,0:T(4,128)}), f32[128,4,2,128]{3,1,2,0:T(4,128)S(1)}, u32[]{:S(2)}, u32[]{:S(2)}) async-start(f32[128,4,2,128]{3,1,2,0:T(4,128)} %copy.117), calls=%async_computation.1 | async-start | bytes 1048576 | tf_op jit(solution)/shard_map/all_to_all | solution.py:153
  88.4 0.2 dynamic-slice_reduce_fusion
  88.8 13.4 %all-to-all-done.1 = f32[128,4,2,128]{3,1,2,0:T(4,128)S(1)} async-done(((f32[128,4,2,128]{3,1,2,0:T(4,128)}), f32[128,4,2,128]{3,1,2,0:T(4,128)S(1)}, u32[]{:S(2)}, u32[]{:S(2)}) %all-to-all-start.1) | async-done | bytes 524320 | tf_op jit(solution)/shard_map/all_to_all | solution.py:153
  102.2 0.3 copy.118
  102.5 0.2 copy.119
  102.7 0.6 fusion.41
  103.3 0.6 copy.120
  (44 shorter events, 1.0 us)
Async XLA Ops:
  0.0 8.8 %copy-start.1 = (s32[512,8]{0,1:T(8,128)S(1)}, s32[512,8]{0,1:T(8,128)}, u32[]{:S(2)}) copy-start(s32[512,8]{0,1:T(8,128)} %param.8) | copy-start | bytes 49156
  0.0 9.2 %copy-start.2 = (s32[512,8]{0,1:T(8,128)S(1)}, s32[512,8]{0,1:T(8,128)}, u32[]{:S(2)}) copy-start(s32[512,8]{0,1:T(8,128)} %param.9) | copy-start | bytes 49156
  0.0 9.5 %copy-start.3 = (s32[512,8]{0,1:T(8,128)S(1)}, s32[512,8]{0,1:T(8,128)}, u32[]{:S(2)}) copy-start(s32[512,8]{0,1:T(8,128)} %param.10) | copy-start | bytes 49156
  0.0 59.5 %all-to-all-start = ((f32[32,32,1024]{2,1,0:T(8,128)}), f32[32,32,1024]{2,1,0:T(8,128)}, u32[]{:S(2)}, u32[]{:S(2)}) async-start(f32[32,32,1024]{2,1,0:T(8,128)} %param.7), calls=%async_computation | async-start | bytes 8388608 | tf_op jit(solution)/shard_map/all_to_all | solution.py:148
  23.2 1.8 %copy-start.4 = (f32[512,8]{0,1:T(8,128)S(1)}, f32[512,8]{0,1:T(8,128)}, u32[]{:S(2)}) copy-start(f32[512,8]{0,1:T(8,128)} %param.12) | copy-start | bytes 49156
  23.2 2.1 %copy-start.5 = (f32[512,8]{0,1:T(8,128)S(1)}, f32[512,8]{0,1:T(8,128)}, u32[]{:S(2)}) copy-start(f32[512,8]{0,1:T(8,128)} %param.11) | copy-start | bytes 49156
  23.2 2.5 %copy-start.6 = (f32[512]{0:T(512)S(1)}, f32[512]{0:T(512)}, u32[]{:S(2)}) copy-start(f32[512]{0:T(512)} %param.13) | copy-start | bytes 6148
  25.0 2.9 %copy-start = (f32[1,1,512,1024]{3,2,1,0:T(8,128)S(1)}, f32[1,1,512,1024]{3,2,1,0:T(8,128)}, u32[]{:S(2)}) copy-start(f32[1,1,512,1024]{3,2,1,0:T(8,128)} %copy.110) | copy-start | bytes 6291460
  79.6 22.5 %all-to-all-start.1 = ((f32[128,4,2,128]{3,1,2,0:T(4,128)}), f32[128,4,2,128]{3,1,2,0:T(4,128)S(1)}, u32[]{:S(2)}, u32[]{:S(2)}) async-start(f32[128,4,2,128]{3,1,2,0:T(4,128)} %copy.117), calls=%async_computation.1 | async-start | bytes 1048576 | tf_op jit(solution)/shard_map/all_to_all | solution.py:153

commit v13 on v9

--- a/solution.py
+++ b/solution.py
@@ -129,7 +129,7 @@
 
     def place(q, side):
         holder = q // own
-        src = (holder % n_slab) * n_img + holder // n_slab
+        src = holder
         return src * slots + (q % own) * 4 + side * 2 + my_rank
 
     flat = recv.reshape(-1, 2, LANES)
@@ -146,7 +146,9 @@
     first_plane = (lax.axis_index("img") * n_slab + lax.axis_index("slab")) * own
     meta = (blk_plane, blk_row, blk_col, frac_plane, frac_row, defocus)
     parts = send_parts(planes, first_plane, meta, box, n_dev)
-    recv = lax.all_to_all(parts, ("slab", "img"), split_axis=0, concat_axis=0, tiled=True)
+    parts = jnp.swapaxes(parts.reshape(n_slab, n_img, *parts.shape[1:]), 0, 1)
+    parts = parts.reshape(n_dev, *parts.shape[2:])
+    recv = lax.all_to_all(parts, ("img", "slab"), split_axis=0, concat_axis=0, tiled=True)
     me = lax.axis_index("slab") * n_img + lax.axis_index("img")
     total = gather_parts(recv, blk_plane, me, own, n_slab, n_img)
     n_blk = blk_plane.shape[1]

time: 104 us -> 105 us (level)
  waiting for transfers between devices: 40 us -> 38 us
  other arithmetic: 14.8 us -> 16.6 us
  local copies, waits for them, and re-layouts: 15.5 us -> 17.2 us
    all_to_all x1, waiting for transfers between devices: 26.5 us -> 24.6 us  [on_device(): lax.all_to_all(volume, 'slab', split_axis=0, concat_axis=1, tiled=True)]
    reshape x0 -> x4, local copies, waits for them, and re-layouts: none -> 1.5 us  [the longest x1 1.19 us: on_device(): parts = parts.reshape(n_dev, *parts.shape[2:])]
    mul x1, other arithmetic: 1.07 us -> 2.55 us  [send_parts(): parts = jnp.stack([scale * o_re, scale * o_im], axis=1)]
    another operation x1 -> x0, local copies, waits for them, and re-layouts: 1.19 us -> none  [send_parts(): parts = jnp.stack([scale * o_re, scale * o_im], axis=1)]
  transfers between devices with their start and end apart: 2 -> 2, of which waited for: 2 -> 2; matrix products, arithmetic and copies ran while one was open for 23% -> 25% of each run, Pallas kernels for 0% -> 0%
where the time goes in v13:
time: 105 us
  waiting for transfers between devices  38 us (36%)
  starting transfers between devices  17.5 us (17%)
  local copies, waits for them, and re-layouts  17.2 us (16%)
  other arithmetic  16.6 us (16%)
  matrix products  15.1 us (14%)
    all_to_all x1, waiting for transfers between devices, on_device(): lax.all_to_all(volume, 'slab', split_axis=0, concat_axis=1, tiled=True)  24.6 us
    all_to_all x1, waiting for transfers between devices, on_device(): lax.all_to_all(parts, ('img', 'slab'), split_axis=0, concat_axis=0, tiled...  13.4 us
    dot_general x1, matrix products, send_parts(): r_t = jnp.einsum('trc,tpsr->tpcs', piece, w_all, precision=MID)  9.97 us
    all_to_all x1, starting transfers between devices, on_device(): lax.all_to_all(volume, 'slab', split_axis=0, concat_axis=1, tiled=True)  8.78 us
    all_to_all x1, starting transfers between devices, on_device(): lax.all_to_all(parts, ('img', 'slab'), split_axis=0, concat_axis=0, tiled...  8.76 us
    sub x2, local copies, waits for them, and re-layouts, row_roots(): a_re[:, :, None] * b_re[:, None, :] - a_im[:, :, None] * b_im[:, None, :]  5.86 us
    mul x1, other arithmetic, send_parts(): w_re = ((1.0 - frac_y) * lo_re + frac_y * hi_re) * norm  5.49 us
    dot_general x1, matrix products, send_parts(): y_j = jnp.einsum('qkpn,tpnjs->tqkjs', w_j, r5, precision=MID)  5.14 us
  transfers between devices with their start and end apart: 2, of which 2 were waited for; matrix products, arithmetic and copies ran while one was open for 25% of the time, Pallas kernels for 0%

profile of v13, /device:TPU:1, one launch (start us, length us, event | category | flops | bytes accessed | tf_op | source)
XLA Modules:
  0.0 104.9 jit_solution(14516877665597696458)
XLA Ops:
  0.0 8.8 %all-to-all-start = ((f32[32,32,1024]{2,1,0:T(8,128)}), f32[32,32,1024]{2,1,0:T(8,128)}, u32[]{:S(2)}, u32[]{:S(2)}) async-start(f32[32,32,1024]{2,1,0:T(8,128)} %param.7), calls=%async_computation | async-start | bytes 8388608 | tf_op jit(solution)/shard_map/all_to_all | solution.py:144
  8.8 0.1 copy.169
  9.0 0.1 eq.85
  9.2 0.1 copy.176
  9.3 0.1 broadcast_in_dim.129
  9.5 0.1 copy.179
  9.6 0.1 broadcast_in_dim.132
  9.8 0.2 convert_reduce_fusion
  10.2 0.2 copy.190
  10.5 0.2 mul.860
  10.7 1.1 %fusion.54 = (f32[512,32]{0,1:T(8,128)S(1)}, f32[512,32]{0,1:T(8,128)S(1)}, f32[512,32]{0,1:T(8,128)S(1)}, f32[512,32]{0,1:T(8,128)S(1)}, f32[512,32]{0,1:T(8,12...) fusion(s32[32]{0:T(128)S(1)} %iota_multiply_fusion, s32[512]{0:T(512)S(1)} %mul.860, ...), kind=kLoop, calls=%fused_computation.105 | loop fusion | flops 983040 | bytes 528512 | tf_op jit(solution)/shard_map/cos | solution.py:21
  11.7 1.9 %multiply_subtract_fusion.1 = (f32[512,32,32]{0,2,1:T(8,128)}, f32[512,32,32]{0,2,1:T(8,128)S(1)}) fusion(f32[512,32]{0,1:T(8,128)S(1)} %get-tuple-element.30, f32[512,32]{0,1:T(8,128)S(1)} %get-tuple-element.25, f32[512,32]{0,1:T(8,128)S(1)} %get-tuple-element.31, f32[512,32]{0,1:T(8,128)S(1)} %get-tuple-element.24), kind=kLoop, calls=%fused_computation.20 | loop fusion | flops 3145728 | bytes 4456448 | tf_op jit(solution)/shard_map/sub | solution.py:76
  13.7 2.9 %copy.191 = f32[1,1,512,1024]{3,2,1,0:T(8,128)} copy(f32[1,1,512,1024]{2,3,1,0:T(8,128)} %bitcast.87) | data formatting | bytes 4194304 | tf_op jit(solution)/shard_map/sub | solution.py:76
  16.6 1.9 %copy.193 = f32[1,1,512,1024]{3,2,1,0:T(8,128)} copy(f32[1,1,512,1024]{2,3,1,0:T(8,128)S(1)} %bitcast.85) | data formatting | bytes 4194304 | tf_op jit(solution)/shard_map/add | solution.py:77
  18.4 1.9 %multiply_subtract_fusion = (f32[512,32,32]{0,2,1:T(8,128)}, f32[512,32,32]{0,2,1:T(8,128)S(1)}) fusion(f32[512,32]{0,1:T(8,128)S(1)} %get-tuple-element.35, f32[512,32]{0,1:T(8,128)S(1)} %get-tuple-element.36, f32[512,32]{0,1:T(8,128)S(1)} %get-tuple-element.34, f32[512,32]{0,1:T(8,128)S(1)} %get-tuple-element.37), kind=kLoop, calls=%fused_computation.19 | loop fusion | flops 3145728 | bytes 4456448 | tf_op jit(solution)/shard_map/sub | solution.py:76
  20.4 3.0 %copy.192 = f32[1,1,512,1024]{3,2,1,0:T(8,128)} copy(f32[1,1,512,1024]{2,3,1,0:T(8,128)} %bitcast.88) | data formatting | bytes 4194304 | tf_op jit(solution)/shard_map/sub | solution.py:76
  23.3 1.8 %copy.194 = f32[1,1,512,1024]{3,2,1,0:T(8,128)} copy(f32[1,1,512,1024]{2,3,1,0:T(8,128)S(1)} %bitcast.86) | data formatting | bytes 4194304 | tf_op jit(solution)/shard_map/add | solution.py:77
  25.1 0.1 copy.173
  25.5 0.1 copy.187
  25.6 0.1 broadcast_in_dim.138
  25.8 0.1 broadcast_in_dim.134
  26.1 0.2 copy.189
  26.2 0.2 broadcast_in_dim_reshape.2
  26.4 0.2 copy.186
  26.6 0.2 mul.843
  26.9 0.1 reshape.1282
  27.0 0.1 eq.97
  27.2 0.3 copy.175
  27.6 0.3 copy.185
  28.3 0.3 copy.178
  28.6 0.3 fusion.55
  28.9 0.3 negate_multiply_fusion
  29.3 5.5 %add_multiply_fusion.1 = (f32[1,1,512,1024]{3,2,1,0:T(8,128)}, f32[1,1,512,1024]{3,2,1,0:T(8,128)}) fusion(f32[1,1,512,1024]{3,2,1,0:T(8,128)} %copy.192, f32[1,1,512,1024]{3,2,1,0:T(8,128)S(1)} %copy-done, f32[512]{0:T(512)S(1)} %broadcast_in_dim_reshape.2, f32[512]{0:T(512)S(1)} %broadcast_subtract_fusion, f32[1,1,512,1024]{3,2,1,0:T(8,128)} %copy.194, ...), kind=kLoop, calls=%fused_computation.18 | loop fusion | flops 4194304 | bytes 12587008 | tf_op jit(solution)/shard_map/mul | solution.py:83
  34.8 24.6 %all-to-all-done = f32[32,32,1024]{2,1,0:T(8,128)} async-done(((f32[32,32,1024]{2,1,0:T(8,128)}), f32[32,32,1024]{2,1,0:T(8,128)}, u32[]{:S(2)}, u32[]{:S(2)}) %all-to-all-start) | async-done | bytes 4194336 | tf_op jit(solution)/shard_map/all_to_all | solution.py:144
  59.5 10.0 %fusion.8 = f32[2,128,8,512,1]{3,2,1,0,4:T(8,128)S(1)} fusion(f32[1024,1024,1]{1,0,2:T(8,128)} %bitcast.7, f32[1,1,512,1024]{3,2,1,0:T(8,128)} %get-tuple-element.23, f32[1,1,512,1024]{3,2,1,0:T(8,128)} %get-tuple-element.22), kind=kOutput, calls=%fused_computation.9 | convolution fusion | flops 6443499520 | bytes 12582912 | tf_op jit(solution)/shard_map/trc,tpsr->tpcs/dot_general | solution.py:96
  69.5 5.1 %fusion.5 = f32[1,2,128,8,512]{2,4,1,3,0:T(8,128)S(1)} fusion(f32[2,128,8,512,1]{3,2,1,0,4:T(8,128)S(1)} %fusion.8, f32[1,128,2,128]{3,1,2,0:T(8,128)S(1)} %get-tuple-element.21, f32[1,128,2,128]{3,1,2,0:T(8,128)S(1)} %get-tuple-element.20), kind=kOutput, calls=%fused_computation.8 | convolution fusion | flops 1610678272 | bytes 8650752 | tf_op jit(solution)/shard_map/qkpn,tpnjs->tqkjs/dot_general | solution.py:100
  74.6 1.4 %subtract_reduce_fusion = (f32[128,512]{0,1:T(8,128)S(1)}, f32[128,512]{0,1:T(8,128)S(1)}) fusion(f32[1,2,128,8,512]{2,4,1,3,0:T(8,128)S(1)} %fusion.5, f32[128,8]{0,1:T(8,128)S(1)} %get-tuple-element.42, f32[8,512]{1,0:T(8,128)S(1)} %get-tuple-element.29, f32[128,8]{0,1:T(8,128)S(1)} %get-tuple-element.43, f32[8,512]{1,0:T(8,128)S(1)} %get-tuple-element.28), kind=kLoop, calls=%fused_computation.13 | loop fusion | flops 7208960 | bytes 4759552 | tf_op jit(solution)/shard_map/reduce_sum | solution.py:114
  76.1 2.5 %fusion.20 = (f32[32,4,4,1,128]{4,2,1,0,3:T(4,128)S(1)}, f32[32,4,4,1,128]{4,2,1,0,3:T(4,128)S(1)}) fusion(f32[32,4,4,1,128]{4,2,1,0,3:T(4,128)S(1)} %bitcast.91, f32[32,4,4]{2,1,0:T(4,128)S(1)} %copy.185, f32[32,4,4]{2,1,0:T(4,128)S(1)} %copy.183, s32[32,4,4]{2,1,0:T(4,128)S(1)} %copy.178, f32[32,4,4]{2,1,0:T(4,128)S(1)} %copy.175, ...), kind=kLoop, calls=%fused_computation.51 | loop fusion | flops 786432 | bytes 1056768 | tf_op jit(solution)/shard_map/mul | solution.py:118
  78.7 0.2 copy.198
  78.9 1.2 %copy.199 = f32[128,4,2,128]{3,2,1,0:T(2,128)} copy(f32[128,4,2,128]{3,0,2,1:T(8,128)S(1)} %bitcast.89) | data formatting | bytes 1048576 | tf_op jit(solution)/shard_map/reshape | solution.py:150
  80.1 8.8 %all-to-all-start.1 = ((f32[128,4,2,128]{3,2,1,0:T(2,128)}), f32[128,4,2,128]{3,2,1,0:T(2,128)S(1)}, u32[]{:S(2)}, u32[]{:S(2)}) async-start(f32[128,4,2,128]{3,2,1,0:T(2,128)} %copy.199), calls=%async_computation.1 | async-start | bytes 1048576 | tf_op jit(solution)/shard_map/all_to_all | solution.py:151
  88.9 0.2 add_reduce_fusion.1
  89.1 13.4 %all-to-all-done.1 = f32[128,4,2,128]{3,2,1,0:T(2,128)S(1)} async-done(((f32[128,4,2,128]{3,2,1,0:T(2,128)}), f32[128,4,2,128]{3,2,1,0:T(2,128)S(1)}, u32[]{:S(2)}, u32[]{:S(2)}) %all-to-all-start.1) | async-done | bytes 524320 | tf_op jit(solution)/shard_map/all_to_all | solution.py:151
  102.5 0.1 copy.200
  102.6 0.4 copy.202
  103.0 0.6 gather_fusion.1
  103.6 0.6 gather_fusion
  104.3 0.6 add.414
  (49 shorter events, 1.7 us)
Async XLA Ops:
  0.0 8.8 %copy-start.1 = (s32[512,8]{0,1:T(8,128)S(1)}, s32[512,8]{0,1:T(8,128)}, u32[]{:S(2)}) copy-start(s32[512,8]{0,1:T(8,128)} %param.8) | copy-start | bytes 49156
  0.0 9.2 %copy-start.2 = (s32[512,8]{0,1:T(8,128)S(1)}, s32[512,8]{0,1:T(8,128)}, u32[]{:S(2)}) copy-start(s32[512,8]{0,1:T(8,128)} %param.10) | copy-start | bytes 49156
  0.0 9.5 %copy-start.3 = (s32[512,8]{0,1:T(8,128)S(1)}, s32[512,8]{0,1:T(8,128)}, u32[]{:S(2)}) copy-start(s32[512,8]{0,1:T(8,128)} %param.9) | copy-start | bytes 49156
  0.0 59.5 %all-to-all-start = ((f32[32,32,1024]{2,1,0:T(8,128)}), f32[32,32,1024]{2,1,0:T(8,128)}, u32[]{:S(2)}, u32[]{:S(2)}) async-start(f32[32,32,1024]{2,1,0:T(8,128)} %param.7), calls=%async_computation | async-start | bytes 8388608 | tf_op jit(solution)/shard_map/all_to_all | solution.py:144
  23.3 1.8 %copy-start.4 = (f32[512,8]{0,1:T(8,128)S(1)}, f32[512,8]{0,1:T(8,128)}, u32[]{:S(2)}) copy-start(f32[512,8]{0,1:T(8,128)} %param.11) | copy-start | bytes 49156
  23.3 2.1 %copy-start.5 = (f32[512,8]{0,1:T(8,128)S(1)}, f32[512,8]{0,1:T(8,128)}, u32[]{:S(2)}) copy-start(f32[512,8]{0,1:T(8,128)} %param.12) | copy-start | bytes 49156
  23.3 2.5 %copy-start.6 = (f32[512]{0:T(512)S(1)}, f32[512]{0:T(512)}, u32[]{:S(2)}) copy-start(f32[512]{0:T(512)} %param.13) | copy-start | bytes 6148
  25.1 4.2 %copy-start = (f32[1,1,512,1024]{3,2,1,0:T(8,128)S(1)}, f32[1,1,512,1024]{3,2,1,0:T(8,128)}, u32[]{:S(2)}) copy-start(f32[1,1,512,1024]{3,2,1,0:T(8,128)} %copy.191) | copy-start | bytes 6291460
  80.1 22.4 %all-to-all-start.1 = ((f32[128,4,2,128]{3,2,1,0:T(2,128)}), f32[128,4,2,128]{3,2,1,0:T(2,128)S(1)}, u32[]{:S(2)}, u32[]{:S(2)}) async-start(f32[128,4,2,128]{3,2,1,0:T(2,128)} %copy.199), calls=%async_computation.1 | async-start | bytes 1048576 | tf_op jit(solution)/shard_map/all_to_all | solution.py:151

commit v14 on v9

--- a/solution.py
+++ b/solution.py
@@ -117,7 +117,7 @@
     o_im = jnp.swapaxes(o_im, 1, 2).reshape(own * n_s, LANES)
     parts = jnp.stack([scale * o_re, scale * o_im], axis=1)
     parts = parts.reshape(own, n_dev, 4, 2, LANES)
-    return jnp.swapaxes(parts, 0, 1).reshape(n_dev, own * 4, 2, LANES)
+    return jnp.swapaxes(parts, 0, 1).reshape(n_dev, own * 4 * 2, LANES)
 
 
 def gather_parts(recv, blk_plane, me, own, n_slab, n_img):

time: 104 us -> 103 us (level)
  waiting for transfers between devices: 40 us -> 38.8 us
    all_to_all x1, waiting for transfers between devices: 26.5 us -> 25.3 us  [on_device(): lax.all_to_all(volume, 'slab', split_axis=0, concat_axis=1, tiled=True)]
  transfers between devices with their start and end apart: 2 -> 2, of which waited for: 2 -> 2; matrix products, arithmetic and copies ran while one was open for 23% -> 25% of each run, Pallas kernels for 0% -> 0%
where the time goes in v14:
time: 103 us
  waiting for transfers between devices  38.8 us (38%)
  starting transfers between devices  17.5 us (17%)
  local copies, waits for them, and re-layouts  16.1 us (16%)
  other arithmetic  15.2 us (15%)
  matrix products  15.1 us (15%)
    all_to_all x1, waiting for transfers between devices, on_device(): lax.all_to_all(volume, 'slab', split_axis=0, concat_axis=1, tiled=True)  25.3 us
    all_to_all x1, waiting for transfers between devices, on_device(): lax.all_to_all(parts, ('slab', 'img'), split_axis=0, concat_axis=0, tiled...  13.5 us
    dot_general x1, matrix products, send_parts(): r_t = jnp.einsum('trc,tpsr->tpcs', piece, w_all, precision=MID)  9.97 us
    all_to_all x1, starting transfers between devices, on_device(): lax.all_to_all(volume, 'slab', split_axis=0, concat_axis=1, tiled=True)  8.78 us
    all_to_all x1, starting transfers between devices, on_device(): lax.all_to_all(parts, ('slab', 'img'), split_axis=0, concat_axis=0, tiled...  8.76 us
    sub x2, local copies, waits for them, and re-layouts, row_roots(): a_re[:, :, None] * b_re[:, None, :] - a_im[:, :, None] * b_im[:, None, :]  5.86 us
    mul x1, other arithmetic, send_parts(): w_re = ((1.0 - frac_y) * lo_re + frac_y * hi_re) * norm  5.49 us
    dot_general x1, matrix products, send_parts(): y_j = jnp.einsum('qkpn,tpnjs->tqkjs', w_j, r5, precision=MID)  5.14 us
  transfers between devices with their start and end apart: 2, of which 2 were waited for; matrix products, arithmetic and copies ran while one was open for 25% of the time, Pallas kernels for 0%

profile of v14, /device:TPU:1, one launch (start us, length us, event | category | flops | bytes accessed | tf_op | source)
XLA Modules:
  0.0 103.1 jit_solution(10031302315176876519)
XLA Ops:
  0.0 8.8 %all-to-all-start = ((f32[32,32,1024]{2,1,0:T(8,128)}), f32[32,32,1024]{2,1,0:T(8,128)}, u32[]{:S(2)}, u32[]{:S(2)}) async-start(f32[32,32,1024]{2,1,0:T(8,128)} %param.7), calls=%async_computation | async-start | bytes 8388608 | tf_op jit(solution)/shard_map/all_to_all | solution.py:144
  8.8 0.1 copy.103
  9.0 0.1 eq.87
  9.2 0.1 copy.111
  9.3 0.1 broadcast_in_dim.129
  9.5 0.1 copy.114
  9.6 0.1 broadcast_in_dim.132
  9.8 0.2 convert_reduce_fusion
  10.2 0.2 copy.116
  10.3 0.2 reshape.1504
  10.5 1.1 %fusion.51 = (f32[512,32]{0,1:T(8,128)S(1)}, f32[512,32]{0,1:T(8,128)S(1)}, f32[512,32]{0,1:T(8,128)S(1)}, f32[512,32]{0,1:T(8,128)S(1)}, f32[512,32]{0,1:T(8,12...) fusion(s32[32]{0:T(128)S(1)} %iota_multiply_fusion, s32[512]{0:T(512)S(1)} %reshape.1504, ...), kind=kLoop, calls=%fused_computation.104 | loop fusion | flops 983040 | bytes 528512 | tf_op jit(solution)/shard_map/cos | solution.py:21
  11.6 1.9 %multiply_subtract_fusion.1 = (f32[512,32,32]{0,2,1:T(8,128)}, f32[512,32,32]{0,2,1:T(8,128)S(1)}) fusion(f32[512,32]{0,1:T(8,128)S(1)} %get-tuple-element.30, f32[512,32]{0,1:T(8,128)S(1)} %get-tuple-element.25, f32[512,32]{0,1:T(8,128)S(1)} %get-tuple-element.31, f32[512,32]{0,1:T(8,128)S(1)} %get-tuple-element.24), kind=kLoop, calls=%fused_computation.20 | loop fusion | flops 3145728 | bytes 4456448 | tf_op jit(solution)/shard_map/sub | solution.py:76
  13.6 2.9 %copy.122 = f32[1,1,512,1024]{3,2,1,0:T(8,128)} copy(f32[1,1,512,1024]{2,3,1,0:T(8,128)} %bitcast.96) | data formatting | bytes 4194304 | tf_op jit(solution)/shard_map/sub | solution.py:76
  16.5 1.9 %copy.124 = f32[1,1,512,1024]{3,2,1,0:T(8,128)} copy(f32[1,1,512,1024]{2,3,1,0:T(8,128)S(1)} %bitcast.94) | data formatting | bytes 4194304 | tf_op jit(solution)/shard_map/add | solution.py:77
  18.3 1.9 %multiply_subtract_fusion = (f32[512,32,32]{0,2,1:T(8,128)}, f32[512,32,32]{0,2,1:T(8,128)S(1)}) fusion(f32[512,32]{0,1:T(8,128)S(1)} %get-tuple-element.35, f32[512,32]{0,1:T(8,128)S(1)} %get-tuple-element.36, f32[512,32]{0,1:T(8,128)S(1)} %get-tuple-element.34, f32[512,32]{0,1:T(8,128)S(1)} %get-tuple-element.37), kind=kLoop, calls=%fused_computation.19 | loop fusion | flops 3145728 | bytes 4456448 | tf_op jit(solution)/shard_map/sub | solution.py:76
  20.3 3.0 %copy.123 = f32[1,1,512,1024]{3,2,1,0:T(8,128)} copy(f32[1,1,512,1024]{2,3,1,0:T(8,128)} %bitcast.97) | data formatting | bytes 4194304 | tf_op jit(solution)/shard_map/sub | solution.py:76
  23.2 1.8 %copy.125 = f32[1,1,512,1024]{3,2,1,0:T(8,128)} copy(f32[1,1,512,1024]{2,3,1,0:T(8,128)S(1)} %bitcast.95) | data formatting | bytes 4194304 | tf_op jit(solution)/shard_map/add | solution.py:77
  25.0 0.1 copy.108
  25.2 0.1 broadcast_in_dim.125
  25.3 0.1 copy.119
  25.5 0.1 broadcast_in_dim.138
  25.7 0.1 broadcast_in_dim.134
  25.9 0.2 copy.121
  26.1 0.2 broadcast_in_dim_reshape.5
  26.3 0.2 copy.113
  26.5 0.2 broadcast_in_dim_reshape.4
  26.7 0.2 copy.110
  26.8 0.2 reshape.1503
  27.0 0.2 copy.107
  27.2 0.2 reshape.1502
  27.4 0.1 eq.99
  27.6 0.2 copy.118
  27.8 0.2 mul.841
  28.0 0.3 fusion.52
  28.3 0.3 negate_multiply_fusion
  28.7 5.5 %add_multiply_fusion.1 = (f32[1,1,512,1024]{3,2,1,0:T(8,128)}, f32[1,1,512,1024]{3,2,1,0:T(8,128)}) fusion(f32[1,1,512,1024]{3,2,1,0:T(8,128)} %copy.123, f32[1,1,512,1024]{3,2,1,0:T(8,128)S(1)} %copy-done, f32[512]{0:T(512)S(1)} %broadcast_in_dim_reshape.5, f32[512]{0:T(512)S(1)} %broadcast_subtract_fusion, f32[1,1,512,1024]{3,2,1,0:T(8,128)} %copy.125, ...), kind=kLoop, calls=%fused_computation.18 | loop fusion | flops 4194304 | bytes 12587008 | tf_op jit(solution)/shard_map/mul | solution.py:83
  34.2 25.3 %all-to-all-done = f32[32,32,1024]{2,1,0:T(8,128)} async-done(((f32[32,32,1024]{2,1,0:T(8,128)}), f32[32,32,1024]{2,1,0:T(8,128)}, u32[]{:S(2)}, u32[]{:S(2)}) %all-to-all-start) | async-done | bytes 4194336 | tf_op jit(solution)/shard_map/all_to_all | solution.py:144
  59.5 10.0 %fusion.8 = f32[2,128,8,512,1]{3,2,1,0,4:T(8,128)S(1)} fusion(f32[1024,1024,1]{1,0,2:T(8,128)} %bitcast.7, f32[1,1,512,1024]{3,2,1,0:T(8,128)} %get-tuple-element.23, f32[1,1,512,1024]{3,2,1,0:T(8,128)} %get-tuple-element.22), kind=kOutput, calls=%fused_computation.9 | convolution fusion | flops 6443499520 | bytes 12582912 | tf_op jit(solution)/shard_map/trc,tpsr->tpcs/dot_general | solution.py:96
  69.5 5.1 %fusion.5 = f32[1,2,128,8,512]{2,4,1,3,0:T(8,128)S(1)} fusion(f32[2,128,8,512,1]{3,2,1,0,4:T(8,128)S(1)} %fusion.8, f32[1,128,2,128]{3,1,2,0:T(8,128)S(1)} %get-tuple-element.19, f32[1,128,2,128]{3,1,2,0:T(8,128)S(1)} %get-tuple-element.18), kind=kOutput, calls=%fused_computation.8 | convolution fusion | flops 1610678272 | bytes 8650752 | tf_op jit(solution)/shard_map/qkpn,tpnjs->tqkjs/dot_general | solution.py:100
  74.6 1.4 %subtract_reduce_fusion = (f32[128,512]{0,1:T(8,128)S(1)}, f32[128,512]{0,1:T(8,128)S(1)}) fusion(f32[1,2,128,8,512]{2,4,1,3,0:T(8,128)S(1)} %fusion.5, f32[128,8]{0,1:T(8,128)S(1)} %get-tuple-element.42, f32[8,512]{1,0:T(8,128)S(1)} %get-tuple-element.29, f32[128,8]{0,1:T(8,128)S(1)} %get-tuple-element.43, f32[8,512]{1,0:T(8,128)S(1)} %get-tuple-element.28), kind=kLoop, calls=%fused_computation.13 | loop fusion | flops 7208960 | bytes 4759552 | tf_op jit(solution)/shard_map/reduce_sum | solution.py:114
  76.1 1.4 %bitcast_multiply_fusion.1 = (f32[512,1,128]{2,0,1:T(8,128)S(1)}, f32[512,1,128]{2,0,1:T(8,128)S(1)}) fusion(f32[128,512]{0,1:T(8,128)S(1)} %get-tuple-element.5, f32[512]{0:T(512)S(1)} %mul.841, f32[512]{0:T(512)S(1)} %fusion.68, s32[512]{0:T(512)S(1)} %broadcast_multiply_fusion.1, f32[512]{0:T(512)S(1)} %fusion.66, f32[128,512]{0,1:T(8,128)S(1)} %get-tuple-element.6), kind=kLoop, calls=%fused_computation.37 | loop fusion | flops 786432 | bytes 1056768 | tf_op jit(solution)/shard_map/mul | solution.py:118
  77.5 1.2 %copy.129 = f32[512,2,128]{2,1,0:T(2,128)} copy(f32[512,2,128]{2,0,1:T(8,128)S(1)} %pad_maximum_fusion) | data formatting | bytes 1048576 | tf_op jit(solution)/shard_map/stack | solution.py:118
  78.7 8.8 %all-to-all-start.1 = ((f32[128,8,128]{2,1,0:T(8,128)}), f32[128,8,128]{2,1,0:T(8,128)S(1)}, u32[]{:S(2)}, u32[]{:S(2)}) async-start(f32[128,8,128]{2,1,0:T(8,128)} %bitcast.28), calls=%async_computation.1 | async-start | bytes 1048576 | tf_op jit(solution)/shard_map/all_to_all | solution.py:149
  87.5 0.2 dynamic-slice_reduce_fusion
  87.7 13.5 %all-to-all-done.1 = f32[128,8,128]{2,1,0:T(8,128)S(1)} async-done(((f32[128,8,128]{2,1,0:T(8,128)}), f32[128,8,128]{2,1,0:T(8,128)S(1)}, u32[]{:S(2)}, u32[]{:S(2)}) %all-to-all-start.1) | async-done | bytes 524320 | tf_op jit(solution)/shard_map/all_to_all | solution.py:149
  101.3 0.6 gather_fusion.1
  101.9 0.6 gather_fusion
  102.5 0.6 add.460
  (41 shorter events, 0.9 us)
Async XLA Ops:
  0.0 8.8 %copy-start.1 = (s32[512,8]{0,1:T(8,128)S(1)}, s32[512,8]{0,1:T(8,128)}, u32[]{:S(2)}) copy-start(s32[512,8]{0,1:T(8,128)} %param.8) | copy-start | bytes 49156
  0.0 9.2 %copy-start.2 = (s32[512,8]{0,1:T(8,128)S(1)}, s32[512,8]{0,1:T(8,128)}, u32[]{:S(2)}) copy-start(s32[512,8]{0,1:T(8,128)} %param.10) | copy-start | bytes 49156
  0.0 9.5 %copy-start.3 = (s32[512,8]{0,1:T(8,128)S(1)}, s32[512,8]{0,1:T(8,128)}, u32[]{:S(2)}) copy-start(s32[512,8]{0,1:T(8,128)} %param.9) | copy-start | bytes 49156
  0.0 59.5 %all-to-all-start = ((f32[32,32,1024]{2,1,0:T(8,128)}), f32[32,32,1024]{2,1,0:T(8,128)}, u32[]{:S(2)}, u32[]{:S(2)}) async-start(f32[32,32,1024]{2,1,0:T(8,128)} %param.7), calls=%async_computation | async-start | bytes 8388608 | tf_op jit(solution)/shard_map/all_to_all | solution.py:144
  23.2 1.8 %copy-start.4 = (f32[512,8]{0,1:T(8,128)S(1)}, f32[512,8]{0,1:T(8,128)}, u32[]{:S(2)}) copy-start(f32[512,8]{0,1:T(8,128)} %param.11) | copy-start | bytes 49156
  23.2 2.1 %copy-start.5 = (f32[512,8]{0,1:T(8,128)S(1)}, f32[512,8]{0,1:T(8,128)}, u32[]{:S(2)}) copy-start(f32[512,8]{0,1:T(8,128)} %param.12) | copy-start | bytes 49156
  23.2 2.5 %copy-start.6 = (f32[512]{0:T(512)S(1)}, f32[512]{0:T(512)}, u32[]{:S(2)}) copy-start(f32[512]{0:T(512)} %param.13) | copy-start | bytes 6148
  25.0 3.7 %copy-start = (f32[1,1,512,1024]{3,2,1,0:T(8,128)S(1)}, f32[1,1,512,1024]{3,2,1,0:T(8,128)}, u32[]{:S(2)}) copy-start(f32[1,1,512,1024]{3,2,1,0:T(8,128)} %copy.122) | copy-start | bytes 6291460
  78.7 22.5 %all-to-all-start.1 = ((f32[128,8,128]{2,1,0:T(8,128)}), f32[128,8,128]{2,1,0:T(8,128)S(1)}, u32[]{:S(2)}, u32[]{:S(2)}) async-start(f32[128,8,128]{2,1,0:T(8,128)} %bitcast.28), calls=%async_computation.1 | async-start | bytes 1048576 | tf_op jit(solution)/shard_map/all_to_all | solution.py:149

commit v15 on v14

--- a/solution.py
+++ b/solution.py
@@ -133,7 +133,11 @@
         return src * slots + (q % own) * 4 + side * 2 + my_rank
 
     flat = recv.reshape(-1, 2, LANES)
-    return flat[place(mine, 0)] + flat[place(mine + 1, 1)]
+    rows = lax.iota(jnp.int32, flat.shape[0])[None, :]
+    pick = (rows == place(mine, 0)[:, None]).astype(jnp.float32) + (
+        rows == place(mine + 1, 1)[:, None]
+    ).astype(jnp.float32)
+    return jnp.einsum("kj,jpl->kpl", pick, flat, precision=lax.Precision.HIGHEST)
 
 
 def on_device(volume, blk_plane, blk_row, blk_col, frac_plane, frac_row, defocus):

time: 103 us -> 103 us (level)
    gather x2 -> x0, local copies, waits for them, and re-layouts: 1.21 us -> none  [gather_parts(): return flat[place(mine, 0)] + flat[place(mine + 1, 1)]]
where the time goes in v15:
time: 103 us; the launch traced here: 102 us
  waiting for transfers between devices  38.6 us (37%)
  starting transfers between devices  17.5 us (17%)
  local copies, waits for them, and re-layouts  15.7 us (15%)
  matrix products  15.5 us (15%)
  other arithmetic  14.6 us (14%)
    all_to_all x1, waiting for transfers between devices, on_device(): lax.all_to_all(volume, 'slab', split_axis=0, concat_axis=1, tiled=True)  25.3 us
    all_to_all x1, waiting for transfers between devices, on_device(): lax.all_to_all(parts, ('slab', 'img'), split_axis=0, concat_axis=0, tiled...  13.4 us
    dot_general x1, matrix products, send_parts(): r_t = jnp.einsum('trc,tpsr->tpcs', piece, w_all, precision=MID)  9.97 us
    all_to_all x1, starting transfers between devices, on_device(): lax.all_to_all(volume, 'slab', split_axis=0, concat_axis=1, tiled=True)  8.78 us
    all_to_all x1, starting transfers between devices, on_device(): lax.all_to_all(parts, ('slab', 'img'), split_axis=0, concat_axis=0, tiled...  8.76 us
    sub x2, local copies, waits for them, and re-layouts, row_roots(): a_re[:, :, None] * b_re[:, None, :] - a_im[:, :, None] * b_im[:, None, :]  5.86 us
    mul x1, other arithmetic, send_parts(): w_re = ((1.0 - frac_y) * lo_re + frac_y * hi_re) * norm  5.49 us
    dot_general x1, matrix products, send_parts(): y_j = jnp.einsum('qkpn,tpnjs->tqkjs', w_j, r5, precision=MID)  5.14 us
  transfers between devices with their start and end apart: 2, of which 2 were waited for; matrix products, arithmetic and copies ran while one was open for 25% of the time, Pallas kernels for 0%

profile of v15, /device:TPU:1, one launch (start us, length us, event | category | flops | bytes accessed | tf_op | source)
XLA Modules:
  0.0 102.3 jit_solution(8622950014853876279)
XLA Ops:
  0.0 8.8 %all-to-all-start = ((f32[32,32,1024]{2,1,0:T(8,128)}), f32[32,32,1024]{2,1,0:T(8,128)}, u32[]{:S(2)}, u32[]{:S(2)}) async-start(f32[32,32,1024]{2,1,0:T(8,128)} %param.7), calls=%async_computation | async-start | bytes 8388608 | tf_op jit(solution)/shard_map/all_to_all | solution.py:148
  8.8 0.1 copy.112
  9.0 0.1 reshape.1419
  9.2 0.1 copy.120
  9.3 0.1 broadcast_in_dim.130
  9.5 0.1 copy.123
  9.6 0.1 broadcast_in_dim.133
  9.8 0.2 convert_reduce_fusion
  10.2 0.2 copy.125
  10.3 0.2 reshape.1422
  10.5 1.1 %fusion.58 = (f32[512,32]{0,1:T(8,128)S(1)}, f32[512,32]{0,1:T(8,128)S(1)}, f32[512,32]{0,1:T(8,128)S(1)}, f32[512,32]{0,1:T(8,128)S(1)}, f32[512,32]{0,1:T(8,12...) fusion(s32[32]{0:T(128)S(1)} %iota_multiply_fusion, s32[512]{0:T(512)S(1)} %reshape.1422, ...), kind=kLoop, calls=%fused_computation.111 | loop fusion | flops 983040 | bytes 528512 | tf_op jit(solution)/shard_map/cos | solution.py:21
  11.6 1.9 %multiply_subtract_fusion.1 = (f32[512,32,32]{0,2,1:T(8,128)}, f32[512,32,32]{0,2,1:T(8,128)S(1)}) fusion(f32[512,32]{0,1:T(8,128)S(1)} %get-tuple-element.30, f32[512,32]{0,1:T(8,128)S(1)} %get-tuple-element.25, f32[512,32]{0,1:T(8,128)S(1)} %get-tuple-element.31, f32[512,32]{0,1:T(8,128)S(1)} %get-tuple-element.24), kind=kLoop, calls=%fused_computation.18 | loop fusion | flops 3145728 | bytes 4456448 | tf_op jit(solution)/shard_map/sub | solution.py:76
  13.6 2.9 %copy.131 = f32[1,1,512,1024]{3,2,1,0:T(8,128)} copy(f32[1,1,512,1024]{2,3,1,0:T(8,128)} %bitcast.75) | data formatting | bytes 4194304 | tf_op jit(solution)/shard_map/sub | solution.py:76
  16.5 1.9 %copy.133 = f32[1,1,512,1024]{3,2,1,0:T(8,128)} copy(f32[1,1,512,1024]{2,3,1,0:T(8,128)S(1)} %bitcast.73) | data formatting | bytes 4194304 | tf_op jit(solution)/shard_map/add | solution.py:77
  18.3 1.9 %multiply_subtract_fusion = (f32[512,32,32]{0,2,1:T(8,128)}, f32[512,32,32]{0,2,1:T(8,128)S(1)}) fusion(f32[512,32]{0,1:T(8,128)S(1)} %get-tuple-element.35, f32[512,32]{0,1:T(8,128)S(1)} %get-tuple-element.36, f32[512,32]{0,1:T(8,128)S(1)} %get-tuple-element.34, f32[512,32]{0,1:T(8,128)S(1)} %get-tuple-element.37), kind=kLoop, calls=%fused_computation.17 | loop fusion | flops 3145728 | bytes 4456448 | tf_op jit(solution)/shard_map/sub | solution.py:76
  20.3 3.0 %copy.132 = f32[1,1,512,1024]{3,2,1,0:T(8,128)} copy(f32[1,1,512,1024]{2,3,1,0:T(8,128)} %bitcast.76) | data formatting | bytes 4194304 | tf_op jit(solution)/shard_map/sub | solution.py:76
  23.2 1.8 %copy.134 = f32[1,1,512,1024]{3,2,1,0:T(8,128)} copy(f32[1,1,512,1024]{2,3,1,0:T(8,128)S(1)} %bitcast.74) | data formatting | bytes 4194304 | tf_op jit(solution)/shard_map/add | solution.py:77
  25.0 0.1 copy.117
  25.2 0.1 broadcast_in_dim.126
  25.3 0.1 copy.128
  25.5 0.1 broadcast_in_dim.139
  25.7 0.1 broadcast_in_dim.135
  25.9 0.2 copy.130
  26.1 0.2 broadcast_in_dim_reshape.5
  26.3 0.2 copy.122
  26.5 0.2 broadcast_in_dim_reshape.4
  26.7 0.2 copy.119
  26.8 0.2 reshape.1421
  27.0 0.2 copy.116
  27.2 0.2 reshape.1420
  27.4 0.1 eq.156
  27.6 0.2 copy.127
  27.8 0.2 mul.838
  28.0 0.3 fusion.61
  28.3 0.3 negate_multiply_fusion
  28.6 0.1 fusion.68
  28.7 5.5 %add_multiply_fusion.1 = (f32[1,1,512,1024]{3,2,1,0:T(8,128)}, f32[1,1,512,1024]{3,2,1,0:T(8,128)}) fusion(f32[1,1,512,1024]{3,2,1,0:T(8,128)} %copy.132, f32[1,1,512,1024]{3,2,1,0:T(8,128)S(1)} %copy-done, f32[512]{0:T(512)S(1)} %broadcast_in_dim_reshape.5, f32[512]{0:T(512)S(1)} %broadcast_subtract_fusion, f32[1,1,512,1024]{3,2,1,0:T(8,128)} %copy.134, ...), kind=kLoop, calls=%fused_computation.16 | loop fusion | flops 4194304 | bytes 12587008 | tf_op jit(solution)/shard_map/mul | solution.py:83
  34.2 25.3 %all-to-all-done = f32[32,32,1024]{2,1,0:T(8,128)} async-done(((f32[32,32,1024]{2,1,0:T(8,128)}), f32[32,32,1024]{2,1,0:T(8,128)}, u32[]{:S(2)}, u32[]{:S(2)}) %all-to-all-start) | async-done | bytes 4194336 | tf_op jit(solution)/shard_map/all_to_all | solution.py:148
  59.5 10.0 %fusion.8 = f32[2,128,8,512,1]{3,2,1,0,4:T(8,128)S(1)} fusion(f32[1024,1024,1]{1,0,2:T(8,128)} %bitcast.10, f32[1,1,512,1024]{3,2,1,0:T(8,128)} %get-tuple-element.23, f32[1,1,512,1024]{3,2,1,0:T(8,128)} %get-tuple-element.22), kind=kOutput, calls=%fused_computation.7 | convolution fusion | flops 6443499520 | bytes 12582912 | tf_op jit(solution)/shard_map/trc,tpsr->tpcs/dot_general | solution.py:96
  69.5 5.1 %fusion.5 = f32[1,2,128,8,512]{2,4,1,3,0:T(8,128)S(1)} fusion(f32[2,128,8,512,1]{3,2,1,0,4:T(8,128)S(1)} %fusion.8, f32[1,128,2,128]{3,1,2,0:T(8,128)S(1)} %get-tuple-element.17, f32[1,128,2,128]{3,1,2,0:T(8,128)S(1)} %get-tuple-element.16), kind=kOutput, calls=%fused_computation.6 | convolution fusion | flops 1610678272 | bytes 8650752 | tf_op jit(solution)/shard_map/qkpn,tpnjs->tqkjs/dot_general | solution.py:100
  74.6 1.4 %subtract_reduce_fusion = (f32[128,512]{0,1:T(8,128)S(1)}, f32[128,512]{0,1:T(8,128)S(1)}) fusion(f32[1,2,128,8,512]{2,4,1,3,0:T(8,128)S(1)} %fusion.5, f32[128,8]{0,1:T(8,128)S(1)} %get-tuple-element.42, f32[8,512]{1,0:T(8,128)S(1)} %get-tuple-element.29, f32[128,8]{0,1:T(8,128)S(1)} %get-tuple-element.43, f32[8,512]{1,0:T(8,128)S(1)} %get-tuple-element.28), kind=kLoop, calls=%fused_computation.11 | loop fusion | flops 7208960 | bytes 4759552 | tf_op jit(solution)/shard_map/reduce_sum | solution.py:114
  76.1 1.4 %bitcast_multiply_fusion.1 = (f32[512,1,128]{2,0,1:T(8,128)S(1)}, f32[512,1,128]{2,0,1:T(8,128)S(1)}) fusion(f32[128,512]{0,1:T(8,128)S(1)} %get-tuple-element.5, f32[512]{0:T(512)S(1)} %mul.838, f32[512]{0:T(512)S(1)} %fusion.86, s32[512]{0:T(512)S(1)} %broadcast_multiply_fusion.1, f32[512]{0:T(512)S(1)} %fusion.84, f32[128,512]{0,1:T(8,128)S(1)} %get-tuple-element.6), kind=kLoop, calls=%fused_computation.38 | loop fusion | flops 786432 | bytes 1056768 | tf_op jit(solution)/shard_map/mul | solution.py:118
  77.5 1.2 %copy.138 = f32[512,2,128]{2,1,0:T(2,128)} copy(f32[512,2,128]{2,0,1:T(8,128)S(1)} %pad_maximum_fusion) | data formatting | bytes 1048576 | tf_op jit(solution)/shard_map/stack | solution.py:118
  78.7 8.8 %all-to-all-start.1 = ((f32[128,8,128]{2,1,0:T(8,128)}), f32[128,8,128]{2,1,0:T(8,128)S(1)}, u32[]{:S(2)}, u32[]{:S(2)}) async-start(f32[128,8,128]{2,1,0:T(8,128)} %bitcast.31), calls=%async_computation.1 | async-start | bytes 1048576 | tf_op jit(solution)/shard_map/all_to_all | solution.py:153
  87.5 0.2 dynamic-slice_reduce_fusion
  87.9 13.4 %all-to-all-done.1 = f32[128,8,128]{2,1,0:T(8,128)S(1)} async-done(((f32[128,8,128]{2,1,0:T(8,128)}), f32[128,8,128]{2,1,0:T(8,128)S(1)}, u32[]{:S(2)}, u32[]{:S(2)}) %all-to-all-start.1) | async-done | bytes 524320 | tf_op jit(solution)/shard_map/all_to_all | solution.py:153
  101.3 0.4 fusion.9
  101.7 0.6 copy.140
  (42 shorter events, 1.0 us)
Async XLA Ops:
  0.0 8.8 %copy-start.1 = (s32[512,8]{0,1:T(8,128)S(1)}, s32[512,8]{0,1:T(8,128)}, u32[]{:S(2)}) copy-start(s32[512,8]{0,1:T(8,128)} %param.8) | copy-start | bytes 49156
  0.0 9.2 %copy-start.2 = (s32[512,8]{0,1:T(8,128)S(1)}, s32[512,8]{0,1:T(8,128)}, u32[]{:S(2)}) copy-start(s32[512,8]{0,1:T(8,128)} %param.10) | copy-start | bytes 49156
  0.0 9.5 %copy-start.3 = (s32[512,8]{0,1:T(8,128)S(1)}, s32[512,8]{0,1:T(8,128)}, u32[]{:S(2)}) copy-start(s32[512,8]{0,1:T(8,128)} %param.9) | copy-start | bytes 49156
  0.0 59.5 %all-to-all-start = ((f32[32,32,1024]{2,1,0:T(8,128)}), f32[32,32,1024]{2,1,0:T(8,128)}, u32[]{:S(2)}, u32[]{:S(2)}) async-start(f32[32,32,1024]{2,1,0:T(8,128)} %param.7), calls=%async_computation | async-start | bytes 8388608 | tf_op jit(solution)/shard_map/all_to_all | solution.py:148
  23.2 1.8 %copy-start.4 = (f32[512,8]{0,1:T(8,128)S(1)}, f32[512,8]{0,1:T(8,128)}, u32[]{:S(2)}) copy-start(f32[512,8]{0,1:T(8,128)} %param.11) | copy-start | bytes 49156
  23.2 2.1 %copy-start.5 = (f32[512,8]{0,1:T(8,128)S(1)}, f32[512,8]{0,1:T(8,128)}, u32[]{:S(2)}) copy-start(f32[512,8]{0,1:T(8,128)} %param.12) | copy-start | bytes 49156
  23.2 2.5 %copy-start.6 = (f32[512]{0:T(512)S(1)}, f32[512]{0:T(512)}, u32[]{:S(2)}) copy-start(f32[512]{0:T(512)} %param.13) | copy-start | bytes 6148
  25.0 3.7 %copy-start = (f32[1,1,512,1024]{3,2,1,0:T(8,128)S(1)}, f32[1,1,512,1024]{3,2,1,0:T(8,128)}, u32[]{:S(2)}) copy-start(f32[1,1,512,1024]{3,2,1,0:T(8,128)} %copy.131) | copy-start | bytes 6291460
  78.7 22.5 %all-to-all-start.1 = ((f32[128,8,128]{2,1,0:T(8,128)}), f32[128,8,128]{2,1,0:T(8,128)S(1)}, u32[]{:S(2)}, u32[]{:S(2)}) async-start(f32[128,8,128]{2,1,0:T(8,128)} %bitcast.31), calls=%async_computation.1 | async-start | bytes 1048576 | tf_op jit(solution)/shard_map/all_to_all | solution.py:153

commit v16 on v15

--- a/solution.py
+++ b/solution.py
@@ -115,9 +115,11 @@
     o_im = jnp.sum(g_re * y_im + g_im * y_re, axis=2)
     o_re = jnp.swapaxes(o_re, 1, 2).reshape(own * n_s, LANES)
     o_im = jnp.swapaxes(o_im, 1, 2).reshape(own * n_s, LANES)
-    parts = jnp.stack([scale * o_re, scale * o_im], axis=1)
-    parts = parts.reshape(own, n_dev, 4, 2, LANES)
-    return jnp.swapaxes(parts, 0, 1).reshape(n_dev, own * 4 * 2, LANES)
+    p_re = jnp.swapaxes((scale * o_re).reshape(own, n_dev, 4, LANES), 0, 1)
+    p_im = jnp.swapaxes((scale * o_im).reshape(own, n_dev, 4, LANES), 0, 1)
+    return jnp.concatenate(
+        [p_re.reshape(n_dev, own * 4, LANES), p_im.reshape(n_dev, own * 4, LANES)], axis=1
+    )
 
 
 def gather_parts(recv, blk_plane, me, own, n_slab, n_img):
@@ -132,12 +134,14 @@
         src = (holder % n_slab) * n_img + holder // n_slab
         return src * slots + (q % own) * 4 + side * 2 + my_rank
 
-    flat = recv.reshape(-1, 2, LANES)
-    rows = lax.iota(jnp.int32, flat.shape[0])[None, :]
+    n_src = recv.shape[0]
+    split = recv.reshape(n_src, 2, slots, LANES)
+    rows = lax.iota(jnp.int32, n_src * slots)[None, :]
     pick = (rows == place(mine, 0)[:, None]).astype(jnp.float32) + (
         rows == place(mine + 1, 1)[:, None]
     ).astype(jnp.float32)
-    return jnp.einsum("kj,jpl->kpl", pick, flat, precision=lax.Precision.HIGHEST)
+    pick = pick.reshape(-1, n_src, slots)
+    return jnp.einsum("kas,apsl->kpl", pick, split, precision=lax.Precision.HIGHEST)
 
 
 def on_device(volume, blk_plane, blk_row, blk_col, frac_plane, frac_row, defocus):

time: 103 us -> 104 us (level)
  other arithmetic: 14.6 us -> 16.6 us
  local copies, waits for them, and re-layouts: 15.7 us -> 13.9 us
    another operation x2 -> x0, local copies, waits for them, and re-layouts: 1.39 us -> none  [the longest x1 1.19 us: send_parts(): parts = jnp.stack([scale * o_re, scale * o_im], axis=1)]
    add x2, local copies, waits for them, and re-layouts: 3.66 us -> 4.79 us  [row_roots(): a_re[:, :, None] * b_im[:, None, :] + a_im[:, :, None] * b_re[:, None, :]]
    sub x2, local copies, waits for them, and re-layouts: 5.86 us -> 4.73 us  [row_roots(): a_re[:, :, None] * b_re[:, None, :] - a_im[:, :, None] * b_im[:, None, :]]
    mul x1, other arithmetic: 1.42 us -> 2.55 us  [send_parts(): p_re = jnp.swapaxes((scale * o_re).reshape(own, n_dev, 4, LANES), 0, 1)]
  transfers between devices with their start and end apart: 2 -> 2, of which waited for: 2 -> 2; matrix products, arithmetic and copies ran while one was open for 25% -> 24% of each run, Pallas kernels for 0% -> 0%
where the time goes in v16:
time: 104 us; the launch traced here: 103 us
  waiting for transfers between devices  39.3 us (38%)
  starting transfers between devices  17.5 us (17%)
  other arithmetic  16.6 us (16%)
  matrix products  15.5 us (15%)
  local copies, waits for them, and re-layouts  13.9 us (13%)
    all_to_all x1, waiting for transfers between devices, on_device(): lax.all_to_all(volume, 'slab', split_axis=0, concat_axis=1, tiled=True)  25.9 us
    all_to_all x1, waiting for transfers between devices, on_device(): lax.all_to_all(parts, ('slab', 'img'), split_axis=0, concat_axis=0, tiled...  13.4 us
    dot_general x1, matrix products, send_parts(): r_t = jnp.einsum('trc,tpsr->tpcs', piece, w_all, precision=MID)  9.97 us
    all_to_all x1, starting transfers between devices, on_device(): lax.all_to_all(volume, 'slab', split_axis=0, concat_axis=1, tiled=True)  8.78 us
    all_to_all x1, starting transfers between devices, on_device(): lax.all_to_all(parts, ('slab', 'img'), split_axis=0, concat_axis=0, tiled...  8.76 us
    mul x1, other arithmetic, send_parts(): w_re = ((1.0 - frac_y) * lo_re + frac_y * hi_re) * norm  5.5 us
    dot_general x1, matrix products, send_parts(): y_j = jnp.einsum('qkpn,tpnjs->tqkjs', w_j, r5, precision=MID)  5.14 us
    add x2, local copies, waits for them, and re-layouts, row_roots(): a_re[:, :, None] * b_im[:, None, :] + a_im[:, :, None] * b_re[:, None, :]  4.79 us
  transfers between devices with their start and end apart: 2, of which 2 were waited for; matrix products, arithmetic and copies ran while one was open for 24% of the time, Pallas kernels for 0%

profile of v16, /device:TPU:1, one launch (start us, length us, event | category | flops | bytes accessed | tf_op | source)
XLA Modules:
  0.0 103.2 jit_solution(871615159604618341)
XLA Ops:
  0.0 8.8 %all-to-all-start = ((f32[32,32,1024]{2,1,0:T(8,128)}), f32[32,32,1024]{2,1,0:T(8,128)}, u32[]{:S(2)}, u32[]{:S(2)}) async-start(f32[32,32,1024]{2,1,0:T(8,128)} %param.7), calls=%async_computation | async-start | bytes 8388608 | tf_op jit(solution)/shard_map/all_to_all | solution.py:152
  8.8 0.1 copy.79
  9.0 0.1 reshape.1274
  9.2 0.1 copy.86
  9.3 0.1 broadcast_in_dim.130
  9.5 0.1 copy.89
  9.6 0.1 broadcast_in_dim.133
  9.8 0.2 convert_reduce_fusion
  10.2 0.2 copy.98
  10.3 0.2 mul.830
  10.5 1.1 %fusion.59 = (f32[512,32]{0,1:T(8,128)S(1)}, f32[512,32]{0,1:T(8,128)S(1)}, f32[512,32]{0,1:T(8,128)S(1)}, f32[512,32]{0,1:T(8,128)S(1)}, f32[512,32]{0,1:T(8,12...) fusion(s32[32]{0:T(128)S(1)} %iota_multiply_fusion, s32[512]{0:T(512)S(1)} %mul.830, ...), kind=kLoop, calls=%fused_computation.108 | loop fusion | flops 983040 | bytes 528512 | tf_op jit(solution)/shard_map/cos | solution.py:21
  11.6 1.9 %multiply_subtract_fusion.1 = (f32[512,32,32]{0,2,1:T(8,128)S(1)}, f32[512,32,32]{0,2,1:T(8,128)}) fusion(f32[512,32]{0,1:T(8,128)S(1)} %get-tuple-element.30, f32[512,32]{0,1:T(8,128)S(1)} %get-tuple-element.25, f32[512,32]{0,1:T(8,128)S(1)} %get-tuple-element.31, f32[512,32]{0,1:T(8,128)S(1)} %get-tuple-element.24), kind=kLoop, calls=%fused_computation.18 | loop fusion | flops 3145728 | bytes 4456448 | tf_op jit(solution)/shard_map/sub | solution.py:76
  13.6 2.9 %copy.101 = f32[1,1,512,1024]{3,2,1,0:T(8,128)} copy(f32[1,1,512,1024]{2,3,1,0:T(8,128)} %bitcast.82) | data formatting | bytes 4194304 | tf_op jit(solution)/shard_map/add | solution.py:77
  16.5 1.9 %copy.99 = f32[1,1,512,1024]{3,2,1,0:T(8,128)} copy(f32[1,1,512,1024]{2,3,1,0:T(8,128)S(1)} %bitcast.80) | data formatting | bytes 4194304 | tf_op jit(solution)/shard_map/sub | solution.py:76
  18.3 2.0 %multiply_subtract_fusion = (f32[512,32,32]{0,2,1:T(8,128)}, f32[512,32,32]{0,2,1:T(8,128)S(1)}) fusion(f32[512,32]{0,1:T(8,128)S(1)} %get-tuple-element.35, f32[512,32]{0,1:T(8,128)S(1)} %get-tuple-element.36, f32[512,32]{0,1:T(8,128)S(1)} %get-tuple-element.34, f32[512,32]{0,1:T(8,128)S(1)} %get-tuple-element.37), kind=kLoop, calls=%fused_computation.17 | loop fusion | flops 3145728 | bytes 4456448 | tf_op jit(solution)/shard_map/sub | solution.py:76
  20.4 2.9 %copy.100 = f32[1,1,512,1024]{3,2,1,0:T(8,128)} copy(f32[1,1,512,1024]{2,3,1,0:T(8,128)} %bitcast.83) | data formatting | bytes 4194304 | tf_op jit(solution)/shard_map/sub | solution.py:76
  23.2 1.9 %copy.102 = f32[1,1,512,1024]{3,2,1,0:T(8,128)} copy(f32[1,1,512,1024]{2,3,1,0:T(8,128)S(1)} %bitcast.81) | data formatting | bytes 4194304 | tf_op jit(solution)/shard_map/add | solution.py:77
  25.1 0.1 copy.83
  25.3 0.1 broadcast_in_dim.126
  25.4 0.1 copy.95
  25.6 0.1 broadcast_in_dim.139
  25.8 0.1 broadcast_in_dim.135
  26.0 0.2 copy.97
  26.2 0.2 broadcast_in_dim_reshape.2
  26.4 0.2 copy.94
  26.6 0.2 mul.813
  26.8 0.1 copy.85
  27.0 0.1 copy.93
  27.1 0.1 copy.88
  27.2 0.1 copy.91
  27.4 0.3 fusion.63
  27.6 0.3 negate_multiply_fusion
  28.0 0.1 fusion.70
  28.1 5.5 %add_multiply_fusion.1 = (f32[1,1,512,1024]{3,2,1,0:T(8,128)}, f32[1,1,512,1024]{3,2,1,0:T(8,128)}) fusion(f32[1,1,512,1024]{3,2,1,0:T(8,128)} %copy.100, f32[1,1,512,1024]{3,2,1,0:T(8,128)} %copy.99, f32[512]{0:T(512)S(1)} %broadcast_in_dim_reshape.2, f32[512]{0:T(512)S(1)} %broadcast_subtract_fusion, f32[1,1,512,1024]{3,2,1,0:T(8,128)} %copy.102, ...), kind=kLoop, calls=%fused_computation.16 | loop fusion | flops 4194304 | bytes 12587008 | tf_op jit(solution)/shard_map/mul | solution.py:83
  33.6 25.9 %all-to-all-done = f32[32,32,1024]{2,1,0:T(8,128)} async-done(((f32[32,32,1024]{2,1,0:T(8,128)}), f32[32,32,1024]{2,1,0:T(8,128)}, u32[]{:S(2)}, u32[]{:S(2)}) %all-to-all-start) | async-done | bytes 4194336 | tf_op jit(solution)/shard_map/all_to_all | solution.py:152
  59.5 10.0 %fusion.8 = f32[2,128,8,512,1]{3,2,1,0,4:T(8,128)S(1)} fusion(f32[1024,1024,1]{1,0,2:T(8,128)} %bitcast.13, f32[1,1,512,1024]{3,2,1,0:T(8,128)} %get-tuple-element.23, f32[1,1,512,1024]{3,2,1,0:T(8,128)} %get-tuple-element.22), kind=kOutput, calls=%fused_computation.7 | convolution fusion | flops 6443499520 | bytes 12582912 | tf_op jit(solution)/shard_map/trc,tpsr->tpcs/dot_general | solution.py:96
  69.5 5.1 %fusion.5 = f32[1,2,128,8,512]{2,4,1,3,0:T(8,128)S(1)} fusion(f32[2,128,8,512,1]{3,2,1,0,4:T(8,128)S(1)} %fusion.8, f32[1,128,2,128]{3,1,2,0:T(8,128)S(1)} %get-tuple-element.19, f32[1,128,2,128]{3,1,2,0:T(8,128)S(1)} %get-tuple-element.18), kind=kOutput, calls=%fused_computation.6 | convolution fusion | flops 1610678272 | bytes 8650752 | tf_op jit(solution)/shard_map/qkpn,tpnjs->tqkjs/dot_general | solution.py:100
  74.6 1.4 %subtract_reduce_fusion = (f32[128,512]{0,1:T(8,128)S(1)}, f32[128,512]{0,1:T(8,128)S(1)}) fusion(f32[1,2,128,8,512]{2,4,1,3,0:T(8,128)S(1)} %fusion.5, f32[128,8]{0,1:T(8,128)S(1)} %get-tuple-element.42, f32[8,512]{1,0:T(8,128)S(1)} %get-tuple-element.29, f32[128,8]{0,1:T(8,128)S(1)} %get-tuple-element.43, f32[8,512]{1,0:T(8,128)S(1)} %get-tuple-element.28), kind=kLoop, calls=%fused_computation.11 | loop fusion | flops 7208960 | bytes 4759552 | tf_op jit(solution)/shard_map/reduce_sum | solution.py:114
  76.1 2.5 %fusion.20 = (f32[128,4,128]{2,1,0:T(4,128)S(1)}, f32[128,4,128]{2,1,0:T(4,128)S(1)}) fusion(f32[128,4,128]{2,1,0:T(4,128)S(1)} %bitcast.85, f32[128,4]{1,0:T(8,128)S(1)} %copy.93, f32[128,4]{1,0:T(8,128)S(1)} %copy.91, s32[128,4]{1,0:T(8,128)S(1)} %copy.88, f32[128,4]{1,0:T(8,128)S(1)} %copy.85, f32[128,4,128]{2,1,0:T(4,128)S(1)} %bitcast.86), kind=kLoop, calls=%fused_computation.50 | loop fusion | flops 786432 | bytes 1056768 | tf_op jit(solution)/shard_map/mul | solution.py:118
  78.6 0.9 pad_maximum_fusion
  79.5 8.8 %all-to-all-start.1 = ((f32[128,8,128]{2,1,0:T(8,128)}), f32[128,8,128]{2,1,0:T(8,128)S(1)}, u32[]{:S(2)}, u32[]{:S(2)}) async-start(f32[128,8,128]{2,1,0:T(8,128)} %pad_maximum_fusion), calls=%async_computation.1 | async-start | bytes 1048576 | tf_op jit(solution)/shard_map/all_to_all | solution.py:157
  88.3 0.2 dynamic-slice_reduce_fusion
  88.5 0.1 squeeze.13
  88.6 0.1 squeeze.12
  88.7 13.4 %all-to-all-done.1 = f32[128,8,128]{2,1,0:T(8,128)S(1)} async-done(((f32[128,8,128]{2,1,0:T(8,128)}), f32[128,8,128]{2,1,0:T(8,128)S(1)}, u32[]{:S(2)}, u32[]{:S(2)}) %all-to-all-start.1) | async-done | bytes 524320 | tf_op jit(solution)/shard_map/all_to_all | solution.py:157
  102.0 0.1 copy.106
  102.2 0.4 convolution_bitcast_fusion
  102.6 0.6 copy.107
  (42 shorter events, 0.8 us)
Async XLA Ops:
  0.0 8.8 %copy-start.1 = (s32[512,8]{0,1:T(8,128)S(1)}, s32[512,8]{0,1:T(8,128)}, u32[]{:S(2)}) copy-start(s32[512,8]{0,1:T(8,128)} %param.8) | copy-start | bytes 49156
  0.0 9.2 %copy-start.2 = (s32[512,8]{0,1:T(8,128)S(1)}, s32[512,8]{0,1:T(8,128)}, u32[]{:S(2)}) copy-start(s32[512,8]{0,1:T(8,128)} %param.10) | copy-start | bytes 49156
  0.0 9.5 %copy-start.3 = (s32[512,8]{0,1:T(8,128)S(1)}, s32[512,8]{0,1:T(8,128)}, u32[]{:S(2)}) copy-start(s32[512,8]{0,1:T(8,128)} %param.9) | copy-start | bytes 49156
  0.0 59.5 %all-to-all-start = ((f32[32,32,1024]{2,1,0:T(8,128)}), f32[32,32,1024]{2,1,0:T(8,128)}, u32[]{:S(2)}, u32[]{:S(2)}) async-start(f32[32,32,1024]{2,1,0:T(8,128)} %param.7), calls=%async_computation | async-start | bytes 8388608 | tf_op jit(solution)/shard_map/all_to_all | solution.py:152
  23.2 1.9 %copy-start.4 = (f32[512,8]{0,1:T(8,128)S(1)}, f32[512,8]{0,1:T(8,128)}, u32[]{:S(2)}) copy-start(f32[512,8]{0,1:T(8,128)} %param.11) | copy-start | bytes 49156
  23.2 2.2 %copy-start.5 = (f32[512,8]{0,1:T(8,128)S(1)}, f32[512,8]{0,1:T(8,128)}, u32[]{:S(2)}) copy-start(f32[512,8]{0,1:T(8,128)} %param.12) | copy-start | bytes 49156
  23.2 2.5 %copy-start.6 = (f32[512]{0:T(512)S(1)}, f32[512]{0:T(512)}, u32[]{:S(2)}) copy-start(f32[512]{0:T(512)} %param.13) | copy-start | bytes 6148
  25.1 2.9 %copy-start = (f32[1,1,512,1024]{3,2,1,0:T(8,128)S(1)}, f32[1,1,512,1024]{3,2,1,0:T(8,128)}, u32[]{:S(2)}) copy-start(f32[1,1,512,1024]{3,2,1,0:T(8,128)} %copy.101) | copy-start | bytes 6291460
  79.5 22.5 %all-to-all-start.1 = ((f32[128,8,128]{2,1,0:T(8,128)}), f32[128,8,128]{2,1,0:T(8,128)S(1)}, u32[]{:S(2)}, u32[]{:S(2)}) async-start(f32[128,8,128]{2,1,0:T(8,128)} %pad_maximum_fusion), calls=%async_computation.1 | async-start | bytes 1048576 | tf_op jit(solution)/shard_map/all_to_all | solution.py:157

commit v17 on v15

--- a/solution.py
+++ b/solution.py
@@ -111,11 +111,12 @@
     t_im = t_im[None, :, :, None]
     g_re = e_re * t_re - e_im * t_im
     g_im = e_re * t_im + e_im * t_re
-    o_re = jnp.sum(g_re * y_re - g_im * y_im, axis=2)
-    o_im = jnp.sum(g_re * y_im + g_im * y_re, axis=2)
+    scale_t = jnp.swapaxes(scale.reshape(own, n_s, LANES), 1, 2)
+    o_re = jnp.sum(g_re * y_re - g_im * y_im, axis=2) * scale_t
+    o_im = jnp.sum(g_re * y_im + g_im * y_re, axis=2) * scale_t
     o_re = jnp.swapaxes(o_re, 1, 2).reshape(own * n_s, LANES)
     o_im = jnp.swapaxes(o_im, 1, 2).reshape(own * n_s, LANES)
-    parts = jnp.stack([scale * o_re, scale * o_im], axis=1)
+    parts = jnp.stack([o_re, o_im], axis=1)
     parts = parts.reshape(own, n_dev, 4, 2, LANES)
     return jnp.swapaxes(parts, 0, 1).reshape(n_dev, own * 4 * 2, LANES)
 

time: 103 us -> 103 us (level)
  other arithmetic: 14.6 us -> 15.8 us
  local copies, waits for them, and re-layouts: 15.7 us -> 14.5 us
    another operation x2 -> x0, local copies, waits for them, and re-layouts: 1.39 us -> none  [the longest x1 1.19 us: send_parts(): parts = jnp.stack([scale * o_re, scale * o_im], axis=1)]
    another operation x1, other arithmetic: 0.04 us -> 1.26 us  [send_parts(): parts = jnp.stack([o_re, o_im], axis=1)]
where the time goes in v17:
time: 103 us; the launch traced here: 102 us
  waiting for transfers between devices  38.6 us (37%)
  starting transfers between devices  17.5 us (17%)
  other arithmetic  15.8 us (15%)
  matrix products  15.5 us (15%)
  local copies, waits for them, and re-layouts  14.5 us (14%)
    all_to_all x1, waiting for transfers between devices, on_device(): lax.all_to_all(volume, 'slab', split_axis=0, concat_axis=1, tiled=True)  25.3 us
    all_to_all x1, waiting for transfers between devices, on_device(): lax.all_to_all(parts, ('slab', 'img'), split_axis=0, concat_axis=0, tiled...  13.4 us
    dot_general x1, matrix products, send_parts(): r_t = jnp.einsum('trc,tpsr->tpcs', piece, w_all, precision=MID)  9.97 us
    all_to_all x1, starting transfers between devices, on_device(): lax.all_to_all(volume, 'slab', split_axis=0, concat_axis=1, tiled=True)  8.78 us
    all_to_all x1, starting transfers between devices, on_device(): lax.all_to_all(parts, ('slab', 'img'), split_axis=0, concat_axis=0, tiled...  8.76 us
    sub x2, local copies, waits for them, and re-layouts, row_roots(): a_re[:, :, None] * b_re[:, None, :] - a_im[:, :, None] * b_im[:, None, :]  5.86 us
    mul x1, other arithmetic, send_parts(): w_re = ((1.0 - frac_y) * lo_re + frac_y * hi_re) * norm  5.49 us
    dot_general x1, matrix products, send_parts(): y_j = jnp.einsum('qkpn,tpnjs->tqkjs', w_j, r5, precision=MID)  5.14 us
  transfers between devices with their start and end apart: 2, of which 2 were waited for; matrix products, arithmetic and copies ran while one was open for 25% of the time, Pallas kernels for 0%

profile of v17, /device:TPU:1, one launch (start us, length us, event | category | flops | bytes accessed | tf_op | source)
XLA Modules:
  0.0 102.3 jit_solution(657977156146307332)
XLA Ops:
  0.0 8.8 %all-to-all-start = ((f32[32,32,1024]{2,1,0:T(8,128)}), f32[32,32,1024]{2,1,0:T(8,128)}, u32[]{:S(2)}, u32[]{:S(2)}) async-start(f32[32,32,1024]{2,1,0:T(8,128)} %param.7), calls=%async_computation | async-start | bytes 8388608 | tf_op jit(solution)/shard_map/all_to_all | solution.py:149
  8.8 0.1 copy.58
  9.0 0.1 reshape.1323
  9.2 0.1 copy.62
  9.3 0.1 broadcast_in_dim.125
  9.5 0.1 copy.68
  9.6 0.1 broadcast_in_dim.131
  9.8 0.2 convert_reduce_fusion
  10.2 0.2 copy.70
  10.3 0.2 mul.829
  10.5 1.1 %fusion.58 = (f32[512,32]{0,1:T(8,128)S(1)}, f32[512,32]{0,1:T(8,128)S(1)}, f32[512,32]{0,1:T(8,128)S(1)}, f32[512,32]{0,1:T(8,128)S(1)}, f32[512,32]{0,1:T(8,12...) fusion(s32[32]{0:T(128)S(1)} %iota_multiply_fusion, s32[512]{0:T(512)S(1)} %mul.829, ...), kind=kLoop, calls=%fused_computation.111 | loop fusion | flops 983040 | bytes 528512 | tf_op jit(solution)/shard_map/cos | solution.py:21
  11.6 1.9 %multiply_subtract_fusion.1 = (f32[512,32,32]{0,2,1:T(8,128)}, f32[512,32,32]{0,2,1:T(8,128)S(1)}) fusion(f32[512,32]{0,1:T(8,128)S(1)} %get-tuple-element.30, f32[512,32]{0,1:T(8,128)S(1)} %get-tuple-element.25, f32[512,32]{0,1:T(8,128)S(1)} %get-tuple-element.31, f32[512,32]{0,1:T(8,128)S(1)} %get-tuple-element.24), kind=kLoop, calls=%fused_computation.18 | loop fusion | flops 3145728 | bytes 4456448 | tf_op jit(solution)/shard_map/sub | solution.py:76
  13.6 2.9 %copy.71 = f32[1,1,512,1024]{3,2,1,0:T(8,128)} copy(f32[1,1,512,1024]{2,3,1,0:T(8,128)} %bitcast.75) | data formatting | bytes 4194304 | tf_op jit(solution)/shard_map/sub | solution.py:76
  16.5 1.9 %copy.73 = f32[1,1,512,1024]{3,2,1,0:T(8,128)} copy(f32[1,1,512,1024]{2,3,1,0:T(8,128)S(1)} %bitcast.73) | data formatting | bytes 4194304 | tf_op jit(solution)/shard_map/add | solution.py:77
  18.3 1.9 %multiply_subtract_fusion = (f32[512,32,32]{0,2,1:T(8,128)}, f32[512,32,32]{0,2,1:T(8,128)S(1)}) fusion(f32[512,32]{0,1:T(8,128)S(1)} %get-tuple-element.35, f32[512,32]{0,1:T(8,128)S(1)} %get-tuple-element.36, f32[512,32]{0,1:T(8,128)S(1)} %get-tuple-element.34, f32[512,32]{0,1:T(8,128)S(1)} %get-tuple-element.37), kind=kLoop, calls=%fused_computation.17 | loop fusion | flops 3145728 | bytes 4456448 | tf_op jit(solution)/shard_map/sub | solution.py:76
  20.3 3.0 %copy.72 = f32[1,1,512,1024]{3,2,1,0:T(8,128)} copy(f32[1,1,512,1024]{2,3,1,0:T(8,128)} %bitcast.76) | data formatting | bytes 4194304 | tf_op jit(solution)/shard_map/sub | solution.py:76
  23.2 1.8 %copy.74 = f32[1,1,512,1024]{3,2,1,0:T(8,128)} copy(f32[1,1,512,1024]{2,3,1,0:T(8,128)S(1)} %bitcast.74) | data formatting | bytes 4194304 | tf_op jit(solution)/shard_map/add | solution.py:77
  25.0 0.1 copy.65
  25.2 0.1 broadcast_in_dim.128
  25.3 0.1 copy.79
  25.5 0.1 broadcast_in_dim.134
  25.7 0.1 broadcast_in_dim.137
  25.9 0.2 copy.67
  26.1 0.2 broadcast_in_dim_reshape.2
  26.3 0.2 copy.64
  26.5 0.2 mul.812
  26.7 0.2 copy.81
  26.8 0.2 reshape.1328
  27.0 0.2 copy.78
  27.2 0.2 reshape.1327
  27.4 0.1 eq.156
  27.6 0.2 copy.83
  27.8 0.2 mul.885
  28.0 0.3 fusion.61
  28.3 0.3 negate_multiply_fusion
  28.6 0.1 fusion.68
  28.7 5.5 %add_multiply_fusion.1 = (f32[1,1,512,1024]{3,2,1,0:T(8,128)}, f32[1,1,512,1024]{3,2,1,0:T(8,128)}) fusion(f32[1,1,512,1024]{3,2,1,0:T(8,128)} %copy.72, f32[1,1,512,1024]{3,2,1,0:T(8,128)S(1)} %copy-done, f32[512]{0:T(512)S(1)} %broadcast_in_dim_reshape.2, f32[512]{0:T(512)S(1)} %broadcast_subtract_fusion, f32[1,1,512,1024]{3,2,1,0:T(8,128)} %copy.74, ...), kind=kLoop, calls=%fused_computation.16 | loop fusion | flops 4194304 | bytes 12587008 | tf_op jit(solution)/shard_map/mul | solution.py:83
  34.2 25.3 %all-to-all-done = f32[32,32,1024]{2,1,0:T(8,128)} async-done(((f32[32,32,1024]{2,1,0:T(8,128)}), f32[32,32,1024]{2,1,0:T(8,128)}, u32[]{:S(2)}, u32[]{:S(2)}) %all-to-all-start) | async-done | bytes 4194336 | tf_op jit(solution)/shard_map/all_to_all | solution.py:149
  59.5 10.0 %fusion.8 = f32[2,128,8,512,1]{3,2,1,0,4:T(8,128)S(1)} fusion(f32[1024,1024,1]{1,0,2:T(8,128)} %bitcast.9, f32[1,1,512,1024]{3,2,1,0:T(8,128)} %get-tuple-element.23, f32[1,1,512,1024]{3,2,1,0:T(8,128)} %get-tuple-element.22), kind=kOutput, calls=%fused_computation.7 | convolution fusion | flops 6443499520 | bytes 12582912 | tf_op jit(solution)/shard_map/trc,tpsr->tpcs/dot_general | solution.py:96
  69.5 5.1 %fusion.5 = f32[1,2,128,8,512]{2,4,1,3,0:T(8,128)S(1)} fusion(f32[2,128,8,512,1]{3,2,1,0,4:T(8,128)S(1)} %fusion.8, f32[1,128,2,128]{3,1,2,0:T(8,128)S(1)} %get-tuple-element.17, f32[1,128,2,128]{3,1,2,0:T(8,128)S(1)} %get-tuple-element.16), kind=kOutput, calls=%fused_computation.6 | convolution fusion | flops 1610678272 | bytes 8650752 | tf_op jit(solution)/shard_map/qkpn,tpnjs->tqkjs/dot_general | solution.py:100
  74.6 1.4 %subtract_reduce_fusion = (f32[128,512]{0,1:T(8,128)S(1)}, f32[128,512]{0,1:T(8,128)S(1)}) fusion(f32[1,2,128,8,512]{2,4,1,3,0:T(8,128)S(1)} %fusion.5, f32[128,8]{0,1:T(8,128)S(1)} %get-tuple-element.42, f32[8,512]{1,0:T(8,128)S(1)} %get-tuple-element.29, f32[128,8]{0,1:T(8,128)S(1)} %get-tuple-element.43, f32[8,512]{1,0:T(8,128)S(1)} %get-tuple-element.28), kind=kLoop, calls=%fused_computation.11 | loop fusion | flops 7208960 | bytes 4759552 | tf_op jit(solution)/shard_map/reduce_sum | solution.py:115
  76.1 1.4 %bitcast_multiply_fusion.1 = (f32[1,512,128]{2,1,0:T(8,128)S(1)}, f32[1,512,128]{2,1,0:T(8,128)S(1)}) fusion(f32[128,512]{0,1:T(8,128)S(1)} %get-tuple-element.5, f32[512]{0:T(512)S(1)} %mul.885, f32[512]{0:T(512)S(1)} %fusion.86, s32[512]{0:T(512)S(1)} %broadcast_multiply_fusion.1, f32[512]{0:T(512)S(1)} %fusion.84, f32[128,512]{0,1:T(8,128)S(1)} %get-tuple-element.6), kind=kLoop, calls=%fused_computation.38 | loop fusion | flops 786432 | bytes 1056768 | tf_op jit(solution)/shard_map/mul | solution.py:115
  77.5 1.3 %pad_maximum_fusion = f32[512,2,128]{2,1,0:T(2,128)} fusion(f32[512,1,128]{2,1,0:T(1,128)S(1)} %bitcast.79, f32[512,1,128]{2,1,0:T(1,128)S(1)} %bitcast.78), kind=kLoop, calls=%fused_computation.20 | loop fusion | flops 131072 | bytes 1048576 | tf_op jit(solution)/shard_map/stack | solution.py:119
  78.8 8.8 %all-to-all-start.1 = ((f32[128,8,128]{2,1,0:T(8,128)}), f32[128,8,128]{2,1,0:T(8,128)S(1)}, u32[]{:S(2)}, u32[]{:S(2)}) async-start(f32[128,8,128]{2,1,0:T(8,128)} %bitcast.32), calls=%async_computation.1 | async-start | bytes 1048576 | tf_op jit(solution)/shard_map/all_to_all | solution.py:154
  87.5 0.2 dynamic-slice_reduce_fusion
  87.9 13.4 %all-to-all-done.1 = f32[128,8,128]{2,1,0:T(8,128)S(1)} async-done(((f32[128,8,128]{2,1,0:T(8,128)}), f32[128,8,128]{2,1,0:T(8,128)S(1)}, u32[]{:S(2)}, u32[]{:S(2)}) %all-to-all-start.1) | async-done | bytes 524320 | tf_op jit(solution)/shard_map/all_to_all | solution.py:154
  101.3 0.4 fusion.9
  101.7 0.6 copy.86
  (41 shorter events, 0.9 us)
Async XLA Ops:
  0.0 8.8 %copy-start.1 = (s32[512,8]{0,1:T(8,128)S(1)}, s32[512,8]{0,1:T(8,128)}, u32[]{:S(2)}) copy-start(s32[512,8]{0,1:T(8,128)} %param.8) | copy-start | bytes 49156
  0.0 9.2 %copy-start.2 = (s32[512,8]{0,1:T(8,128)S(1)}, s32[512,8]{0,1:T(8,128)}, u32[]{:S(2)}) copy-start(s32[512,8]{0,1:T(8,128)} %param.10) | copy-start | bytes 49156
  0.0 9.5 %copy-start.3 = (s32[512,8]{0,1:T(8,128)S(1)}, s32[512,8]{0,1:T(8,128)}, u32[]{:S(2)}) copy-start(s32[512,8]{0,1:T(8,128)} %param.9) | copy-start | bytes 49156
  0.0 59.5 %all-to-all-start = ((f32[32,32,1024]{2,1,0:T(8,128)}), f32[32,32,1024]{2,1,0:T(8,128)}, u32[]{:S(2)}, u32[]{:S(2)}) async-start(f32[32,32,1024]{2,1,0:T(8,128)} %param.7), calls=%async_computation | async-start | bytes 8388608 | tf_op jit(solution)/shard_map/all_to_all | solution.py:149
  23.2 1.8 %copy-start.4 = (f32[512,8]{0,1:T(8,128)S(1)}, f32[512,8]{0,1:T(8,128)}, u32[]{:S(2)}) copy-start(f32[512,8]{0,1:T(8,128)} %param.12) | copy-start | bytes 49156
  23.2 2.1 %copy-start.5 = (f32[512,8]{0,1:T(8,128)S(1)}, f32[512,8]{0,1:T(8,128)}, u32[]{:S(2)}) copy-start(f32[512,8]{0,1:T(8,128)} %param.11) | copy-start | bytes 49156
  23.2 2.5 %copy-start.6 = (f32[512]{0:T(512)S(1)}, f32[512]{0:T(512)}, u32[]{:S(2)}) copy-start(f32[512]{0:T(512)} %param.13) | copy-start | bytes 6148
  25.0 3.7 %copy-start = (f32[1,1,512,1024]{3,2,1,0:T(8,128)S(1)}, f32[1,1,512,1024]{3,2,1,0:T(8,128)}, u32[]{:S(2)}) copy-start(f32[1,1,512,1024]{3,2,1,0:T(8,128)} %copy.71) | copy-start | bytes 6291460
  78.8 22.5 %all-to-all-start.1 = ((f32[128,8,128]{2,1,0:T(8,128)}), f32[128,8,128]{2,1,0:T(8,128)S(1)}, u32[]{:S(2)}, u32[]{:S(2)}) async-start(f32[128,8,128]{2,1,0:T(8,128)} %bitcast.32), calls=%async_computation.1 | async-start | bytes 1048576 | tf_op jit(solution)/shard_map/all_to_all | solution.py:154

commit v18 on v15

--- a/solution.py
+++ b/solution.py
@@ -137,7 +137,7 @@
     pick = (rows == place(mine, 0)[:, None]).astype(jnp.float32) + (
         rows == place(mine + 1, 1)[:, None]
     ).astype(jnp.float32)
-    return jnp.einsum("kj,jpl->kpl", pick, flat, precision=lax.Precision.HIGHEST)
+    return jnp.einsum("kj,jpl->kpl", pick, flat, precision=MID)
 
 
 def on_device(volume, blk_plane, blk_row, blk_col, frac_plane, frac_row, defocus):

time: 103 us -> 102 us (level)
  no operation moved by 1% of the time
where the time goes in v18:
time: 102 us
  waiting for transfers between devices  38.6 us (38%)
  starting transfers between devices  17.5 us (17%)
  local copies, waits for them, and re-layouts  15.7 us (15%)
  matrix products  15.4 us (15%)
  other arithmetic  14.6 us (14%)
    all_to_all x1, waiting for transfers between devices, on_device(): lax.all_to_all(volume, 'slab', split_axis=0, concat_axis=1, tiled=True)  25.3 us
    all_to_all x1, waiting for transfers between devices, on_device(): lax.all_to_all(parts, ('slab', 'img'), split_axis=0, concat_axis=0, tiled...  13.4 us
    dot_general x1, matrix products, send_parts(): r_t = jnp.einsum('trc,tpsr->tpcs', piece, w_all, precision=MID)  9.97 us
    all_to_all x1, starting transfers between devices, on_device(): lax.all_to_all(volume, 'slab', split_axis=0, concat_axis=1, tiled=True)  8.78 us
    all_to_all x1, starting transfers between devices, on_device(): lax.all_to_all(parts, ('slab', 'img'), split_axis=0, concat_axis=0, tiled...  8.76 us
    sub x2, local copies, waits for them, and re-layouts, row_roots(): a_re[:, :, None] * b_re[:, None, :] - a_im[:, :, None] * b_im[:, None, :]  5.86 us
    mul x1, other arithmetic, send_parts(): w_re = ((1.0 - frac_y) * lo_re + frac_y * hi_re) * norm  5.49 us
    dot_general x1, matrix products, send_parts(): y_j = jnp.einsum('qkpn,tpnjs->tqkjs', w_j, r5, precision=MID)  5.14 us
  transfers between devices with their start and end apart: 2, of which 2 were waited for; matrix products, arithmetic and copies ran while one was open for 25% of the time, Pallas kernels for 0%

profile of v18, /device:TPU:1, one launch (start us, length us, event | category | flops | bytes accessed | tf_op | source)
XLA Modules:
  0.0 102.2 jit_solution(388681232603613997)
XLA Ops:
  0.0 8.8 %all-to-all-start = ((f32[32,32,1024]{2,1,0:T(8,128)}), f32[32,32,1024]{2,1,0:T(8,128)}, u32[]{:S(2)}, u32[]{:S(2)}) async-start(f32[32,32,1024]{2,1,0:T(8,128)} %param.7), calls=%async_computation | async-start | bytes 8388608 | tf_op jit(solution)/shard_map/all_to_all | solution.py:148
  8.8 0.1 copy.112
  9.0 0.1 reshape.1419
  9.2 0.1 copy.120
  9.3 0.1 broadcast_in_dim.130
  9.5 0.1 copy.123
  9.6 0.1 broadcast_in_dim.133
  9.8 0.2 convert_reduce_fusion
  10.2 0.2 copy.125
  10.3 0.2 reshape.1422
  10.5 1.1 %fusion.58 = (f32[512,32]{0,1:T(8,128)S(1)}, f32[512,32]{0,1:T(8,128)S(1)}, f32[512,32]{0,1:T(8,128)S(1)}, f32[512,32]{0,1:T(8,128)S(1)}, f32[512,32]{0,1:T(8,12...) fusion(s32[32]{0:T(128)S(1)} %iota_multiply_fusion, s32[512]{0:T(512)S(1)} %reshape.1422, ...), kind=kLoop, calls=%fused_computation.111 | loop fusion | flops 983040 | bytes 528512 | tf_op jit(solution)/shard_map/cos | solution.py:21
  11.6 1.9 %multiply_subtract_fusion.1 = (f32[512,32,32]{0,2,1:T(8,128)}, f32[512,32,32]{0,2,1:T(8,128)S(1)}) fusion(f32[512,32]{0,1:T(8,128)S(1)} %get-tuple-element.30, f32[512,32]{0,1:T(8,128)S(1)} %get-tuple-element.25, f32[512,32]{0,1:T(8,128)S(1)} %get-tuple-element.31, f32[512,32]{0,1:T(8,128)S(1)} %get-tuple-element.24), kind=kLoop, calls=%fused_computation.18 | loop fusion | flops 3145728 | bytes 4456448 | tf_op jit(solution)/shard_map/sub | solution.py:76
  13.6 2.9 %copy.131 = f32[1,1,512,1024]{3,2,1,0:T(8,128)} copy(f32[1,1,512,1024]{2,3,1,0:T(8,128)} %bitcast.75) | data formatting | bytes 4194304 | tf_op jit(solution)/shard_map/sub | solution.py:76
  16.5 1.9 %copy.133 = f32[1,1,512,1024]{3,2,1,0:T(8,128)} copy(f32[1,1,512,1024]{2,3,1,0:T(8,128)S(1)} %bitcast.73) | data formatting | bytes 4194304 | tf_op jit(solution)/shard_map/add | solution.py:77
  18.3 1.9 %multiply_subtract_fusion = (f32[512,32,32]{0,2,1:T(8,128)}, f32[512,32,32]{0,2,1:T(8,128)S(1)}) fusion(f32[512,32]{0,1:T(8,128)S(1)} %get-tuple-element.35, f32[512,32]{0,1:T(8,128)S(1)} %get-tuple-element.36, f32[512,32]{0,1:T(8,128)S(1)} %get-tuple-element.34, f32[512,32]{0,1:T(8,128)S(1)} %get-tuple-element.37), kind=kLoop, calls=%fused_computation.17 | loop fusion | flops 3145728 | bytes 4456448 | tf_op jit(solution)/shard_map/sub | solution.py:76
  20.3 3.0 %copy.132 = f32[1,1,512,1024]{3,2,1,0:T(8,128)} copy(f32[1,1,512,1024]{2,3,1,0:T(8,128)} %bitcast.76) | data formatting | bytes 4194304 | tf_op jit(solution)/shard_map/sub | solution.py:76
  23.2 1.8 %copy.134 = f32[1,1,512,1024]{3,2,1,0:T(8,128)} copy(f32[1,1,512,1024]{2,3,1,0:T(8,128)S(1)} %bitcast.74) | data formatting | bytes 4194304 | tf_op jit(solution)/shard_map/add | solution.py:77
  25.0 0.1 copy.117
  25.2 0.1 broadcast_in_dim.126
  25.3 0.1 copy.128
  25.5 0.1 broadcast_in_dim.139
  25.7 0.1 broadcast_in_dim.135
  25.9 0.2 copy.130
  26.1 0.2 broadcast_in_dim_reshape.5
  26.3 0.2 copy.122
  26.5 0.2 broadcast_in_dim_reshape.4
  26.7 0.2 copy.119
  26.8 0.2 reshape.1421
  27.0 0.2 copy.116
  27.2 0.2 reshape.1420
  27.4 0.1 eq.156
  27.6 0.2 copy.127
  27.8 0.2 mul.838
  28.0 0.3 fusion.61
  28.3 0.3 negate_multiply_fusion
  28.6 0.1 fusion.68
  28.7 5.5 %add_multiply_fusion.1 = (f32[1,1,512,1024]{3,2,1,0:T(8,128)}, f32[1,1,512,1024]{3,2,1,0:T(8,128)}) fusion(f32[1,1,512,1024]{3,2,1,0:T(8,128)} %copy.132, f32[1,1,512,1024]{3,2,1,0:T(8,128)S(1)} %copy-done, f32[512]{0:T(512)S(1)} %broadcast_in_dim_reshape.5, f32[512]{0:T(512)S(1)} %broadcast_subtract_fusion, f32[1,1,512,1024]{3,2,1,0:T(8,128)} %copy.134, ...), kind=kLoop, calls=%fused_computation.16 | loop fusion | flops 4194304 | bytes 12587008 | tf_op jit(solution)/shard_map/mul | solution.py:83
  34.2 25.3 %all-to-all-done = f32[32,32,1024]{2,1,0:T(8,128)} async-done(((f32[32,32,1024]{2,1,0:T(8,128)}), f32[32,32,1024]{2,1,0:T(8,128)}, u32[]{:S(2)}, u32[]{:S(2)}) %all-to-all-start) | async-done | bytes 4194336 | tf_op jit(solution)/shard_map/all_to_all | solution.py:148
  59.5 10.0 %fusion.8 = f32[2,128,8,512,1]{3,2,1,0,4:T(8,128)S(1)} fusion(f32[1024,1024,1]{1,0,2:T(8,128)} %bitcast.10, f32[1,1,512,1024]{3,2,1,0:T(8,128)} %get-tuple-element.23, f32[1,1,512,1024]{3,2,1,0:T(8,128)} %get-tuple-element.22), kind=kOutput, calls=%fused_computation.7 | convolution fusion | flops 6443499520 | bytes 12582912 | tf_op jit(solution)/shard_map/trc,tpsr->tpcs/dot_general | solution.py:96
  69.5 5.1 %fusion.5 = f32[1,2,128,8,512]{2,4,1,3,0:T(8,128)S(1)} fusion(f32[2,128,8,512,1]{3,2,1,0,4:T(8,128)S(1)} %fusion.8, f32[1,128,2,128]{3,1,2,0:T(8,128)S(1)} %get-tuple-element.17, f32[1,128,2,128]{3,1,2,0:T(8,128)S(1)} %get-tuple-element.16), kind=kOutput, calls=%fused_computation.6 | convolution fusion | flops 1610678272 | bytes 8650752 | tf_op jit(solution)/shard_map/qkpn,tpnjs->tqkjs/dot_general | solution.py:100
  74.6 1.4 %subtract_reduce_fusion = (f32[128,512]{0,1:T(8,128)S(1)}, f32[128,512]{0,1:T(8,128)S(1)}) fusion(f32[1,2,128,8,512]{2,4,1,3,0:T(8,128)S(1)} %fusion.5, f32[128,8]{0,1:T(8,128)S(1)} %get-tuple-element.42, f32[8,512]{1,0:T(8,128)S(1)} %get-tuple-element.29, f32[128,8]{0,1:T(8,128)S(1)} %get-tuple-element.43, f32[8,512]{1,0:T(8,128)S(1)} %get-tuple-element.28), kind=kLoop, calls=%fused_computation.11 | loop fusion | flops 7208960 | bytes 4759552 | tf_op jit(solution)/shard_map/reduce_sum | solution.py:114
  76.1 1.4 %bitcast_multiply_fusion.1 = (f32[512,1,128]{2,0,1:T(8,128)S(1)}, f32[512,1,128]{2,0,1:T(8,128)S(1)}) fusion(f32[128,512]{0,1:T(8,128)S(1)} %get-tuple-element.5, f32[512]{0:T(512)S(1)} %mul.838, f32[512]{0:T(512)S(1)} %fusion.86, s32[512]{0:T(512)S(1)} %broadcast_multiply_fusion.1, f32[512]{0:T(512)S(1)} %fusion.84, f32[128,512]{0,1:T(8,128)S(1)} %get-tuple-element.6), kind=kLoop, calls=%fused_computation.38 | loop fusion | flops 786432 | bytes 1056768 | tf_op jit(solution)/shard_map/mul | solution.py:118
  77.5 1.2 %copy.138 = f32[512,2,128]{2,1,0:T(2,128)} copy(f32[512,2,128]{2,0,1:T(8,128)S(1)} %pad_maximum_fusion) | data formatting | bytes 1048576 | tf_op jit(solution)/shard_map/stack | solution.py:118
  78.7 8.8 %all-to-all-start.1 = ((f32[128,8,128]{2,1,0:T(8,128)}), f32[128,8,128]{2,1,0:T(8,128)S(1)}, u32[]{:S(2)}, u32[]{:S(2)}) async-start(f32[128,8,128]{2,1,0:T(8,128)} %bitcast.31), calls=%async_computation.1 | async-start | bytes 1048576 | tf_op jit(solution)/shard_map/all_to_all | solution.py:153
  87.5 0.2 dynamic-slice_reduce_fusion
  87.9 13.4 %all-to-all-done.1 = f32[128,8,128]{2,1,0:T(8,128)S(1)} async-done(((f32[128,8,128]{2,1,0:T(8,128)}), f32[128,8,128]{2,1,0:T(8,128)S(1)}, u32[]{:S(2)}, u32[]{:S(2)}) %all-to-all-start.1) | async-done | bytes 524320 | tf_op jit(solution)/shard_map/all_to_all | solution.py:153
  101.3 0.3 fusion.9
  101.6 0.6 copy.140
  (42 shorter events, 1.0 us)
Async XLA Ops:
  0.0 8.8 %copy-start.1 = (s32[512,8]{0,1:T(8,128)S(1)}, s32[512,8]{0,1:T(8,128)}, u32[]{:S(2)}) copy-start(s32[512,8]{0,1:T(8,128)} %param.8) | copy-start | bytes 49156
  0.0 9.2 %copy-start.2 = (s32[512,8]{0,1:T(8,128)S(1)}, s32[512,8]{0,1:T(8,128)}, u32[]{:S(2)}) copy-start(s32[512,8]{0,1:T(8,128)} %param.10) | copy-start | bytes 49156
  0.0 9.5 %copy-start.3 = (s32[512,8]{0,1:T(8,128)S(1)}, s32[512,8]{0,1:T(8,128)}, u32[]{:S(2)}) copy-start(s32[512,8]{0,1:T(8,128)} %param.9) | copy-start | bytes 49156
  0.0 59.5 %all-to-all-start = ((f32[32,32,1024]{2,1,0:T(8,128)}), f32[32,32,1024]{2,1,0:T(8,128)}, u32[]{:S(2)}, u32[]{:S(2)}) async-start(f32[32,32,1024]{2,1,0:T(8,128)} %param.7), calls=%async_computation | async-start | bytes 8388608 | tf_op jit(solution)/shard_map/all_to_all | solution.py:148
  23.2 1.8 %copy-start.4 = (f32[512,8]{0,1:T(8,128)S(1)}, f32[512,8]{0,1:T(8,128)}, u32[]{:S(2)}) copy-start(f32[512,8]{0,1:T(8,128)} %param.11) | copy-start | bytes 49156
  23.2 2.1 %copy-start.5 = (f32[512,8]{0,1:T(8,128)S(1)}, f32[512,8]{0,1:T(8,128)}, u32[]{:S(2)}) copy-start(f32[512,8]{0,1:T(8,128)} %param.12) | copy-start | bytes 49156
  23.2 2.5 %copy-start.6 = (f32[512]{0:T(512)S(1)}, f32[512]{0:T(512)}, u32[]{:S(2)}) copy-start(f32[512]{0:T(512)} %param.13) | copy-start | bytes 6148
  25.0 3.7 %copy-start = (f32[1,1,512,1024]{3,2,1,0:T(8,128)S(1)}, f32[1,1,512,1024]{3,2,1,0:T(8,128)}, u32[]{:S(2)}) copy-start(f32[1,1,512,1024]{3,2,1,0:T(8,128)} %copy.131) | copy-start | bytes 6291460
  78.7 22.5 %all-to-all-start.1 = ((f32[128,8,128]{2,1,0:T(8,128)}), f32[128,8,128]{2,1,0:T(8,128)S(1)}, u32[]{:S(2)}, u32[]{:S(2)}) async-start(f32[128,8,128]{2,1,0:T(8,128)} %bitcast.31), calls=%async_computation.1 | async-start | bytes 1048576 | tf_op jit(solution)/shard_map/all_to_all | solution.py:153

commit v19 on v15

--- a/solution.py
+++ b/solution.py
@@ -111,11 +111,14 @@
     t_im = t_im[None, :, :, None]
     g_re = e_re * t_re - e_im * t_im
     g_im = e_re * t_im + e_im * t_re
+    scale_t = jnp.swapaxes(scale.reshape(own, n_s, LANES), 1, 2)[:, :, None, :]
+    g_re = g_re * scale_t
+    g_im = g_im * scale_t
     o_re = jnp.sum(g_re * y_re - g_im * y_im, axis=2)
     o_im = jnp.sum(g_re * y_im + g_im * y_re, axis=2)
     o_re = jnp.swapaxes(o_re, 1, 2).reshape(own * n_s, LANES)
     o_im = jnp.swapaxes(o_im, 1, 2).reshape(own * n_s, LANES)
-    parts = jnp.stack([scale * o_re, scale * o_im], axis=1)
+    parts = jnp.stack([o_re, o_im], axis=1)
     parts = parts.reshape(own, n_dev, 4, 2, LANES)
     return jnp.swapaxes(parts, 0, 1).reshape(n_dev, own * 4 * 2, LANES)
 

time: 103 us -> 101 us (0.981)
  local copies, waits for them, and re-layouts: 15.7 us -> 14.5 us
    another operation x2 -> x0, local copies, waits for them, and re-layouts: 1.39 us -> none  [the longest x1 1.19 us: send_parts(): parts = jnp.stack([scale * o_re, scale * o_im], axis=1)]
    another operation x1, other arithmetic: 0.04 us -> 1.26 us  [send_parts(): parts = jnp.stack([o_re, o_im], axis=1)]
    all_to_all x1, waiting for transfers between devices: 25.3 us -> 24.2 us  [on_device(): lax.all_to_all(volume, 'slab', split_axis=0, concat_axis=1, tiled=True)]
  transfers between devices with their start and end apart: 2 -> 2, of which waited for: 2 -> 2; matrix products, arithmetic and copies ran while one was open for 25% -> 26% of each run, Pallas kernels for 0% -> 0%
where the time goes in v19:
time: 101 us
  waiting for transfers between devices  37.6 us (37%)
  starting transfers between devices  17.5 us (17%)
  other arithmetic  15.5 us (15%)
  matrix products  15.3 us (15%)
  local copies, waits for them, and re-layouts  14.5 us (14%)
    all_to_all x1, waiting for transfers between devices, on_device(): lax.all_to_all(volume, 'slab', split_axis=0, concat_axis=1, tiled=True)  24.2 us
    all_to_all x1, waiting for transfers between devices, on_device(): lax.all_to_all(parts, ('slab', 'img'), split_axis=0, concat_axis=0, tiled...  13.4 us
    dot_general x1, matrix products, send_parts(): r_t = jnp.einsum('trc,tpsr->tpcs', piece, w_all, precision=MID)  9.79 us
    all_to_all x1, starting transfers between devices, on_device(): lax.all_to_all(volume, 'slab', split_axis=0, concat_axis=1, tiled=True)  8.78 us
    all_to_all x1, starting transfers between devices, on_device(): lax.all_to_all(parts, ('slab', 'img'), split_axis=0, concat_axis=0, tiled...  8.76 us
    sub x2, local copies, waits for them, and re-layouts, row_roots(): a_re[:, :, None] * b_re[:, None, :] - a_im[:, :, None] * b_im[:, None, :]  5.86 us
    mul x1, other arithmetic, send_parts(): w_re = ((1.0 - frac_y) * lo_re + frac_y * hi_re) * norm  5.49 us
    dot_general x1, matrix products, send_parts(): y_j = jnp.einsum('qkpn,tpnjs->tqkjs', w_j, r5, precision=MID)  5.14 us
  transfers between devices with their start and end apart: 2, of which 2 were waited for; matrix products, arithmetic and copies ran while one was open for 26% of the time, Pallas kernels for 0%

profile of v19, /device:TPU:1, one launch (start us, length us, event | category | flops | bytes accessed | tf_op | source)
XLA Modules:
  0.0 100.8 jit_solution(5700221563044915023)
XLA Ops:
  0.0 8.8 %all-to-all-start = ((f32[32,32,1024]{2,1,0:T(8,128)}), f32[32,32,1024]{2,1,0:T(8,128)}, u32[]{:S(2)}, u32[]{:S(2)}) async-start(f32[32,32,1024]{2,1,0:T(8,128)} %param.7), calls=%async_computation | async-start | bytes 8388608 | tf_op jit(solution)/shard_map/all_to_all | solution.py:151
  8.9 0.1 copy.56
  9.0 0.1 reshape.1336
  9.2 0.1 copy.60
  9.3 0.1 broadcast_in_dim.126
  9.5 0.1 copy.67
  9.7 0.1 broadcast_in_dim.134
  9.8 0.2 convert_reduce_fusion
  10.2 0.2 copy.69
  10.4 0.2 reshape.1339
  10.6 1.1 %fusion.59 = (f32[512,32]{0,1:T(8,128)S(1)}, f32[512,32]{0,1:T(8,128)S(1)}, f32[512,32]{0,1:T(8,128)S(1)}, f32[512,32]{0,1:T(8,128)S(1)}, f32[512,32]{0,1:T(8,12...) fusion(s32[32]{0:T(128)S(1)} %iota_multiply_fusion, s32[512]{0:T(512)S(1)} %reshape.1339, ...), kind=kLoop, calls=%fused_computation.110 | loop fusion | flops 983040 | bytes 528512 | tf_op jit(solution)/shard_map/cos | solution.py:21
  11.6 1.9 %multiply_subtract_fusion.1 = (f32[512,32,32]{0,2,1:T(8,128)}, f32[512,32,32]{0,2,1:T(8,128)S(1)}) fusion(f32[512,32]{0,1:T(8,128)S(1)} %get-tuple-element.28, f32[512,32]{0,1:T(8,128)S(1)} %get-tuple-element.23, f32[512,32]{0,1:T(8,128)S(1)} %get-tuple-element.29, f32[512,32]{0,1:T(8,128)S(1)} %get-tuple-element.22), kind=kLoop, calls=%fused_computation.18 | loop fusion | flops 3145728 | bytes 4456448 | tf_op jit(solution)/shard_map/sub | solution.py:76
  13.6 2.9 %copy.75 = f32[1,1,512,1024]{3,2,1,0:T(8,128)} copy(f32[1,1,512,1024]{2,3,1,0:T(8,128)} %bitcast.77) | data formatting | bytes 4194304 | tf_op jit(solution)/shard_map/sub | solution.py:76
  16.5 1.9 %copy.77 = f32[1,1,512,1024]{3,2,1,0:T(8,128)} copy(f32[1,1,512,1024]{2,3,1,0:T(8,128)S(1)} %bitcast.75) | data formatting | bytes 4194304 | tf_op jit(solution)/shard_map/add | solution.py:77
  18.3 1.9 %multiply_subtract_fusion = (f32[512,32,32]{0,2,1:T(8,128)}, f32[512,32,32]{0,2,1:T(8,128)S(1)}) fusion(f32[512,32]{0,1:T(8,128)S(1)} %get-tuple-element.33, f32[512,32]{0,1:T(8,128)S(1)} %get-tuple-element.34, f32[512,32]{0,1:T(8,128)S(1)} %get-tuple-element.32, f32[512,32]{0,1:T(8,128)S(1)} %get-tuple-element.35), kind=kLoop, calls=%fused_computation.17 | loop fusion | flops 3145728 | bytes 4456448 | tf_op jit(solution)/shard_map/sub | solution.py:76
  20.3 3.0 %copy.76 = f32[1,1,512,1024]{3,2,1,0:T(8,128)} copy(f32[1,1,512,1024]{2,3,1,0:T(8,128)} %bitcast.78) | data formatting | bytes 4194304 | tf_op jit(solution)/shard_map/sub | solution.py:76
  23.2 1.8 %copy.78 = f32[1,1,512,1024]{3,2,1,0:T(8,128)} copy(f32[1,1,512,1024]{2,3,1,0:T(8,128)S(1)} %bitcast.76) | data formatting | bytes 4194304 | tf_op jit(solution)/shard_map/add | solution.py:77
  25.0 0.1 copy.64
  25.2 0.1 broadcast_in_dim.130
  25.3 0.1 copy.72
  25.5 0.1 broadcast_in_dim.140
  25.7 0.1 broadcast_in_dim.136
  25.9 0.2 copy.74
  26.1 0.2 broadcast_in_dim_reshape.2
  26.3 0.2 copy.66
  26.5 0.2 reshape.1338
  26.7 0.2 copy.63
  26.9 0.2 reshape.1337
  27.1 0.1 eq.156
  27.2 0.2 copy.71
  27.4 0.2 mul.865
  27.6 0.2 copy.62
  27.8 0.2 mul.842
  28.0 0.3 fusion.62
  28.3 0.3 negate_multiply_fusion
  28.6 0.1 fusion.69
  28.7 1.0 %fusion.20 = f32[128,512]{0,1:T(8,128)S(1)} fusion(f32[512]{0:T(512)S(1)} %mul.865, f32[512]{0:T(512)S(1)} %fusion.87, s32[512]{0:T(512)S(1)} %broadcast_multiply_fusion.1, f32[512]{0:T(512)S(1)} %fusion.85), kind=kLoop, calls=%fused_computation.34 | loop fusion | flops 655360 | bytes 270336 | tf_op jit(solution)/shard_map/mul | solution.py:115
  29.8 5.5 %add_multiply_fusion.2 = (f32[1,1,512,1024]{3,2,1,0:T(8,128)}, f32[1,1,512,1024]{3,2,1,0:T(8,128)}) fusion(f32[1,1,512,1024]{3,2,1,0:T(8,128)} %copy.76, f32[1,1,512,1024]{3,2,1,0:T(8,128)S(1)} %copy-done, f32[512]{0:T(512)S(1)} %broadcast_in_dim_reshape.2, f32[512]{0:T(512)S(1)} %broadcast_subtract_fusion, f32[1,1,512,1024]{3,2,1,0:T(8,128)} %copy.78, ...), kind=kLoop, calls=%fused_computation.16 | loop fusion | flops 4194304 | bytes 12587008 | tf_op jit(solution)/shard_map/mul | solution.py:83
  35.3 24.2 %all-to-all-done = f32[32,32,1024]{2,1,0:T(8,128)} async-done(((f32[32,32,1024]{2,1,0:T(8,128)}), f32[32,32,1024]{2,1,0:T(8,128)}, u32[]{:S(2)}, u32[]{:S(2)}) %all-to-all-start) | async-done | bytes 4194336 | tf_op jit(solution)/shard_map/all_to_all | solution.py:151
  59.5 9.8 %fusion.8 = f32[2,128,8,512,1]{3,2,1,0,4:T(8,128)S(1)} fusion(f32[1024,1024,1]{1,0,2:T(8,128)} %bitcast.12, f32[1,1,512,1024]{3,2,1,0:T(8,128)} %get-tuple-element.21, f32[1,1,512,1024]{3,2,1,0:T(8,128)} %get-tuple-element.20), kind=kOutput, calls=%fused_computation.7 | convolution fusion | flops 6443499520 | bytes 12582912 | tf_op jit(solution)/shard_map/trc,tpsr->tpcs/dot_general | solution.py:96
  69.3 5.1 %fusion.5 = f32[1,2,128,8,512]{2,4,1,3,0:T(8,128)S(1)} fusion(f32[2,128,8,512,1]{3,2,1,0,4:T(8,128)S(1)} %fusion.8, f32[1,128,2,128]{3,1,2,0:T(8,128)S(1)} %get-tuple-element.17, f32[1,128,2,128]{3,1,2,0:T(8,128)S(1)} %get-tuple-element.16), kind=kOutput, calls=%fused_computation.6 | convolution fusion | flops 1610678272 | bytes 8650752 | tf_op jit(solution)/shard_map/qkpn,tpnjs->tqkjs/dot_general | solution.py:100
  74.4 1.5 %subtract_reduce_fusion = (f32[128,512]{0,1:T(8,128)S(1)}, f32[128,512]{0,1:T(8,128)S(1)}) fusion(f32[1,2,128,8,512]{2,4,1,3,0:T(8,128)S(1)} %fusion.5, f32[128,512]{0,1:T(8,128)S(1)} %fusion.20, f32[128,8]{0,1:T(8,128)S(1)} %get-tuple-element.40, f32[8,512]{1,0:T(8,128)S(1)} %get-tuple-element.27, f32[128,8]{0,1:T(8,128)S(1)} %get-tuple-element.41, ...), kind=kLoop, calls=%fused_computation.11 | loop fusion | flops 8257536 | bytes 5021696 | tf_op jit(solution)/shard_map/reduce_sum | solution.py:117
  75.9 1.3 %pad_maximum_fusion = f32[512,2,128]{2,1,0:T(2,128)} fusion(f32[512,1,128]{2,1,0:T(1,128)S(1)} %bitcast.81, f32[512,1,128]{2,1,0:T(1,128)S(1)} %bitcast.80), kind=kLoop, calls=%fused_computation.20 | loop fusion | flops 131072 | bytes 1048576 | tf_op jit(solution)/shard_map/stack | solution.py:121
  77.2 8.8 %all-to-all-start.1 = ((f32[128,8,128]{2,1,0:T(8,128)}), f32[128,8,128]{2,1,0:T(8,128)S(1)}, u32[]{:S(2)}, u32[]{:S(2)}) async-start(f32[128,8,128]{2,1,0:T(8,128)} %bitcast.33), calls=%async_computation.1 | async-start | bytes 1048576 | tf_op jit(solution)/shard_map/all_to_all | solution.py:156
  86.0 0.2 dynamic-slice_reduce_fusion
  86.3 13.4 %all-to-all-done.1 = f32[128,8,128]{2,1,0:T(8,128)S(1)} async-done(((f32[128,8,128]{2,1,0:T(8,128)}), f32[128,8,128]{2,1,0:T(8,128)S(1)}, u32[]{:S(2)}, u32[]{:S(2)}) %all-to-all-start.1) | async-done | bytes 524320 | tf_op jit(solution)/shard_map/all_to_all | solution.py:156
  99.7 0.4 fusion.9
  100.1 0.6 copy.83
  (41 shorter events, 0.9 us)
Async XLA Ops:
  0.0 8.8 %copy-start.1 = (s32[512,8]{0,1:T(8,128)S(1)}, s32[512,8]{0,1:T(8,128)}, u32[]{:S(2)}) copy-start(s32[512,8]{0,1:T(8,128)} %param.8) | copy-start | bytes 49156
  0.0 9.2 %copy-start.2 = (s32[512,8]{0,1:T(8,128)S(1)}, s32[512,8]{0,1:T(8,128)}, u32[]{:S(2)}) copy-start(s32[512,8]{0,1:T(8,128)} %param.10) | copy-start | bytes 49156
  0.0 9.5 %copy-start.3 = (s32[512,8]{0,1:T(8,128)S(1)}, s32[512,8]{0,1:T(8,128)}, u32[]{:S(2)}) copy-start(s32[512,8]{0,1:T(8,128)} %param.9) | copy-start | bytes 49156
  0.0 59.5 %all-to-all-start = ((f32[32,32,1024]{2,1,0:T(8,128)}), f32[32,32,1024]{2,1,0:T(8,128)}, u32[]{:S(2)}, u32[]{:S(2)}) async-start(f32[32,32,1024]{2,1,0:T(8,128)} %param.7), calls=%async_computation | async-start | bytes 8388608 | tf_op jit(solution)/shard_map/all_to_all | solution.py:151
  23.2 1.8 %copy-start.4 = (f32[512,8]{0,1:T(8,128)S(1)}, f32[512,8]{0,1:T(8,128)}, u32[]{:S(2)}) copy-start(f32[512,8]{0,1:T(8,128)} %param.11) | copy-start | bytes 49156
  23.2 2.1 %copy-start.5 = (f32[512,8]{0,1:T(8,128)S(1)}, f32[512,8]{0,1:T(8,128)}, u32[]{:S(2)}) copy-start(f32[512,8]{0,1:T(8,128)} %param.12) | copy-start | bytes 49156
  23.2 2.5 %copy-start.6 = (f32[512]{0:T(512)S(1)}, f32[512]{0:T(512)}, u32[]{:S(2)}) copy-start(f32[512]{0:T(512)} %param.13) | copy-start | bytes 6148
  25.0 4.7 %copy-start = (f32[1,1,512,1024]{3,2,1,0:T(8,128)S(1)}, f32[1,1,512,1024]{3,2,1,0:T(8,128)}, u32[]{:S(2)}) copy-start(f32[1,1,512,1024]{3,2,1,0:T(8,128)} %copy.75) | copy-start | bytes 6291460
  77.2 22.5 %all-to-all-start.1 = ((f32[128,8,128]{2,1,0:T(8,128)}), f32[128,8,128]{2,1,0:T(8,128)S(1)}, u32[]{:S(2)}, u32[]{:S(2)}) async-start(f32[128,8,128]{2,1,0:T(8,128)} %bitcast.33), calls=%async_computation.1 | async-start | bytes 1048576 | tf_op jit(solution)/shard_map/all_to_all | solution.py:156

commit v20 on v16

--- a/solution.py
+++ b/solution.py
@@ -111,12 +111,15 @@
     t_im = t_im[None, :, :, None]
     g_re = e_re * t_re - e_im * t_im
     g_im = e_re * t_im + e_im * t_re
+    scale_t = jnp.swapaxes(scale.reshape(own, n_s, LANES), 1, 2)[:, :, None, :]
+    g_re = g_re * scale_t
+    g_im = g_im * scale_t
     o_re = jnp.sum(g_re * y_re - g_im * y_im, axis=2)
     o_im = jnp.sum(g_re * y_im + g_im * y_re, axis=2)
     o_re = jnp.swapaxes(o_re, 1, 2).reshape(own * n_s, LANES)
     o_im = jnp.swapaxes(o_im, 1, 2).reshape(own * n_s, LANES)
-    p_re = jnp.swapaxes((scale * o_re).reshape(own, n_dev, 4, LANES), 0, 1)
-    p_im = jnp.swapaxes((scale * o_im).reshape(own, n_dev, 4, LANES), 0, 1)
+    p_re = jnp.swapaxes(o_re.reshape(own, n_dev, 4, LANES), 0, 1)
+    p_im = jnp.swapaxes(o_im.reshape(own, n_dev, 4, LANES), 0, 1)
     return jnp.concatenate(
         [p_re.reshape(n_dev, own * 4, LANES), p_im.reshape(n_dev, own * 4, LANES)], axis=1
     )

time: 104 us -> 101 us (0.971)
  waiting for transfers between devices: 39.3 us -> 37.6 us
  other arithmetic: 16.6 us -> 15.1 us
    all_to_all x1, waiting for transfers between devices: 25.9 us -> 24.2 us  [on_device(): lax.all_to_all(volume, 'slab', split_axis=0, concat_axis=1, tiled=True)]
    mul x1, other arithmetic: 2.55 us -> 1.04 us  [send_parts(): g_re = g_re * scale_t]
    add x2, local copies, waits for them, and re-layouts: 4.79 us -> 3.66 us  [row_roots(): a_re[:, :, None] * b_im[:, None, :] + a_im[:, :, None] * b_re[:, None, :]]
    sub x2, local copies, waits for them, and re-layouts: 4.73 us -> 5.86 us  [row_roots(): a_re[:, :, None] * b_re[:, None, :] - a_im[:, :, None] * b_im[:, None, :]]
  transfers between devices with their start and end apart: 2 -> 2, of which waited for: 2 -> 2; matrix products, arithmetic and copies ran while one was open for 24% -> 26% of each run, Pallas kernels for 0% -> 0%
where the time goes in v20:
time: 101 us; the launch traced here: 100 us
  waiting for transfers between devices  37.6 us (37%)
  starting transfers between devices  17.5 us (17%)
  matrix products  15.3 us (15%)
  other arithmetic  15.1 us (15%)
  local copies, waits for them, and re-layouts  14.6 us (14%)
    all_to_all x1, waiting for transfers between devices, on_device(): lax.all_to_all(volume, 'slab', split_axis=0, concat_axis=1, tiled=True)  24.2 us
    all_to_all x1, waiting for transfers between devices, on_device(): lax.all_to_all(parts, ('slab', 'img'), split_axis=0, concat_axis=0, tiled...  13.4 us
    dot_general x1, matrix products, send_parts(): r_t = jnp.einsum('trc,tpsr->tpcs', piece, w_all, precision=MID)  9.79 us
    all_to_all x1, starting transfers between devices, on_device(): lax.all_to_all(volume, 'slab', split_axis=0, concat_axis=1, tiled=True)  8.78 us
    all_to_all x1, starting transfers between devices, on_device(): lax.all_to_all(parts, ('slab', 'img'), split_axis=0, concat_axis=0, tiled...  8.76 us
    sub x2, local copies, waits for them, and re-layouts, row_roots(): a_re[:, :, None] * b_re[:, None, :] - a_im[:, :, None] * b_im[:, None, :]  5.86 us
    mul x1, other arithmetic, send_parts(): w_re = ((1.0 - frac_y) * lo_re + frac_y * hi_re) * norm  5.49 us
    dot_general x1, matrix products, send_parts(): y_j = jnp.einsum('qkpn,tpnjs->tqkjs', w_j, r5, precision=MID)  5.14 us
  transfers between devices with their start and end apart: 2, of which 2 were waited for; matrix products, arithmetic and copies ran while one was open for 26% of the time, Pallas kernels for 0%

profile of v20, /device:TPU:1, one launch (start us, length us, event | category | flops | bytes accessed | tf_op | source)
XLA Modules:
  0.0 100.5 jit_solution(6278184756325568997)
XLA Ops:
  0.0 8.8 %all-to-all-start = ((f32[32,32,1024]{2,1,0:T(8,128)}), f32[32,32,1024]{2,1,0:T(8,128)}, u32[]{:S(2)}, u32[]{:S(2)}) async-start(f32[32,32,1024]{2,1,0:T(8,128)} %param.7), calls=%async_computation | async-start | bytes 8388608 | tf_op jit(solution)/shard_map/all_to_all | solution.py:155
  8.9 0.1 copy.56
  9.0 0.1 reshape.1344
  9.2 0.1 copy.60
  9.3 0.1 broadcast_in_dim.126
  9.5 0.1 copy.67
  9.7 0.1 broadcast_in_dim.134
  9.8 0.2 convert_reduce_fusion
  10.2 0.2 copy.69
  10.4 0.2 reshape.1347
  10.6 1.1 %fusion.58 = (f32[512,32]{0,1:T(8,128)S(1)}, f32[512,32]{0,1:T(8,128)S(1)}, f32[512,32]{0,1:T(8,128)S(1)}, f32[512,32]{0,1:T(8,128)S(1)}, f32[512,32]{0,1:T(8,12...) fusion(s32[32]{0:T(128)S(1)} %iota_multiply_fusion, s32[512]{0:T(512)S(1)} %reshape.1347, ...), kind=kLoop, calls=%fused_computation.108 | loop fusion | flops 983040 | bytes 528512 | tf_op jit(solution)/shard_map/cos | solution.py:21
  11.6 1.9 %multiply_subtract_fusion.1 = (f32[512,32,32]{0,2,1:T(8,128)}, f32[512,32,32]{0,2,1:T(8,128)S(1)}) fusion(f32[512,32]{0,1:T(8,128)S(1)} %get-tuple-element.28, f32[512,32]{0,1:T(8,128)S(1)} %get-tuple-element.23, f32[512,32]{0,1:T(8,128)S(1)} %get-tuple-element.29, f32[512,32]{0,1:T(8,128)S(1)} %get-tuple-element.22), kind=kLoop, calls=%fused_computation.18 | loop fusion | flops 3145728 | bytes 4456448 | tf_op jit(solution)/shard_map/sub | solution.py:76
  13.6 2.9 %copy.75 = f32[1,1,512,1024]{3,2,1,0:T(8,128)} copy(f32[1,1,512,1024]{2,3,1,0:T(8,128)} %bitcast.78) | data formatting | bytes 4194304 | tf_op jit(solution)/shard_map/sub | solution.py:76
  16.5 1.9 %copy.77 = f32[1,1,512,1024]{3,2,1,0:T(8,128)} copy(f32[1,1,512,1024]{2,3,1,0:T(8,128)S(1)} %bitcast.76) | data formatting | bytes 4194304 | tf_op jit(solution)/shard_map/add | solution.py:77
  18.3 1.9 %multiply_subtract_fusion = (f32[512,32,32]{0,2,1:T(8,128)}, f32[512,32,32]{0,2,1:T(8,128)S(1)}) fusion(f32[512,32]{0,1:T(8,128)S(1)} %get-tuple-element.33, f32[512,32]{0,1:T(8,128)S(1)} %get-tuple-element.34, f32[512,32]{0,1:T(8,128)S(1)} %get-tuple-element.32, f32[512,32]{0,1:T(8,128)S(1)} %get-tuple-element.35), kind=kLoop, calls=%fused_computation.17 | loop fusion | flops 3145728 | bytes 4456448 | tf_op jit(solution)/shard_map/sub | solution.py:76
  20.3 3.0 %copy.76 = f32[1,1,512,1024]{3,2,1,0:T(8,128)} copy(f32[1,1,512,1024]{2,3,1,0:T(8,128)} %bitcast.79) | data formatting | bytes 4194304 | tf_op jit(solution)/shard_map/sub | solution.py:76
  23.2 1.8 %copy.78 = f32[1,1,512,1024]{3,2,1,0:T(8,128)} copy(f32[1,1,512,1024]{2,3,1,0:T(8,128)S(1)} %bitcast.77) | data formatting | bytes 4194304 | tf_op jit(solution)/shard_map/add | solution.py:77
  25.0 0.1 copy.64
  25.2 0.1 broadcast_in_dim.130
  25.3 0.1 copy.72
  25.5 0.1 broadcast_in_dim.140
  25.7 0.1 broadcast_in_dim.136
  25.9 0.2 copy.74
  26.1 0.2 broadcast_in_dim_reshape.2
  26.3 0.2 copy.66
  26.5 0.2 reshape.1346
  26.7 0.2 copy.63
  26.9 0.2 reshape.1345
  27.1 0.1 eq.152
  27.2 0.2 copy.71
  27.4 0.2 mul.865
  27.6 0.2 copy.62
  27.8 0.2 mul.842
  28.0 0.3 fusion.62
  28.3 0.3 negate_multiply_fusion
  28.7 1.0 %fusion.17 = f32[128,512]{0,1:T(8,128)S(1)} fusion(f32[512]{0:T(512)S(1)} %mul.865, f32[512]{0:T(512)S(1)} %fusion.87, s32[512]{0:T(512)S(1)} %broadcast_multiply_fusion.1, f32[512]{0:T(512)S(1)} %fusion.85), kind=kLoop, calls=%fused_computation.32 | loop fusion | flops 655360 | bytes 270336 | tf_op jit(solution)/shard_map/mul | solution.py:115
  29.8 5.5 %add_multiply_fusion.2 = (f32[1,1,512,1024]{3,2,1,0:T(8,128)}, f32[1,1,512,1024]{3,2,1,0:T(8,128)}) fusion(f32[1,1,512,1024]{3,2,1,0:T(8,128)} %copy.76, f32[1,1,512,1024]{3,2,1,0:T(8,128)S(1)} %copy-done, f32[512]{0:T(512)S(1)} %broadcast_in_dim_reshape.2, f32[512]{0:T(512)S(1)} %broadcast_subtract_fusion, f32[1,1,512,1024]{3,2,1,0:T(8,128)} %copy.78, ...), kind=kLoop, calls=%fused_computation.16 | loop fusion | flops 4194304 | bytes 12587008 | tf_op jit(solution)/shard_map/mul | solution.py:83
  35.3 24.2 %all-to-all-done = f32[32,32,1024]{2,1,0:T(8,128)} async-done(((f32[32,32,1024]{2,1,0:T(8,128)}), f32[32,32,1024]{2,1,0:T(8,128)}, u32[]{:S(2)}, u32[]{:S(2)}) %all-to-all-start) | async-done | bytes 4194336 | tf_op jit(solution)/shard_map/all_to_all | solution.py:155
  59.5 9.8 %fusion.8 = f32[2,128,8,512,1]{3,2,1,0,4:T(8,128)S(1)} fusion(f32[1024,1024,1]{1,0,2:T(8,128)} %bitcast.11, f32[1,1,512,1024]{3,2,1,0:T(8,128)} %get-tuple-element.21, f32[1,1,512,1024]{3,2,1,0:T(8,128)} %get-tuple-element.20), kind=kOutput, calls=%fused_computation.7 | convolution fusion | flops 6443499520 | bytes 12582912 | tf_op jit(solution)/shard_map/trc,tpsr->tpcs/dot_general | solution.py:96
  69.3 5.1 %fusion.5 = f32[1,2,128,8,512]{2,4,1,3,0:T(8,128)S(1)} fusion(f32[2,128,8,512,1]{3,2,1,0,4:T(8,128)S(1)} %fusion.8, f32[1,128,2,128]{3,1,2,0:T(8,128)S(1)} %get-tuple-element.17, f32[1,128,2,128]{3,1,2,0:T(8,128)S(1)} %get-tuple-element.16), kind=kOutput, calls=%fused_computation.6 | convolution fusion | flops 1610678272 | bytes 8650752 | tf_op jit(solution)/shard_map/qkpn,tpnjs->tqkjs/dot_general | solution.py:100
  74.4 1.5 %subtract_reduce_fusion = (f32[128,512]{0,1:T(8,128)S(1)}, f32[128,512]{0,1:T(8,128)S(1)}) fusion(f32[1,2,128,8,512]{2,4,1,3,0:T(8,128)S(1)} %fusion.5, f32[128,512]{0,1:T(8,128)S(1)} %fusion.17, f32[128,8]{0,1:T(8,128)S(1)} %get-tuple-element.40, f32[8,512]{1,0:T(8,128)S(1)} %get-tuple-element.27, f32[128,8]{0,1:T(8,128)S(1)} %get-tuple-element.41, ...), kind=kLoop, calls=%fused_computation.11 | loop fusion | flops 8257536 | bytes 5021696 | tf_op jit(solution)/shard_map/reduce_sum | solution.py:117
  75.9 0.9 pad_maximum_fusion
  76.8 8.8 %all-to-all-start.1 = ((f32[128,8,128]{2,1,0:T(8,128)}), f32[128,8,128]{2,1,0:T(8,128)S(1)}, u32[]{:S(2)}, u32[]{:S(2)}) async-start(f32[128,8,128]{2,1,0:T(8,128)} %pad_maximum_fusion), calls=%async_computation.1 | async-start | bytes 1048576 | tf_op jit(solution)/shard_map/all_to_all | solution.py:160
  85.6 0.2 dynamic-slice_reduce_fusion
  86.0 13.4 %all-to-all-done.1 = f32[128,8,128]{2,1,0:T(8,128)S(1)} async-done(((f32[128,8,128]{2,1,0:T(8,128)}), f32[128,8,128]{2,1,0:T(8,128)S(1)}, u32[]{:S(2)}, u32[]{:S(2)}) %all-to-all-start.1) | async-done | bytes 524320 | tf_op jit(solution)/shard_map/all_to_all | solution.py:160
  99.3 0.1 copy.82
  99.4 0.4 convolution_bitcast_fusion
  99.9 0.6 copy.83
  (43 shorter events, 1.0 us)
Async XLA Ops:
  0.0 8.8 %copy-start.1 = (s32[512,8]{0,1:T(8,128)S(1)}, s32[512,8]{0,1:T(8,128)}, u32[]{:S(2)}) copy-start(s32[512,8]{0,1:T(8,128)} %param.8) | copy-start | bytes 49156
  0.0 9.2 %copy-start.2 = (s32[512,8]{0,1:T(8,128)S(1)}, s32[512,8]{0,1:T(8,128)}, u32[]{:S(2)}) copy-start(s32[512,8]{0,1:T(8,128)} %param.10) | copy-start | bytes 49156
  0.0 9.5 %copy-start.3 = (s32[512,8]{0,1:T(8,128)S(1)}, s32[512,8]{0,1:T(8,128)}, u32[]{:S(2)}) copy-start(s32[512,8]{0,1:T(8,128)} %param.9) | copy-start | bytes 49156
  0.0 59.5 %all-to-all-start = ((f32[32,32,1024]{2,1,0:T(8,128)}), f32[32,32,1024]{2,1,0:T(8,128)}, u32[]{:S(2)}, u32[]{:S(2)}) async-start(f32[32,32,1024]{2,1,0:T(8,128)} %param.7), calls=%async_computation | async-start | bytes 8388608 | tf_op jit(solution)/shard_map/all_to_all | solution.py:155
  23.2 1.8 %copy-start.4 = (f32[512,8]{0,1:T(8,128)S(1)}, f32[512,8]{0,1:T(8,128)}, u32[]{:S(2)}) copy-start(f32[512,8]{0,1:T(8,128)} %param.11) | copy-start | bytes 49156
  23.2 2.1 %copy-start.5 = (f32[512,8]{0,1:T(8,128)S(1)}, f32[512,8]{0,1:T(8,128)}, u32[]{:S(2)}) copy-start(f32[512,8]{0,1:T(8,128)} %param.12) | copy-start | bytes 49156
  23.2 2.5 %copy-start.6 = (f32[512]{0:T(512)S(1)}, f32[512]{0:T(512)}, u32[]{:S(2)}) copy-start(f32[512]{0:T(512)} %param.13) | copy-start | bytes 6148
  25.0 4.7 %copy-start = (f32[1,1,512,1024]{3,2,1,0:T(8,128)S(1)}, f32[1,1,512,1024]{3,2,1,0:T(8,128)}, u32[]{:S(2)}) copy-start(f32[1,1,512,1024]{3,2,1,0:T(8,128)} %copy.75) | copy-start | bytes 6291460
  76.8 22.5 %all-to-all-start.1 = ((f32[128,8,128]{2,1,0:T(8,128)}), f32[128,8,128]{2,1,0:T(8,128)S(1)}, u32[]{:S(2)}, u32[]{:S(2)}) async-start(f32[128,8,128]{2,1,0:T(8,128)} %pad_maximum_fusion), calls=%async_computation.1 | async-start | bytes 1048576 | tf_op jit(solution)/shard_map/all_to_all | solution.py:160
